TPU v7x, 32 devices: a whole 2x2x4 slice. The times are simulated.
32 devices in a mesh: chan: 4 (over y, x), tm: 8 (over z, core).
Axes of the slice: x: 2, y: 2, z: 4, core: 2. Of those that a mesh axis runs over, the one named last changes fastest.
Arguments:
- raw_samples: float32 [32, 512, 2048], P('tm', 'chan'), may hold values from -80 to 80
Outputs:
- correlations: float32 [512, 512, 256], P(('chan', 'tm'))
All inputs are finite; a program needn't handle non-finite values.
Results may differ from a plain program's by a relative error of at most 0.0043.
Values may be sent and summed in bfloat16 or wider, within the bound.
No kernel may reach another device: no remote copies, remote signals or barrier semaphores. Data moves between devices by JAX's collectives and lax.ppermute only.
A program may use at most 192 MiB of HBM per device.

v0:
```python
import math

import jax
import jax.numpy as jnp
from jax import lax
from jax.sharding import PartitionSpec as P

LAGS = 256


def spread(value, axis, source):
    kept = jnp.where(lax.axis_index(axis) == source, value, 0).astype(value.dtype)
    return lax.psum(kept, axis)


def decimate(raw_samples):
    even_taps = raw_samples[..., 0::2]
    odd_taps = raw_samples[..., 1::2]
    odd_before = jnp.concatenate([jnp.zeros_like(odd_taps[..., :1]), odd_taps[..., :-1]], axis=-1)
    return 0.25 * odd_before + 0.5 * even_taps + 0.25 * odd_taps


def whiten(real_part, imag_part):
    power = real_part * real_part + imag_part * imag_part
    level = jnp.mean(power, axis=-1, keepdims=True)
    factor = 1.0 / jnp.sqrt(power + 0.1 * level + 1e-06)
    return (real_part * factor, imag_part * factor)


def lag_table(freq_count, sample_count, lag_count):
    freq_index = jnp.arange(1, freq_count + 1, dtype=jnp.int32)
    lag_index = jnp.arange(lag_count, dtype=jnp.int32) - lag_count // 2
    turns = freq_index[:, None] * (lag_index[None, :] % sample_count) % sample_count
    angle = turns.astype(jnp.float32) * (2.0 * math.pi / sample_count)
    return jnp.concatenate([jnp.cos(angle), -jnp.sin(angle)], axis=0).astype(jnp.bfloat16)


def transform_tables(sample_count, freq_count):
    time_index = jnp.arange(sample_count, dtype=jnp.int32)
    freq_index = jnp.arange(1, freq_count + 1, dtype=jnp.int32)
    turns = time_index[:, None] * freq_index[None, :] % sample_count
    angle = turns.astype(jnp.float32) * (2.0 * math.pi / sample_count)
    return (jnp.cos(angle), -jnp.sin(angle))


def cross_block(local_spec, turned_spec, remote_spec):
    real_cross = jnp.einsum(
        "sik,sjk->ijk", local_spec, remote_spec, preferred_element_type=jnp.float32
    )
    imag_cross = jnp.einsum(
        "sik,sjk->ijk", turned_spec, remote_spec, preferred_element_type=jnp.float32
    )
    return jnp.concatenate([real_cross, imag_cross], axis=-1).astype(jnp.bfloat16)


def per_device(raw_samples):
    seg_count, block_width, raw_length = raw_samples.shape
    sample_count = raw_length // 2
    freq_count = sample_count // 8
    chan_count = lax.axis_size("chan")
    time_count = lax.axis_size("tm")
    channel_total = block_width * chan_count
    signal = decimate(raw_samples).reshape(seg_count * block_width, sample_count)
    cos_table, sin_table = transform_tables(sample_count, freq_count)
    real_part = jnp.dot(
        signal, cos_table, precision=lax.Precision.HIGHEST, preferred_element_type=jnp.float32
    )
    imag_part = jnp.dot(
        signal, sin_table, precision=lax.Precision.HIGHEST, preferred_element_type=jnp.float32
    )
    real_part = real_part.reshape(seg_count, block_width, freq_count)
    imag_part = imag_part.reshape(seg_count, block_width, freq_count)
    real_w, imag_w = whiten(real_part, imag_part)
    local_spec = jnp.concatenate([real_w, imag_w], axis=0).astype(jnp.bfloat16)
    table = lag_table(freq_count, sample_count, LAGS)
    norm_scale = 1.0 / math.sqrt(freq_count * seg_count * time_count)
    tm_index = lax.axis_index("tm")
    pair_spec = local_spec.reshape(2, seg_count, block_width, freq_count)
    all_spec = lax.all_gather(pair_spec, "tm", axis=1, tiled=True)
    span_width = channel_total // time_count
    span_offset = tm_index * span_width % block_width
    own_span = lax.dynamic_slice_in_dim(all_spec, span_offset, span_width, 2)
    root_block = tm_index * span_width // block_width
    column_spec = spread(own_span, "chan", root_block)

    def add_group(group_index, total):
        seg_start = (group_index * seg_count).astype(jnp.int32)
        left_group = lax.dynamic_slice_in_dim(all_spec, seg_start, seg_count, 1)
        right_group = lax.dynamic_slice_in_dim(column_spec, seg_start, seg_count, 1)
        left_rows = left_group.reshape(2 * seg_count, block_width, freq_count)
        turned_rows = jnp.concatenate([left_group[1], -left_group[0]], axis=0)
        right_rows = right_group.reshape(2 * seg_count, span_width, freq_count)
        return total + cross_block(left_rows, turned_rows, right_rows).astype(jnp.float32)

    summed = lax.fori_loop(
        0, time_count, add_group, jnp.zeros((block_width, span_width, 2 * freq_count), jnp.float32)
    )
    pair_lags = (
        jnp.einsum(
            "ijk,kl->ijl", summed, table.astype(jnp.float32), precision=lax.Precision.HIGHEST
        )
        * norm_scale
    )
    return lax.all_to_all(pair_lags, "tm", split_axis=0, concat_axis=1, tiled=True)


def solution(mesh):
    return jax.shard_map(
        per_device,
        mesh=mesh,
        in_specs=(P("tm", "chan", None),),
        out_specs=P(("chan", "tm"), None, None),
        check_vma=False,
    )
```

profile of v0, /device:TPU:0, one launch (start us, length us, event | category | flops | bytes accessed | tf_op | source)
XLA Modules:
  0.0 571.0 jit_solution(17318905619053049182)
XLA Ops:
  6.5 70.9 %slice.23 = f32[4,128,1024]{2,1,0:T(8,128)S(1)} slice(f32[4,128,2048]{2,1,0:T(8,128)} %param.3), slice={[0:4:1], [0:128:1], [1:2048:2]} | slice | bytes 4194304 | tf_op jit(solution)/shard_map/slice | solution.py:18
  77.4 71.3 %slice.25 = f32[4,128,1024]{2,1,0:T(8,128)} slice(f32[4,128,2048]{2,1,0:T(8,128)} %param.3), slice={[0:4:1], [0:128:1], [0:2048:2]} | slice | bytes 4194304 | tf_op jit(solution)/shard_map/slice | solution.py:17
  148.7 6.3 %fusion.13 = f32[4,128,128]{1,2,0:T(8,128)S(1)} fusion(s32[128]{0:T(128)S(1)} %iota_add_fusion, f32[4,128,1024]{2,1,0:T(8,128)S(1)} %slice.23, f32[4,128,1024]{2,1,0:T(8,128)} %slice.25, f32[4,128,1023]{2,1,0:T(8,128)S(1)} %bitcast.48), kind=kOutput, calls=%fused_computation.24 | convolution fusion | flops 809762816 | bytes 6552064 | tf_op jit(solution)/shard_map/dot_general | solution.py:65
  155.1 4.7 fusion.23
  160.9 31.9 %all-gather.2.cloned.1.call-done = bf16[2,32,128,128]{3,2,0,1:T(8,128)(2,1)} async-done(((bf16[2,4,128,128]{3,2,0,1:T(8,128)(2,1)}), bf16[2,32,128,128]{3,2,0,1:T(8,128)(2,1)}) %all-gather.2.cloned.1.call-update) | async-done | bytes 2097168 | tf_op jit(solution)/shard_map/all_gather | solution.py:79
  192.7 2.6 dynamic-slice_select_fusion
  196.0 51.9 %all-reduce.3.cloned.1.call-done = bf16[2,32,64,128]{3,2,0,1:T(8,128)(2,1)} async-done(((bf16[2,32,64,128]{3,2,0,1:T(8,128)(2,1)}), bf16[2,32,64,128]{3,2,0,1:T(8,128)(2,1)}) %all-reduce.3.cloned.1.call-update) | async-done | bytes 1048592 | tf_op jit(solution)/shard_map/psum | solution.py:13
  247.9 104.6 %while.14 = (s32[]{:T(128)}, f32[128,64,256]{0,1,2:T(8,128)}, bf16[2,32,64,128]{3,2,0,1:T(8,128)(2,1)}, bf16[2,32,128,128]{3,2,0,1:T(8,128)(2,1)}, s32[]{:T(128)}, /*index=5*/s32[]{:T(128)}, s32[]{:T(128)}, s32[]{:T(128)}, s32[]{}) while((s32[]{:T(128)}, f32[128,64,256]{0,1,2:T(8,128)}, bf16[2,32,64,128]{3,2,0,1:T(8,128)(2,1)}, ...), condition=%wide.region_3.4_spmd.clone, body=%wide.region_2.3_spmd.clone.sunk | while | flops 44630024 | bytes 28573872 | solution.py:95
  247.9 1.0 constant_dynamic-slice_fusion.7
  249.2 0.9 constant_dynamic-slice_fusion.6
  251.1 1.0 constant_dynamic-slice_fusion.8
  252.2 2.1 convert_bitcast_fusion.5
  254.3 5.3 select_add_fusion.2
  259.6 1.0 constant_dynamic-slice_fusion.7
  260.9 0.9 constant_dynamic-slice_fusion.6
  262.8 1.0 constant_dynamic-slice_fusion.8
  264.0 2.1 convert_bitcast_fusion.5
  266.0 6.8 %select_add_fusion.2 = f32[128,64,256]{0,1,2:T(8,128)} fusion(f32[128,64,256]{0,1,2:T(8,128)} %get-tuple-element.163, bf16[128,64,128]{0,1,2:T(8,128)(2,1)S(1)} %convert_bitcast_fusion.4, bf16[128,64,128]{0,1,2:T(8,128)(2,1)} %convert_bitcast_fusion.5, pred[]{:T(512)S(6)} %compare.13), kind=kLoop, calls=%fused_computation.clone.1 | loop fusion | flops 8388608 | bytes 20971520 | tf_op jit(solution)/shard_map/while/body/eval_jaxpr/add | solution.py:93
  272.9 1.0 constant_dynamic-slice_fusion.7
  274.2 0.9 constant_dynamic-slice_fusion.6
  276.1 1.0 constant_dynamic-slice_fusion.8
  277.2 2.1 convert_bitcast_fusion.5
  279.3 6.8 %select_add_fusion.2 = f32[128,64,256]{0,1,2:T(8,128)} fusion(f32[128,64,256]{0,1,2:T(8,128)} %get-tuple-element.163, bf16[128,64,128]{0,1,2:T(8,128)(2,1)S(1)} %convert_bitcast_fusion.4, bf16[128,64,128]{0,1,2:T(8,128)(2,1)} %convert_bitcast_fusion.5, pred[]{:T(512)S(6)} %compare.13), kind=kLoop, calls=%fused_computation.clone.1 | loop fusion | flops 8388608 | bytes 20971520 | tf_op jit(solution)/shard_map/while/body/eval_jaxpr/add | solution.py:93
  286.1 1.0 constant_dynamic-slice_fusion.7
  287.4 0.9 constant_dynamic-slice_fusion.6
  289.3 1.0 constant_dynamic-slice_fusion.8
  290.5 2.1 convert_bitcast_fusion.5
  292.6 6.8 %select_add_fusion.2 = f32[128,64,256]{0,1,2:T(8,128)} fusion(f32[128,64,256]{0,1,2:T(8,128)} %get-tuple-element.163, bf16[128,64,128]{0,1,2:T(8,128)(2,1)S(1)} %convert_bitcast_fusion.4, bf16[128,64,128]{0,1,2:T(8,128)(2,1)} %convert_bitcast_fusion.5, pred[]{:T(512)S(6)} %compare.13), kind=kLoop, calls=%fused_computation.clone.1 | loop fusion | flops 8388608 | bytes 20971520 | tf_op jit(solution)/shard_map/while/body/eval_jaxpr/add | solution.py:93
  299.4 1.0 constant_dynamic-slice_fusion.7
  302.6 1.0 constant_dynamic-slice_fusion.8
  303.8 2.1 convert_bitcast_fusion.5
  305.8 6.8 %select_add_fusion.2 = f32[128,64,256]{0,1,2:T(8,128)} fusion(f32[128,64,256]{0,1,2:T(8,128)} %get-tuple-element.163, bf16[128,64,128]{0,1,2:T(8,128)(2,1)S(1)} %convert_bitcast_fusion.4, bf16[128,64,128]{0,1,2:T(8,128)(2,1)} %convert_bitcast_fusion.5, pred[]{:T(512)S(6)} %compare.13), kind=kLoop, calls=%fused_computation.clone.1 | loop fusion | flops 8388608 | bytes 20971520 | tf_op jit(solution)/shard_map/while/body/eval_jaxpr/add | solution.py:93
  312.7 1.0 constant_dynamic-slice_fusion.7
  315.9 1.0 constant_dynamic-slice_fusion.8
  317.0 2.1 convert_bitcast_fusion.5
  319.1 6.8 %select_add_fusion.2 = f32[128,64,256]{0,1,2:T(8,128)} fusion(f32[128,64,256]{0,1,2:T(8,128)} %get-tuple-element.163, bf16[128,64,128]{0,1,2:T(8,128)(2,1)S(1)} %convert_bitcast_fusion.4, bf16[128,64,128]{0,1,2:T(8,128)(2,1)} %convert_bitcast_fusion.5, pred[]{:T(512)S(6)} %compare.13), kind=kLoop, calls=%fused_computation.clone.1 | loop fusion | flops 8388608 | bytes 20971520 | tf_op jit(solution)/shard_map/while/body/eval_jaxpr/add | solution.py:93
  325.9 1.0 constant_dynamic-slice_fusion.7
  329.1 1.0 constant_dynamic-slice_fusion.8
  330.3 2.1 convert_bitcast_fusion.5
  332.4 6.8 %select_add_fusion.2 = f32[128,64,256]{0,1,2:T(8,128)} fusion(f32[128,64,256]{0,1,2:T(8,128)} %get-tuple-element.163, bf16[128,64,128]{0,1,2:T(8,128)(2,1)S(1)} %convert_bitcast_fusion.4, bf16[128,64,128]{0,1,2:T(8,128)(2,1)} %convert_bitcast_fusion.5, pred[]{:T(512)S(6)} %compare.13), kind=kLoop, calls=%fused_computation.clone.1 | loop fusion | flops 8388608 | bytes 20971520 | tf_op jit(solution)/shard_map/while/body/eval_jaxpr/add | solution.py:93
  339.2 1.0 constant_dynamic-slice_fusion.7
  342.4 1.0 constant_dynamic-slice_fusion.8
  343.6 2.1 convert_bitcast_fusion.5
  345.6 6.8 %select_add_fusion.2 = f32[128,64,256]{0,1,2:T(8,128)} fusion(f32[128,64,256]{0,1,2:T(8,128)} %get-tuple-element.163, bf16[128,64,128]{0,1,2:T(8,128)(2,1)S(1)} %convert_bitcast_fusion.4, bf16[128,64,128]{0,1,2:T(8,128)(2,1)} %convert_bitcast_fusion.5, pred[]{:T(512)S(6)} %compare.13), kind=kLoop, calls=%fused_computation.clone.1 | loop fusion | flops 8388608 | bytes 20971520 | tf_op jit(solution)/shard_map/while/body/eval_jaxpr/add | solution.py:93
  352.5 14.2 %broadcast_multiply_fusion = f32[128,64,256]{2,0,1:T(8,128)S(1)} fusion(f32[128,64,256]{0,1,2:T(8,128)} %get-tuple-element.84, bf16[128,256]{1,0:T(8,128)(2,1)S(1)} %get-tuple-element.121, bf16[128,256]{1,0:T(8,128)(2,1)S(1)} %get-tuple-element.120), kind=kOutput, calls=%fused_computation.13 | convolution fusion | flops 6444810240 | bytes 16908288 | tf_op jit(solution)/shard_map/ijk,kl->ijl/dot_general | solution.py:99
  366.7 4.9 copy.12
  371.6 188.5 %all_to_all.18 = f32[128,64,256]{2,1,0:T(8,128)S(1)} all-to-all(f32[128,64,256]{2,1,0:T(8,128)S(1)} %copy.12), channel_id=1, replica_groups=mesh['chan'=4,'tm'=8] {'tm'}, dimensions={0} | all-to-all | bytes 16777216 | tf_op jit(solution)/shard_map/all_to_all | solution.py:104
  560.1 4.0 copy.13
  (58 shorter events, 16.8 us)
Async XLA Ops:
  6.5 186.2 %all-gather.2.cloned.1.call-start = ((), (), s32[]{:S(2)}) async-start(), calls=%async_computation.1 | async-start | bytes 2359296 | tf_op jit(solution)/shard_map/all_gather | solution.py:79
  148.7 6.3 %copy-start = (f32[4,128,1024]{2,1,0:T(8,128)S(1)}, f32[4,128,1024]{2,1,0:T(8,128)}, u32[]{:S(2)}) copy-start(f32[4,128,1024]{2,1,0:T(8,128)} %slice.25) | copy-start | bytes 6291460
  160.8 87.1 %all-reduce.3.cloned.1.call-start = ((), (), s32[]{:S(2)}) async-start(), calls=%async_computation.2 | async-start | bytes 2097152 | tf_op jit(solution)/shard_map/psum | solution.py:13
Sparse Core Ops, SparseCore 0:
  160.9 31.7 all-gather.1
  195.8 52.0 all-reduce.2
where the time goes:
time: 572 us; the launch traced here: 571 us
  blocking collectives  189 us (33%)
  local copies, waits for them, and re-layouts  172 us (30%)
  waiting for transfers between devices  83.8 us (15%)
  other arithmetic  64.5 us (11%)
  matrix products  47.8 us (8%)
  between operations  13.5 us (2%)
    all_to_all x1, blocking collectives, per_device(): lax.all_to_all(pair_lags, 'tm', split_axis=0, concat_axis=1, tiled=True)  189 us
    slice x1, local copies, waits for them, and re-layouts, decimate(): even_taps = raw_samples[..., 0::2]  71.3 us
    slice x1, local copies, waits for them, and re-layouts, decimate(): odd_taps = raw_samples[..., 1::2]  70.9 us
    add x8, other arithmetic, add_group(): total + cross_block(left_rows, turned_rows, right_rows).astype(jnp.float32)  53.2 us
    psum x1, waiting for transfers between devices, spread(): return lax.psum(kept, axis)  51.9 us
    all_gather x1, waiting for transfers between devices, per_device(): all_spec = lax.all_gather(pair_spec, 'tm', axis=1, tiled=True)  31.9 us
    dot_general x8, matrix products, cross_block(): jnp.einsum('sik,sjk->ijk', local_spec, remote_spec, preferred_element_typ...  16.6 us
    dot_general x1, matrix products, per_device(): jnp.einsum('ijk,kl->ijl', summed, table.astype(jnp.float32), precision=la...  14.2 us
  transfers between devices with their start and end apart: 2, of which 2 were waited for; matrix products, arithmetic and copies ran while one was open for 0% of the time, Pallas kernels for 0%

commit v1 on v0

v1 whole, which is shorter than its diff:
```python
import math

import jax
import jax.numpy as jnp
from jax import lax
from jax.sharding import PartitionSpec as P

LAGS = 256


def decimate(raw_samples):
    even_taps = raw_samples[..., 0::2]
    odd_taps = raw_samples[..., 1::2]
    odd_before = jnp.concatenate([jnp.zeros_like(odd_taps[..., :1]), odd_taps[..., :-1]], axis=-1)
    return 0.25 * odd_before + 0.5 * even_taps + 0.25 * odd_taps


def whiten(real_part, imag_part):
    power = real_part * real_part + imag_part * imag_part
    level = jnp.mean(power, axis=-1, keepdims=True)
    factor = 1.0 / jnp.sqrt(power + 0.1 * level + 1e-06)
    return (real_part * factor, imag_part * factor)


def lag_table(freq_count, sample_count, lag_count):
    freq_index = jnp.arange(1, freq_count + 1, dtype=jnp.int32)
    lag_index = jnp.arange(lag_count, dtype=jnp.int32) - lag_count // 2
    turns = freq_index[:, None] * (lag_index[None, :] % sample_count) % sample_count
    angle = turns.astype(jnp.float32) * (2.0 * math.pi / sample_count)
    return jnp.concatenate([jnp.cos(angle), -jnp.sin(angle)], axis=0).astype(jnp.bfloat16)


def transform_tables(sample_count, freq_count):
    time_index = jnp.arange(sample_count, dtype=jnp.int32)
    freq_index = jnp.arange(1, freq_count + 1, dtype=jnp.int32)
    turns = time_index[:, None] * freq_index[None, :] % sample_count
    angle = turns.astype(jnp.float32) * (2.0 * math.pi / sample_count)
    return (jnp.cos(angle), -jnp.sin(angle))


def per_device(raw_samples):
    seg_count, block_width, raw_length = raw_samples.shape
    sample_count = raw_length // 2
    freq_count = sample_count // 8
    chan_count = lax.axis_size("chan")
    time_count = lax.axis_size("tm")
    channel_total = block_width * chan_count
    row_width = channel_total // (chan_count * time_count)
    signal = decimate(raw_samples).reshape(seg_count * block_width, sample_count)
    cos_table, sin_table = transform_tables(sample_count, freq_count)
    real_part = jnp.dot(
        signal, cos_table, precision=lax.Precision.HIGHEST, preferred_element_type=jnp.float32
    )
    imag_part = jnp.dot(
        signal, sin_table, precision=lax.Precision.HIGHEST, preferred_element_type=jnp.float32
    )
    real_part = real_part.reshape(seg_count, block_width, freq_count)
    imag_part = imag_part.reshape(seg_count, block_width, freq_count)
    real_w, imag_w = whiten(real_part, imag_part)
    local_spec = jnp.stack([real_w, imag_w], axis=0).astype(jnp.bfloat16)
    every = lax.all_gather(local_spec, ("chan", "tm"), axis=0)
    every = every.reshape(chan_count, time_count, 2, seg_count, block_width, freq_count)
    chan_index = lax.axis_index("chan")
    tm_index = lax.axis_index("tm")
    own_block = lax.dynamic_index_in_dim(every, chan_index, 0, keepdims=False)
    rows = lax.dynamic_slice_in_dim(own_block, tm_index * row_width, row_width, axis=3)
    turned = jnp.stack([rows[:, 1], -rows[:, 0]], axis=1)
    left = jnp.concatenate([rows, turned], axis=3)
    cross = jnp.einsum("trsak,ctrswk->kacw", left, every, preferred_element_type=jnp.float32)
    cross = cross.reshape(freq_count, 2, row_width, channel_total)
    table = lag_table(freq_count, sample_count, LAGS).reshape(2, freq_count, LAGS)
    high = cross.astype(jnp.bfloat16)
    low = (cross - high.astype(jnp.float32)).astype(jnp.bfloat16)
    pair_lags = jnp.einsum(
        "krij,rkl->ijl", high, table, preferred_element_type=jnp.float32
    ) + jnp.einsum("krij,rkl->ijl", low, table, preferred_element_type=jnp.float32)
    norm_scale = 1.0 / math.sqrt(freq_count * seg_count * time_count)
    return pair_lags * norm_scale


def solution(mesh):
    return jax.shard_map(
        per_device,
        mesh=mesh,
        in_specs=(P("tm", "chan", None),),
        out_specs=P(("chan", "tm"), None, None),
        check_vma=False,
    )
```

time: 572 us -> 299 us (0.52)
  blocking collectives: 189 us -> 0 us
  other arithmetic: 64.5 us -> 0.83 us
  matrix products: 47.8 us -> 31 us
    all_to_all x1 -> x0, blocking collectives: 189 us -> none  [per_device(): lax.all_to_all(pair_lags, 'tm', split_axis=0, concat_axis=1, tiled=True)]
    add x8 -> x0, other arithmetic: 53.2 us -> none  [add_group(): total + cross_block(left_rows, turned_rows, right_rows).astype(jnp.float32)]
    psum x1 -> x0, waiting for transfers between devices: 51.9 us -> none  [spread(): return lax.psum(kept, axis)]
    all_gather x1, waiting for transfers between devices: 31.9 us -> 79.6 us  [per_device(): every = lax.all_gather(local_spec, ('chan', 'tm'), axis=0)]
    dynamic_slice x32 -> x1, local copies, waits for them, and re-layouts: 18.2 us -> 1.1 us  [per_device(): lax.dynamic_slice_in_dim(own_block, tm_index * row_width, row_width, axis=3)]
    dot_general x17 -> x3, matrix products: 36.8 us -> 20 us  [the longest x1 8.14 us: per_device(): jnp.einsum('trsak,ctrswk->kacw', left, every, preferred_element_type=jnp....]
    reshape x0 -> x1, local copies, waits for them, and re-layouts: none -> 14.5 us  [per_device(): every.reshape(chan_count, time_count, 2, seg_count, block_width, freq_count)]
    dot_general x0 -> x1, local copies, waits for them, and re-layouts: none -> 10.2 us  [per_device(): jnp.einsum('trsak,ctrswk->kacw', left, every, preferred_element_type=jnp....]
  transfers between devices with their start and end apart: 2 -> 1, of which waited for: 2 -> 1; matrix products, arithmetic and copies ran while one was open for 0% -> 0% of each run, Pallas kernels for 0% -> 0%
where the time goes in v1:
time: 299 us; the launch traced here: 298 us
  local copies, waits for them, and re-layouts  173 us (58%)
  waiting for transfers between devices  79.6 us (27%)
  matrix products  31 us (10%)
  between operations  13.5 us (5%)
    all_gather x1, waiting for transfers between devices, per_device(): every = lax.all_gather(local_spec, ('chan', 'tm'), axis=0)  79.6 us
    slice x1, local copies, waits for them, and re-layouts, decimate(): even_taps = raw_samples[..., 0::2]  71.3 us
    slice x1, local copies, waits for them, and re-layouts, decimate(): odd_taps = raw_samples[..., 1::2]  70.9 us
    reshape x1, local copies, waits for them, and re-layouts, per_device(): every.reshape(chan_count, time_count, 2, seg_count, block_width, freq_count)  14.5 us
    dot_general x1, local copies, waits for them, and re-layouts, per_device(): jnp.einsum('trsak,ctrswk->kacw', left, every, preferred_element_type=jnp....  10.2 us
    dot_general x1, matrix products, per_device(): jnp.einsum('trsak,ctrswk->kacw', left, every, preferred_element_type=jnp....  8.14 us
    dot_general x1, matrix products, per_device(): jnp.einsum('krij,rkl->ijl', low, table, preferred_element_type=jnp.float32)  7.19 us
    dot_general x1, matrix products, per_device(): jnp.dot(signal, cos_table, precision=lax.Precision.HIGHEST, preferred_ele...  6.32 us
  transfers between devices with their start and end apart: 1, of which 1 were waited for; matrix products, arithmetic and copies ran while one was open for 0% of the time, Pallas kernels for 0%

profile of v1, /device:TPU:0, one launch (start us, length us, event | category | flops | bytes accessed | tf_op | source)
XLA Modules:
  0.0 297.9 jit_solution(14491355278636896896)
XLA Ops:
  6.5 0.0 all-gather.2.cloned.1.call-start
  6.5 70.9 %slice.15 = f32[4,128,1024]{2,1,0:T(8,128)S(1)} slice(f32[4,128,2048]{2,1,0:T(8,128)} %param.1), slice={[0:4:1], [0:128:1], [1:2048:2]} | slice | bytes 4194304 | tf_op jit(solution)/shard_map/slice | solution.py:13
  77.4 71.3 %slice.17 = f32[4,128,1024]{2,1,0:T(8,128)} slice(f32[4,128,2048]{2,1,0:T(8,128)} %param.1), slice={[0:4:1], [0:128:1], [0:2048:2]} | slice | bytes 4194304 | tf_op jit(solution)/shard_map/slice | solution.py:12
  148.7 0.0 copy-start.1
  148.7 6.3 %fusion.9 = f32[4,128,128]{1,2,0:T(8,128)S(1)} fusion(s32[128]{0:T(128)S(1)} %iota_add_fusion, f32[4,128,1024]{2,1,0:T(8,128)S(1)} %slice.15, f32[4,128,1024]{2,1,0:T(8,128)} %slice.17, f32[4,128,1023]{2,1,0:T(8,128)S(1)} %bitcast.40), kind=kOutput, calls=%fused_computation.17 | convolution fusion | flops 809762816 | bytes 6552064 | tf_op jit(solution)/shard_map/dot_general | solution.py:51
  155.1 0.0 copy-done.1
  155.1 4.7 %fusion.19 = (f32[4,128]{1,0:T(4,128)S(1)}, f32[4,128,128]{1,2,0:T(8,128)S(1)}) fusion(f32[4,128,128]{1,2,0:T(8,128)S(1)} %fusion.9, s32[128]{0:T(128)S(1)} %iota_add_fusion, f32[4,128,1024]{2,1,0:T(8,128)S(1)} %slice.15, f32[4,128,1024]{2,1,0:T(8,128)S(1)} %copy-done.1, f32[4,128,1023]{2,1,0:T(8,128)S(1)} %bitcast.41), kind=kOutput, calls=%fused_computation.36 | convolution fusion | flops 810155520 | bytes 6816256 | tf_op jit(solution)/shard_map/dot_general | solution.py:54
  159.8 0.1 fusion.23
  159.9 0.9 copy.12
  160.8 0.0 all-gather.2.cloned.1.call-update
  160.8 0.6 cosine_convert_fusion
  161.4 79.6 %all-gather.2.cloned.1.call-done = bf16[32,2,4,128,128]{4,3,2,1,0:T(8,128)(2,1)} async-done(((bf16[1,2,4,128,128]{4,3,2,1,0:T(8,128)(2,1)}), bf16[32,2,4,128,128]{4,3,2,1,0:T(8,128)(2,1)}) %all-gather.2.cloned.1.call-update) | async-done | bytes 8388624 | tf_op jit(solution)/shard_map/all_gather | solution.py:61
  241.0 14.5 %copy.14 = bf16[4,8,2,4,128,128]{4,1,3,2,0,5:T(8,128)(2,1)} copy(bf16[4,8,2,4,128,128]{5,4,3,2,1,0:T(8,128)(2,1)} %bitcast.42) | data formatting | bytes 16777216 | tf_op jit(solution)/shard_map/reshape | solution.py:62
  255.6 1.1 dynamic-slice_bitcast_fusion
  256.8 3.2 %copy.16 = bf16[8,2,4,32,128,1]{3,0,2,1,5,4:T(8,128)(2,1)S(1)} copy(bf16[8,2,4,32,128,1]{4,3,2,1,0,5:T(8,128)(2,1)S(1)} %maximum_bitcast_fusion) | data formatting | bytes 1048576 | tf_op jit(solution)/shard_map/concatenate | solution.py:68
  260.0 8.1 %convolution_bitcast_fusion = f32[128,32,4,128]{3,1,2,0:T(8,128)} fusion(bf16[8,2,4,32,128,1]{3,0,2,1,5,4:T(8,128)(2,1)S(1)} %copy.16, bf16[4,8,2,4,128,128]{4,1,3,2,0,5:T(8,128)(2,1)} %copy.14), kind=kOutput, calls=%fused_computation.4 | convolution fusion | flops 268435456 | bytes 17301504 | tf_op jit(solution)/shard_map/trsak,ctrswk->kacw/dot_general | solution.py:69
  268.1 10.2 %copy.15 = f32[128,32,4,128]{0,3,2,1:T(8,128)} copy(f32[128,32,4,128]{3,1,2,0:T(8,128)} %convolution_bitcast_fusion) | data formatting | bytes 16777216 | tf_op jit(solution)/shard_map/trsak,ctrswk->kacw/dot_general | solution.py:69
  278.3 0.0 copy-start
  278.3 7.2 %fusion.1 = f32[16,512,256,1]{2,1,0,3:T(8,128)S(1)} fusion(bf16[2,128,256,1]{2,1,3,0:T(8,128)(2,1)S(1)} %bitcast.44, f32[128,2,16,512]{0,3,2,1:T(8,128)} %bitcast.38), kind=kOutput, calls=%fused_computation.3 | convolution fusion | flops 1082130432 | bytes 16908288 | tf_op jit(solution)/shard_map/krij,rkl->ijl/dot_general | solution.py:76
  285.5 1.0 copy-done
  286.4 4.7 %fusion = f32[16,512,256]{2,1,0:T(8,128)} fusion(f32[16,512,256,1]{2,1,0,3:T(8,128)S(1)} %fusion.1, bf16[2,128,256,1]{2,1,3,0:T(8,128)(2,1)S(1)} %bitcast.45, f32[128,2,16,512]{0,3,2,1:T(8,128)S(1)} %bitcast.39), kind=kOutput, calls=%fused_computation.1 | convolution fusion | flops 1080033280 | bytes 25296896 | tf_op jit(solution)/shard_map/krij,rkl->ijl/dot_general | solution.py:74
  (7 shorter events, 0.1 us)
Async XLA Ops:
  6.5 234.5 %all-gather.2.cloned.1.call-start = ((), (), s32[]{:S(2)}) async-start(), calls=%async_computation | async-start | bytes 8650752 | tf_op jit(solution)/shard_map/all_gather | solution.py:61
  148.7 6.3 %copy-start.1 = (f32[4,128,1024]{2,1,0:T(8,128)S(1)}, f32[4,128,1024]{2,1,0:T(8,128)}, u32[]{:S(2)}) copy-start(f32[4,128,1024]{2,1,0:T(8,128)} %slice.17) | copy-start | bytes 6291460
  278.3 8.2 %copy-start = (f32[128,32,4,128]{0,3,2,1:T(8,128)S(1)}, f32[128,32,4,128]{0,3,2,1:T(8,128)}, u32[]{:S(2)}) copy-start(f32[128,32,4,128]{0,3,2,1:T(8,128)} %copy.15) | copy-start | bytes 25165828
Sparse Core Ops, SparseCore 0:
  160.9 80.0 all-gather.1

commit v2 on v1

--- a/solution.py
+++ b/solution.py
@@ -6,13 +6,6 @@
 from jax.sharding import PartitionSpec as P
 
 LAGS = 256
-
-
-def decimate(raw_samples):
-    even_taps = raw_samples[..., 0::2]
-    odd_taps = raw_samples[..., 1::2]
-    odd_before = jnp.concatenate([jnp.zeros_like(odd_taps[..., :1]), odd_taps[..., :-1]], axis=-1)
-    return 0.25 * odd_before + 0.5 * even_taps + 0.25 * odd_taps
 
 
 def whiten(real_part, imag_part):
@@ -46,16 +39,17 @@
     time_count = lax.axis_size("tm")
     channel_total = block_width * chan_count
     row_width = channel_total // (chan_count * time_count)
-    signal = decimate(raw_samples).reshape(seg_count * block_width, sample_count)
+    raw_rows = raw_samples.reshape(seg_count * block_width, raw_length)
     cos_table, sin_table = transform_tables(sample_count, freq_count)
-    real_part = jnp.dot(
-        signal, cos_table, precision=lax.Precision.HIGHEST, preferred_element_type=jnp.float32
+    both_tables = jnp.concatenate([cos_table, sin_table], axis=1)
+    next_tables = jnp.concatenate([both_tables[1:], jnp.zeros_like(both_tables[:1])], axis=0)
+    folded = jnp.stack([0.5 * both_tables, 0.25 * both_tables + 0.25 * next_tables], axis=1)
+    folded = folded.reshape(raw_length, 2 * freq_count)
+    spectrum = jnp.dot(
+        raw_rows, folded, precision=lax.Precision.HIGHEST, preferred_element_type=jnp.float32
     )
-    imag_part = jnp.dot(
-        signal, sin_table, precision=lax.Precision.HIGHEST, preferred_element_type=jnp.float32
-    )
-    real_part = real_part.reshape(seg_count, block_width, freq_count)
-    imag_part = imag_part.reshape(seg_count, block_width, freq_count)
+    real_part = spectrum[:, :freq_count].reshape(seg_count, block_width, freq_count)
+    imag_part = spectrum[:, freq_count:].reshape(seg_count, block_width, freq_count)
     real_w, imag_w = whiten(real_part, imag_part)
     local_spec = jnp.stack([real_w, imag_w], axis=0).astype(jnp.bfloat16)
     every = lax.all_gather(local_spec, ("chan", "tm"), axis=0)

time: 299 us -> 163 us (0.55)
  local copies, waits for them, and re-layouts: 173 us -> 34.4 us
  other arithmetic: 0.83 us -> 5.87 us
    slice x2 -> x0, local copies, waits for them, and re-layouts: 142 us -> none  [the longest x1 71.3 us: decimate(): even_taps = raw_samples[..., 0::2]]
    dot_general x2 -> x1, matrix products: 11 us -> 9.32 us  [per_device(): jnp.dot(raw_rows, folded, precision=lax.Precision.HIGHEST, preferred_elem...]
where the time goes in v2:
time: 163 us
  waiting for transfers between devices  79.6 us (49%)
  local copies, waits for them, and re-layouts  34.4 us (21%)
  matrix products  29.3 us (18%)
  between operations  13.5 us (8%)
  other arithmetic  5.87 us (4%)
    all_gather x1, waiting for transfers between devices, per_device(): every = lax.all_gather(local_spec, ('chan', 'tm'), axis=0)  79.6 us
    reshape x1, local copies, waits for them, and re-layouts, per_device(): every.reshape(chan_count, time_count, 2, seg_count, block_width, freq_count)  14.5 us
    dot_general x1, local copies, waits for them, and re-layouts, per_device(): jnp.einsum('trsak,ctrswk->kacw', left, every, preferred_element_type=jnp....  10.2 us
    dot_general x1, matrix products, per_device(): jnp.dot(raw_rows, folded, precision=lax.Precision.HIGHEST, preferred_elem...  9.32 us
    dot_general x1, matrix products, per_device(): jnp.einsum('trsak,ctrswk->kacw', left, every, preferred_element_type=jnp....  8.14 us
    dot_general x1, matrix products, per_device(): jnp.einsum('krij,rkl->ijl', low, table, preferred_element_type=jnp.float32)  7.19 us
    dot_general x1, matrix products, per_device(): jnp.einsum('krij,rkl->ijl', high, table, preferred_element_type=jnp.float32)  4.65 us
  transfers between devices with their start and end apart: 1, of which 1 were waited for; matrix products, arithmetic and copies ran while one was open for 0% of the time, Pallas kernels for 0%

profile of v2, /device:TPU:0, one launch (start us, length us, event | category | flops | bytes accessed | tf_op | source)
XLA Modules:
  0.0 162.7 jit_solution(1322328708049449907)
XLA Ops:
  6.5 0.0 all-gather.2.cloned.1.call-start
  6.5 2.1 %fusion.14 = (f32[1024,1,128]{2,0,1:T(8,128)S(1)}, f32[1024,1,128]{2,0,1:T(8,128)S(1)}, f32[1024,128]{1,0:T(8,128)S(1)}, f32[1024,128]{1,0:T(8,128)S(1)}) fusion(s32[128]{0:T(128)S(1)} %iota_add_fusion), kind=kLoop, calls=%fused_computation.37 | loop fusion | flops 1966080 | bytes 2097664 | tf_op jit(solution)/shard_map/concatenate | solution.py:44
  8.6 0.1 fusion.4
  8.7 0.1 fusion.6
  8.8 0.7 stack.20
  9.5 0.1 maximum_multiply_fusion
  9.6 1.1 copy.14
  10.7 1.9 %pad_maximum_fusion = f32[1024,2,256]{2,1,0:T(2,128)S(1)} fusion(f32[1024,1,256]{2,1,0:T(1,128)S(1)} %stack.20, f32[1024,1,256]{2,1,0:T(1,128)S(1)} %copy.14), kind=kLoop, calls=%fused_computation.5 | loop fusion | flops 524288 | bytes 4194304 | tf_op jit(solution)/shard_map/stack | solution.py:46
  12.6 2.6 %reshape.227 = f32[2048,256]{1,0:T(8,128)} reshape(f32[1024,2,256]{2,1,0:T(2,128)S(1)} %pad_maximum_fusion) | data formatting | bytes 4194304 | tf_op jit(solution)/shard_map/reshape | solution.py:47
  15.2 9.3 %convolution_bitcast_fusion.1 = f32[512,256]{0,1:T(8,128)S(1)} fusion(f32[2048,256]{1,0:T(8,128)} %reshape.227, f32[512,2048]{1,0:T(8,128)} %bitcast.46), kind=kOutput, calls=%fused_computation.11 | convolution fusion | flops 3221225472 | bytes 6815744 | tf_op jit(solution)/shard_map/dot_general | solution.py:48
  24.6 0.1 add_reduce_fusion
  24.6 0.1 copy.29
  24.8 0.1 copy.30
  24.9 0.2 fusion.19
  25.1 0.7 pad_maximum_fusion.2
  25.8 0.0 all-gather.2.cloned.1.call-update
  25.8 0.6 cosine_convert_fusion
  26.5 79.6 %all-gather.2.cloned.1.call-done = bf16[32,2,4,128,128]{4,3,2,1,0:T(8,128)(2,1)} async-done(((bf16[1,2,4,128,128]{4,3,2,1,0:T(8,128)(2,1)}), bf16[32,2,4,128,128]{4,3,2,1,0:T(8,128)(2,1)}) %all-gather.2.cloned.1.call-update) | async-done | bytes 8388624 | tf_op jit(solution)/shard_map/all_gather | solution.py:55
  106.1 14.5 %copy.22 = bf16[4,8,2,4,128,128]{4,1,3,2,0,5:T(8,128)(2,1)} copy(bf16[4,8,2,4,128,128]{5,4,3,2,1,0:T(8,128)(2,1)} %bitcast.44) | data formatting | bytes 16777216 | tf_op jit(solution)/shard_map/reshape | solution.py:56
  120.6 1.1 dynamic-slice_bitcast_fusion
  121.8 3.0 %copy.24 = bf16[8,2,4,32,128,1]{3,0,2,1,5,4:T(8,128)(2,1)S(1)} copy(bf16[8,2,4,32,128,1]{4,3,2,1,0,5:T(8,128)(2,1)S(1)} %maximum_bitcast_fusion) | data formatting | bytes 1048576 | tf_op jit(solution)/shard_map/concatenate | solution.py:62
  124.8 8.1 %convolution_bitcast_fusion = f32[128,32,4,128]{3,1,2,0:T(8,128)} fusion(bf16[8,2,4,32,128,1]{3,0,2,1,5,4:T(8,128)(2,1)S(1)} %copy.24, bf16[4,8,2,4,128,128]{4,1,3,2,0,5:T(8,128)(2,1)} %copy.22), kind=kOutput, calls=%fused_computation.4 | convolution fusion | flops 268435456 | bytes 17301504 | tf_op jit(solution)/shard_map/trsak,ctrswk->kacw/dot_general | solution.py:63
  132.9 10.2 %copy.23 = f32[128,32,4,128]{0,3,2,1:T(8,128)} copy(f32[128,32,4,128]{3,1,2,0:T(8,128)} %convolution_bitcast_fusion) | data formatting | bytes 16777216 | tf_op jit(solution)/shard_map/trsak,ctrswk->kacw/dot_general | solution.py:63
  143.1 0.0 copy-start
  143.1 7.2 %fusion.1 = f32[16,512,256,1]{2,1,0,3:T(8,128)S(1)} fusion(bf16[2,128,256,1]{2,1,3,0:T(8,128)(2,1)S(1)} %bitcast.47, f32[128,2,16,512]{0,3,2,1:T(8,128)} %bitcast.42), kind=kOutput, calls=%fused_computation.3 | convolution fusion | flops 1082130432 | bytes 16908288 | tf_op jit(solution)/shard_map/krij,rkl->ijl/dot_general | solution.py:70
  150.3 1.0 copy-done
  151.2 4.7 %fusion = f32[16,512,256]{2,1,0:T(8,128)} fusion(f32[16,512,256,1]{2,1,0,3:T(8,128)S(1)} %fusion.1, bf16[2,128,256,1]{2,1,3,0:T(8,128)(2,1)S(1)} %bitcast.48, f32[128,2,16,512]{0,3,2,1:T(8,128)S(1)} %bitcast.43), kind=kOutput, calls=%fused_computation.1 | convolution fusion | flops 1080033280 | bytes 25296896 | tf_op jit(solution)/shard_map/krij,rkl->ijl/dot_general | solution.py:68
  (6 shorter events, 0.1 us)
Async XLA Ops:
  6.5 99.5 %all-gather.2.cloned.1.call-start = ((), (), s32[]{:S(2)}) async-start(), calls=%async_computation | async-start | bytes 8650752 | tf_op jit(solution)/shard_map/all_gather | solution.py:55
  143.1 8.2 %copy-start = (f32[128,32,4,128]{0,3,2,1:T(8,128)S(1)}, f32[128,32,4,128]{0,3,2,1:T(8,128)}, u32[]{:S(2)}) copy-start(f32[128,32,4,128]{0,3,2,1:T(8,128)} %copy.23) | copy-start | bytes 25165828
Sparse Core Ops, SparseCore 0:
  25.9 80.0 all-gather.1

commit v3 on v2

v3 whole, which is shorter than its diff:
```python
import math

import jax
import jax.numpy as jnp
from jax import lax
from jax.sharding import PartitionSpec as P

LAGS = 256


def whiten(real_part, imag_part):
    power = real_part * real_part + imag_part * imag_part
    level = jnp.mean(power, axis=-1, keepdims=True)
    factor = 1.0 / jnp.sqrt(power + 0.1 * level + 1e-06)
    return (real_part * factor, imag_part * factor)


def lag_table(freq_count, sample_count, lag_count):
    freq_index = jnp.arange(1, freq_count + 1, dtype=jnp.int32)
    lag_index = jnp.arange(lag_count, dtype=jnp.int32) - lag_count // 2
    turns = freq_index[:, None] * (lag_index[None, :] % sample_count) % sample_count
    angle = turns.astype(jnp.float32) * (2.0 * math.pi / sample_count)
    return jnp.concatenate([jnp.cos(angle), -jnp.sin(angle)], axis=0).astype(jnp.bfloat16)


def folded_tables(sample_count, freq_count):
    raw_index = jnp.arange(2 * sample_count, dtype=jnp.int32)[:, None]
    freq_index = jnp.arange(1, freq_count + 1, dtype=jnp.int32)[None, :]
    base_time = raw_index // 2
    odd = (raw_index % 2) == 1
    scale = 2.0 * math.pi / sample_count
    first_angle = (base_time * freq_index % sample_count).astype(jnp.float32) * scale
    second_angle = ((base_time + 1) * freq_index % sample_count).astype(jnp.float32) * scale
    has_next = odd & (base_time + 1 < sample_count)
    first_weight = jnp.where(odd, 0.25, 0.5)
    second_weight = jnp.where(has_next, 0.25, 0.0)
    cos_part = first_weight * jnp.cos(first_angle) + second_weight * jnp.cos(second_angle)
    sin_part = -(first_weight * jnp.sin(first_angle) + second_weight * jnp.sin(second_angle))
    return jnp.concatenate([cos_part, sin_part], axis=1)


def per_device(raw_samples):
    seg_count, block_width, raw_length = raw_samples.shape
    sample_count = raw_length // 2
    freq_count = sample_count // 8
    chan_count = lax.axis_size("chan")
    time_count = lax.axis_size("zz") * lax.axis_size("core")
    channel_total = block_width * chan_count
    row_width = channel_total // (chan_count * time_count)
    raw_rows = raw_samples.reshape(seg_count * block_width, raw_length)
    folded = folded_tables(sample_count, freq_count)
    spectrum = jnp.dot(
        raw_rows, folded, precision=lax.Precision.HIGH, preferred_element_type=jnp.float32
    )
    real_part = spectrum[:, :freq_count].reshape(seg_count, block_width, freq_count)
    imag_part = spectrum[:, freq_count:].reshape(seg_count, block_width, freq_count)
    real_w, imag_w = whiten(real_part, imag_part)
    local_spec = jnp.stack([real_w, imag_w], axis=0).astype(jnp.bfloat16)
    core_count = 2
    same_core = lax.all_gather(local_spec, ("chan", "zz"), axis=0)
    every = lax.all_gather(same_core, "core", axis=0)
    every = every.reshape(
        core_count, chan_count, time_count // core_count, 2, seg_count, block_width, freq_count
    )
    chan_index = lax.axis_index("chan")
    tm_index = lax.axis_index("zz") * core_count + lax.axis_index("core")
    own_block = lax.dynamic_index_in_dim(every, chan_index, 1, keepdims=False)
    rows = lax.dynamic_slice_in_dim(own_block, tm_index * row_width, row_width, axis=4)
    turned = jnp.stack([rows[:, :, 1], -rows[:, :, 0]], axis=2)
    left = jnp.concatenate([rows, turned], axis=4)
    cross = jnp.einsum("hzrsak,hczrswk->kacw", left, every, preferred_element_type=jnp.float32)
    cross = cross.reshape(freq_count, 2, row_width, channel_total)
    table = lag_table(freq_count, sample_count, LAGS).reshape(2, freq_count, LAGS)
    high = cross.astype(jnp.bfloat16)
    low = (cross - high.astype(jnp.float32)).astype(jnp.bfloat16)
    pair_lags = jnp.einsum(
        "krij,rkl->ijl", high, table, preferred_element_type=jnp.float32
    ) + jnp.einsum("krij,rkl->ijl", low, table, preferred_element_type=jnp.float32)
    norm_scale = 1.0 / math.sqrt(freq_count * seg_count * time_count)
    return pair_lags * norm_scale


def solution(mesh):
    chan_count, time_count = mesh.devices.shape
    split_mesh = jax.sharding.Mesh(
        mesh.devices.reshape(chan_count, time_count // 2, 2), ("chan", "zz", "core")
    )
    return jax.shard_map(
        per_device,
        mesh=split_mesh,
        in_specs=(P(("zz", "core"), "chan", None),),
        out_specs=P(("chan", "zz", "core"), None, None),
        check_vma=False,
    )
```

time: 163 us -> 183 us (1.12)
  waiting for transfers between devices: 79.6 us -> 97.9 us
  local copies, waits for them, and re-layouts: 34.4 us -> 28.9 us
  other arithmetic: 5.87 us -> 10.9 us
    all_gather x1 -> x2, waiting for transfers between devices: 79.6 us -> 97.9 us  [the longest x1 78.5 us: per_device(): same_core = lax.all_gather(local_spec, ('chan', 'zz'), axis=0)]
    add x2, other arithmetic: 0.11 us -> 9.28 us  [the longest x1 9.28 us: folded_tables(): first_weight * jnp.cos(first_angle) + second_weight * jnp.cos(second_angle)]
    reshape x2 -> x1, local copies, waits for them, and re-layouts: 17.2 us -> 14.5 us  [per_device(): every.reshape(core_count, chan_count, time_count // core_count, 2, seg_co...]
    concatenate x3 -> x1, other arithmetic: 2.19 us -> 0.04 us  [per_device(): left = jnp.concatenate([rows, turned], axis=4)]
    another operation x2 -> x1, other arithmetic: 2.5 us -> 0.61 us  [the longest x1 1.89 us: per_device(): jnp.stack([0.5 * both_tables, 0.25 * both_tables + 0.25 * next_tables], a...]
  transfers between devices with their start and end apart: 1 -> 2, of which waited for: 1 -> 2; matrix products, arithmetic and copies ran while one was open for 0% -> 0% of each run, Pallas kernels for 0% -> 0%
where the time goes in v3:
time: 183 us; the launch traced here: 182 us
  waiting for transfers between devices  97.9 us (53%)
  matrix products  30.4 us (17%)
  local copies, waits for them, and re-layouts  28.9 us (16%)
  between operations  13.5 us (7%)
  other arithmetic  10.9 us (6%)
    all_gather x1, waiting for transfers between devices, per_device(): same_core = lax.all_gather(local_spec, ('chan', 'zz'), axis=0)  78.5 us
    all_gather x1, waiting for transfers between devices, per_device(): every = lax.all_gather(same_core, 'core', axis=0)  19.3 us
    reshape x1, local copies, waits for them, and re-layouts, per_device(): every.reshape(core_count, chan_count, time_count // core_count, 2, seg_co...  14.5 us
    dot_general x1, matrix products, per_device(): jnp.einsum('hzrsak,hczrswk->kacw', left, every, preferred_element_type=jn...  12.7 us
    dot_general x1, local copies, waits for them, and re-layouts, per_device(): jnp.einsum('hzrsak,hczrswk->kacw', left, every, preferred_element_type=jn...  10.2 us
    add x1, other arithmetic, folded_tables(): first_weight * jnp.cos(first_angle) + second_weight * jnp.cos(second_angle)  9.28 us
    dot_general x1, matrix products, per_device(): jnp.einsum('krij,rkl->ijl', low, table, preferred_element_type=jnp.float32)  7.19 us
    dot_general x1, matrix products, per_device(): jnp.dot(raw_rows, folded, precision=lax.Precision.HIGH, preferred_element...  5.85 us
  transfers between devices with their start and end apart: 2, of which 2 were waited for; matrix products, arithmetic and copies ran while one was open for 0% of the time, Pallas kernels for 0%

profile of v3, /device:TPU:0, one launch (start us, length us, event | category | flops | bytes accessed | tf_op | source)
XLA Modules:
  0.0 181.9 jit_solution(13722958136162670204)
XLA Ops:
  6.5 0.0 all-gather.4.cloned.1.call-start
  6.6 9.3 %multiply_add_fusion = (f32[2048,128]{1,0:T(8,128)S(1)}, f32[2048,128]{1,0:T(8,128)S(1)}) fusion(f32[2048]{0:T(1024)S(1)} %get-tuple-element.18, s32[128]{0:T(128)S(1)} %iota_add_fusion, s32[2048]{0:T(1024)S(1)} %get-tuple-element.17, s32[2048]{0:T(1024)S(1)} %get-tuple-element.16, f32[2048]{0:T(1024)S(1)} %get-tuple-element.19), kind=kLoop, calls=%fused_computation.29 | loop fusion | flops 9175040 | bytes 2130432 | tf_op jit(solution)/shard_map/add | solution.py:37
  15.8 5.8 %fusion.8 = f32[512,256]{0,1:T(8,128)S(1)} fusion(f32[512,2048]{1,0:T(8,128)} %bitcast.39, f32[2048,128]{1,0:T(8,128)S(1)} %get-tuple-element.13, f32[2048,128]{1,0:T(8,128)S(1)} %get-tuple-element.12), kind=kOutput, calls=%fused_computation.21 | convolution fusion | flops 1611137024 | bytes 6815744 | tf_op jit(solution)/shard_map/dot_general | solution.py:52
  21.7 0.1 add_reduce_fusion
  21.8 0.1 copy.31
  21.9 0.1 copy.32
  22.1 0.2 fusion.20
  22.2 0.7 pad_maximum_fusion
  22.9 0.0 all-gather.4.cloned.1.call-update
  23.0 0.2 all-gather.6.cloned.1.call-start
  23.2 78.5 %all-gather.4.cloned.1.call-done = bf16[16,2,4,128,128]{4,3,2,1,0:T(8,128)(2,1)} async-done(((bf16[1,2,4,128,128]{4,3,2,1,0:T(8,128)(2,1)}), bf16[16,2,4,128,128]{4,3,2,1,0:T(8,128)(2,1)}) %all-gather.4.cloned.1.call-update) | async-done | bytes 4194320 | tf_op jit(solution)/shard_map/all_gather | solution.py:60
  101.7 0.0 all-gather.6.cloned.1.call-update
  101.8 0.6 cosine_convert_fusion
  102.4 19.3 %all-gather.6.cloned.1.call-done = bf16[32,2,4,128,128]{4,3,2,1,0:T(8,128)(2,1)} async-done(((bf16[16,2,4,128,128]{4,3,2,1,0:T(8,128)(2,1)}), bf16[32,2,4,128,128]{4,3,2,1,0:T(8,128)(2,1)}) %all-gather.6.cloned.1.call-update) | async-done | bytes 8388624 | tf_op jit(solution)/shard_map/all_gather | solution.py:61
  121.8 14.5 %copy.23 = bf16[2,4,4,2,4,128,128]{5,2,4,3,0,1,6:T(4,128)(2,1)} copy(bf16[2,4,4,2,4,128,128]{6,5,4,3,2,1,0:T(8,128)(2,1)} %bitcast.37) | data formatting | bytes 16777216 | tf_op jit(solution)/shard_map/reshape | solution.py:62
  136.3 1.1 dynamic-slice_bitcast_fusion
  137.5 1.9 %copy.22 = bf16[2,4,2,4,32,128,1]{4,1,3,2,0,6,5:T(4,128)(2,1)S(1)} copy(bf16[2,4,2,4,32,128,1]{5,4,3,2,1,0,6:T(8,128)(2,1)S(1)} %maximum_bitcast_fusion) | data formatting | bytes 1048576 | tf_op jit(solution)/shard_map/concatenate | solution.py:70
  139.4 12.7 %convolution_bitcast_fusion = f32[128,32,4,128]{3,1,2,0:T(8,128)} fusion(bf16[2,4,2,4,32,128,1]{4,1,3,2,0,6,5:T(4,128)(2,1)S(1)} %copy.22, bf16[2,4,4,2,4,128,128]{5,2,4,3,0,1,6:T(4,128)(2,1)} %copy.23), kind=kOutput, calls=%fused_computation.4 | convolution fusion | flops 268435456 | bytes 17301504 | tf_op jit(solution)/shard_map/hzrsak,hczrswk->kacw/dot_general | solution.py:71
  152.1 10.2 %copy.21 = f32[128,32,4,128]{0,3,2,1:T(8,128)} copy(f32[128,32,4,128]{3,1,2,0:T(8,128)} %convolution_bitcast_fusion) | data formatting | bytes 16777216 | tf_op jit(solution)/shard_map/hzrsak,hczrswk->kacw/dot_general | solution.py:71
  162.2 0.0 copy-start
  162.2 7.2 %fusion.1 = f32[16,512,256,1]{2,1,0,3:T(8,128)S(1)} fusion(bf16[2,128,256,1]{2,1,3,0:T(8,128)(2,1)S(1)} %bitcast.40, f32[128,2,16,512]{0,3,2,1:T(8,128)} %bitcast.35), kind=kOutput, calls=%fused_computation.3 | convolution fusion | flops 1082130432 | bytes 16908288 | tf_op jit(solution)/shard_map/krij,rkl->ijl/dot_general | solution.py:78
  169.4 1.0 copy-done
  170.4 4.7 %fusion = f32[16,512,256]{2,1,0:T(8,128)} fusion(f32[16,512,256,1]{2,1,0,3:T(8,128)S(1)} %fusion.1, bf16[2,128,256,1]{2,1,3,0:T(8,128)(2,1)S(1)} %bitcast.41, f32[128,2,16,512]{0,3,2,1:T(8,128)S(1)} %bitcast.36), kind=kOutput, calls=%fused_computation.1 | convolution fusion | flops 1080033280 | bytes 25296896 | tf_op jit(solution)/shard_map/krij,rkl->ijl/dot_general | solution.py:76
  (8 shorter events, 0.1 us)
Async XLA Ops:
  6.5 95.2 %all-gather.4.cloned.1.call-start = ((), (), s32[]{:S(2)}) async-start(), calls=%async_computation | async-start | bytes 4456448 | tf_op jit(solution)/shard_map/all_gather | solution.py:60
  23.0 98.8 %all-gather.6.cloned.1.call-start = ((), (), s32[]{:S(2)}) async-start(), calls=%async_computation.1 | async-start | bytes 12582912 | tf_op jit(solution)/shard_map/all_gather | solution.py:61
  162.2 8.2 %copy-start = (f32[128,32,4,128]{0,3,2,1:T(8,128)S(1)}, f32[128,32,4,128]{0,3,2,1:T(8,128)}, u32[]{:S(2)}) copy-start(f32[128,32,4,128]{0,3,2,1:T(8,128)} %copy.21) | copy-start | bytes 25165828
Sparse Core Ops, SparseCore 0:
  23.1 78.5 all-gather.3
  103.3 18.4 all-gather.5

commit v4 on v2

--- a/solution.py
+++ b/solution.py
@@ -23,12 +23,34 @@
     return jnp.concatenate([jnp.cos(angle), -jnp.sin(angle)], axis=0).astype(jnp.bfloat16)
 
 
-def transform_tables(sample_count, freq_count):
-    time_index = jnp.arange(sample_count, dtype=jnp.int32)
-    freq_index = jnp.arange(1, freq_count + 1, dtype=jnp.int32)
-    turns = time_index[:, None] * freq_index[None, :] % sample_count
-    angle = turns.astype(jnp.float32) * (2.0 * math.pi / sample_count)
-    return (jnp.cos(angle), -jnp.sin(angle))
+def folded_tables(sample_count, freq_count):
+    fine_rows = 64
+    coarse_rows = 2 * sample_count // fine_rows
+    scale = 2.0 * math.pi / sample_count
+    freq_index = jnp.arange(1, freq_count + 1, dtype=jnp.int32)[None, None, :]
+    coarse_time = jnp.arange(coarse_rows, dtype=jnp.int32)[:, None, None] * (fine_rows // 2)
+    fine = jnp.arange(fine_rows, dtype=jnp.int32)[None, :, None]
+    fine_time = fine // 2
+    odd = (fine % 2) == 1
+
+    def angle(times):
+        return (times * freq_index % sample_count).astype(jnp.float32) * scale
+
+    coarse_angle = angle(coarse_time)
+    coarse_cos, coarse_sin = jnp.cos(coarse_angle), jnp.sin(coarse_angle)
+    this_angle = angle(fine_time)
+    next_angle = angle(fine_time + 1)
+    this_cos = coarse_cos * jnp.cos(this_angle) - coarse_sin * jnp.sin(this_angle)
+    this_sin = coarse_sin * jnp.cos(this_angle) + coarse_cos * jnp.sin(this_angle)
+    next_cos = coarse_cos * jnp.cos(next_angle) - coarse_sin * jnp.sin(next_angle)
+    next_sin = coarse_sin * jnp.cos(next_angle) + coarse_cos * jnp.sin(next_angle)
+    last_row = (coarse_time + fine_time + 1) >= sample_count
+    this_weight = jnp.where(odd, 0.25, 0.5)
+    next_weight = jnp.where(odd & ~last_row, 0.25, 0.0)
+    cos_part = this_weight * this_cos + next_weight * next_cos
+    sin_part = -(this_weight * this_sin + next_weight * next_sin)
+    both = jnp.concatenate([cos_part, sin_part], axis=-1)
+    return both.reshape(2 * sample_count, 2 * freq_count)
 
 
 def per_device(raw_samples):
@@ -40,13 +62,9 @@
     channel_total = block_width * chan_count
     row_width = channel_total // (chan_count * time_count)
     raw_rows = raw_samples.reshape(seg_count * block_width, raw_length)
-    cos_table, sin_table = transform_tables(sample_count, freq_count)
-    both_tables = jnp.concatenate([cos_table, sin_table], axis=1)
-    next_tables = jnp.concatenate([both_tables[1:], jnp.zeros_like(both_tables[:1])], axis=0)
-    folded = jnp.stack([0.5 * both_tables, 0.25 * both_tables + 0.25 * next_tables], axis=1)
-    folded = folded.reshape(raw_length, 2 * freq_count)
+    folded = folded_tables(sample_count, freq_count)
     spectrum = jnp.dot(
-        raw_rows, folded, precision=lax.Precision.HIGHEST, preferred_element_type=jnp.float32
+        raw_rows, folded, precision=lax.Precision.HIGH, preferred_element_type=jnp.float32
     )
     real_part = spectrum[:, :freq_count].reshape(seg_count, block_width, freq_count)
     imag_part = spectrum[:, freq_count:].reshape(seg_count, block_width, freq_count)

time: 163 us -> 152 us (0.933)
  matrix products: 29.3 us -> 23.6 us
  local copies, waits for them, and re-layouts: 34.4 us -> 30.9 us
  other arithmetic: 5.87 us -> 3.77 us
    dot_general x1, matrix products: 9.32 us -> 3.63 us  [per_device(): jnp.dot(raw_rows, folded, precision=lax.Precision.HIGH, preferred_element...]
    reshape x1 -> x0, local copies, waits for them, and re-layouts: 2.62 us -> none  [per_device(): folded = folded.reshape(raw_length, 2 * freq_count)]
    concatenate x2 -> x0, other arithmetic: 2.15 us -> none  [per_device(): both_tables = jnp.concatenate([cos_table, sin_table], axis=1)]
    another operation x2 -> x1, other arithmetic: 2.5 us -> 0.61 us  [the longest x1 1.89 us: per_device(): jnp.stack([0.5 * both_tables, 0.25 * both_tables + 0.25 * next_tables], a...]
where the time goes in v4:
time: 152 us
  waiting for transfers between devices  79.6 us (52%)
  local copies, waits for them, and re-layouts  30.9 us (20%)
  matrix products  23.6 us (16%)
  between operations  13.6 us (9%)
  other arithmetic  3.77 us (2%)
    all_gather x1, waiting for transfers between devices, per_device(): every = lax.all_gather(local_spec, ('chan', 'tm'), axis=0)  79.6 us
    reshape x1, local copies, waits for them, and re-layouts, per_device(): every.reshape(chan_count, time_count, 2, seg_count, block_width, freq_count)  14.5 us
    dot_general x1, local copies, waits for them, and re-layouts, per_device(): jnp.einsum('trsak,ctrswk->kacw', left, every, preferred_element_type=jnp....  10.2 us
    dot_general x1, matrix products, per_device(): jnp.einsum('trsak,ctrswk->kacw', left, every, preferred_element_type=jnp....  8.15 us
    dot_general x1, matrix products, per_device(): jnp.einsum('krij,rkl->ijl', low, table, preferred_element_type=jnp.float32)  7.18 us
    dot_general x1, matrix products, per_device(): jnp.einsum('krij,rkl->ijl', high, table, preferred_element_type=jnp.float32)  4.66 us
    dot_general x1, matrix products, per_device(): jnp.dot(raw_rows, folded, precision=lax.Precision.HIGH, preferred_element...  3.63 us
  transfers between devices with their start and end apart: 1, of which 1 were waited for; matrix products, arithmetic and copies ran while one was open for 0% of the time, Pallas kernels for 0%

profile of v4, /device:TPU:0, one launch (start us, length us, event | category | flops | bytes accessed | tf_op | source)
XLA Modules:
  0.0 151.5 jit_solution(12316861653045598019)
XLA Ops:
  6.5 0.0 all-gather.2.cloned.1.call-start
  6.6 0.3 fusion.31
  6.9 0.2 fusion.33
  7.1 0.1 add.306
  7.2 0.1 add.303
  7.2 0.1 add.304
  7.3 0.1 and.156
  7.4 0.1 mul.429
  7.5 0.0 copy-start.1
  7.5 0.6 multiply_subtract_fusion.1
  8.1 1.0 fusion.13
  9.1 0.6 copy-done.1
  9.7 3.6 %fusion.8 = f32[512,256]{0,1:T(8,128)S(1)} fusion(f32[512,2048]{1,0:T(8,128)S(1)} %bitcast.61, f32[2048,128]{1,0:T(8,128)S(1)} %get-tuple-element.19, f32[2048,128]{1,0:T(8,128)S(1)} %get-tuple-element.18), kind=kOutput, calls=%fused_computation.11 | convolution fusion | flops 1611137024 | bytes 6815744 | tf_op jit(solution)/shard_map/dot_general | solution.py:66
  13.3 0.1 add_reduce_fusion
  13.4 0.1 copy.27
  13.5 0.1 copy.28
  13.7 0.2 fusion.17
  13.8 0.7 pad_maximum_fusion
  14.6 0.0 all-gather.2.cloned.1.call-update
  14.6 0.6 cosine_convert_fusion
  15.2 79.6 %all-gather.2.cloned.1.call-done = bf16[32,2,4,128,128]{4,3,2,1,0:T(8,128)(2,1)} async-done(((bf16[1,2,4,128,128]{4,3,2,1,0:T(8,128)(2,1)}), bf16[32,2,4,128,128]{4,3,2,1,0:T(8,128)(2,1)}) %all-gather.2.cloned.1.call-update) | async-done | bytes 8388624 | tf_op jit(solution)/shard_map/all_gather | solution.py:73
  94.8 14.5 %copy.20 = bf16[4,8,2,4,128,128]{4,1,3,2,0,5:T(8,128)(2,1)} copy(bf16[4,8,2,4,128,128]{5,4,3,2,1,0:T(8,128)(2,1)} %bitcast.59) | data formatting | bytes 16777216 | tf_op jit(solution)/shard_map/reshape | solution.py:74
  109.4 1.1 dynamic-slice_bitcast_fusion
  110.5 3.0 %copy.22 = bf16[8,2,4,32,128,1]{3,0,2,1,5,4:T(8,128)(2,1)S(1)} copy(bf16[8,2,4,32,128,1]{4,3,2,1,0,5:T(8,128)(2,1)S(1)} %maximum_bitcast_fusion) | data formatting | bytes 1048576 | tf_op jit(solution)/shard_map/concatenate | solution.py:80
  113.5 8.2 %convolution_bitcast_fusion = f32[128,32,4,128]{3,1,2,0:T(8,128)} fusion(bf16[8,2,4,32,128,1]{3,0,2,1,5,4:T(8,128)(2,1)S(1)} %copy.22, bf16[4,8,2,4,128,128]{4,1,3,2,0,5:T(8,128)(2,1)} %copy.20), kind=kOutput, calls=%fused_computation.4 | convolution fusion | flops 268435456 | bytes 17301504 | tf_op jit(solution)/shard_map/trsak,ctrswk->kacw/dot_general | solution.py:81
  121.7 10.2 %copy.21 = f32[128,32,4,128]{0,3,2,1:T(8,128)} copy(f32[128,32,4,128]{3,1,2,0:T(8,128)} %convolution_bitcast_fusion) | data formatting | bytes 16777216 | tf_op jit(solution)/shard_map/trsak,ctrswk->kacw/dot_general | solution.py:81
  131.8 0.0 copy-start
  131.8 7.2 %fusion.1 = f32[16,512,256,1]{2,1,0,3:T(8,128)S(1)} fusion(bf16[2,128,256,1]{2,1,3,0:T(8,128)(2,1)S(1)} %bitcast.62, f32[128,2,16,512]{0,3,2,1:T(8,128)} %bitcast.57), kind=kOutput, calls=%fused_computation.3 | convolution fusion | flops 1082130432 | bytes 16908288 | tf_op jit(solution)/shard_map/krij,rkl->ijl/dot_general | solution.py:88
  139.0 1.0 copy-done
  140.0 4.7 %fusion = f32[16,512,256]{2,1,0:T(8,128)} fusion(f32[16,512,256,1]{2,1,0,3:T(8,128)S(1)} %fusion.1, bf16[2,128,256,1]{2,1,3,0:T(8,128)(2,1)S(1)} %bitcast.63, f32[128,2,16,512]{0,3,2,1:T(8,128)S(1)} %bitcast.58), kind=kOutput, calls=%fused_computation.1 | convolution fusion | flops 1080033280 | bytes 25296896 | tf_op jit(solution)/shard_map/krij,rkl->ijl/dot_general | solution.py:86
  (14 shorter events, 0.2 us)
Async XLA Ops:
  6.5 88.3 %all-gather.2.cloned.1.call-start = ((), (), s32[]{:S(2)}) async-start(), calls=%async_computation | async-start | bytes 8650752 | tf_op jit(solution)/shard_map/all_gather | solution.py:73
  7.5 2.2 %copy-start.1 = (f32[4,128,2048]{2,1,0:T(8,128)S(1)}, f32[4,128,2048]{2,1,0:T(8,128)}, u32[]{:S(2)}) copy-start(f32[4,128,2048]{2,1,0:T(8,128)} %param.1) | copy-start | bytes 12582916
  131.8 8.2 %copy-start = (f32[128,32,4,128]{0,3,2,1:T(8,128)S(1)}, f32[128,32,4,128]{0,3,2,1:T(8,128)}, u32[]{:S(2)}) copy-start(f32[128,32,4,128]{0,3,2,1:T(8,128)} %copy.21) | copy-start | bytes 25165828
Sparse Core Ops, SparseCore 0:
  14.7 80.0 all-gather.1

commit v5 on v4

--- a/solution.py
+++ b/solution.py
@@ -70,22 +70,35 @@
     imag_part = spectrum[:, freq_count:].reshape(seg_count, block_width, freq_count)
     real_w, imag_w = whiten(real_part, imag_part)
     local_spec = jnp.stack([real_w, imag_w], axis=0).astype(jnp.bfloat16)
-    every = lax.all_gather(local_spec, ("chan", "tm"), axis=0)
-    every = every.reshape(chan_count, time_count, 2, seg_count, block_width, freq_count)
+    local_spec = jnp.transpose(local_spec, (3, 0, 1, 2)).reshape(
+        freq_count, 2 * seg_count, block_width
+    )
+    every = lax.all_gather(local_spec, ("chan", "tm"), axis=1)
+    every = every.reshape(freq_count, chan_count, time_count, 2 * seg_count, block_width)
     chan_index = lax.axis_index("chan")
     tm_index = lax.axis_index("tm")
-    own_block = lax.dynamic_index_in_dim(every, chan_index, 0, keepdims=False)
+    own_block = lax.dynamic_index_in_dim(every, chan_index, 1, keepdims=False)
     rows = lax.dynamic_slice_in_dim(own_block, tm_index * row_width, row_width, axis=3)
-    turned = jnp.stack([rows[:, 1], -rows[:, 0]], axis=1)
-    left = jnp.concatenate([rows, turned], axis=3)
-    cross = jnp.einsum("trsak,ctrswk->kacw", left, every, preferred_element_type=jnp.float32)
-    cross = cross.reshape(freq_count, 2, row_width, channel_total)
+    rows = rows.reshape(freq_count, time_count, 2, seg_count, row_width)
+    turned = jnp.stack([rows[:, :, 1], -rows[:, :, 0]], axis=2)
+    left = jnp.concatenate([rows, turned], axis=4).reshape(
+        freq_count, time_count * 2 * seg_count, 2 * row_width
+    )
+    every = every.reshape(freq_count, chan_count, time_count * 2 * seg_count, block_width)
     table = lag_table(freq_count, sample_count, LAGS).reshape(2, freq_count, LAGS)
-    high = cross.astype(jnp.bfloat16)
-    low = (cross - high.astype(jnp.float32)).astype(jnp.bfloat16)
-    pair_lags = jnp.einsum(
-        "krij,rkl->ijl", high, table, preferred_element_type=jnp.float32
-    ) + jnp.einsum("krij,rkl->ijl", low, table, preferred_element_type=jnp.float32)
+    column_blocks = []
+    for column_chan in range(chan_count):
+        cross = jnp.einsum(
+            "kqa,kqw->kaw", left, every[:, column_chan], preferred_element_type=jnp.float32
+        )
+        cross = cross.reshape(freq_count, 2, row_width, block_width)
+        high = cross.astype(jnp.bfloat16)
+        low = (cross - high.astype(jnp.float32)).astype(jnp.bfloat16)
+        column_blocks.append(
+            jnp.einsum("kriw,rkl->iwl", high, table, preferred_element_type=jnp.float32)
+            + jnp.einsum("kriw,rkl->iwl", low, table, preferred_element_type=jnp.float32)
+        )
+    pair_lags = jnp.concatenate(column_blocks, axis=1)
     norm_scale = 1.0 / math.sqrt(freq_count * seg_count * time_count)
     return pair_lags * norm_scale
 

time: 152 us -> 160 us (1.053)
  other arithmetic: 3.77 us -> 6.82 us
  local copies, waits for them, and re-layouts: 30.9 us -> 33.2 us
  matrix products: 23.6 us -> 25.9 us
    dot_general x1 -> x0, local copies, waits for them, and re-layouts: 10.2 us -> none  [per_device(): jnp.einsum('trsak,ctrswk->kacw', left, every, preferred_element_type=jnp....]
    all_gather x0 -> x1, local copies, waits for them, and re-layouts: none -> 9.18 us  [per_device(): every = lax.all_gather(local_spec, ('chan', 'tm'), axis=1)]
    reshape x1 -> x4, local copies, waits for them, and re-layouts: 14.5 us -> 8.89 us  [per_device(): cross = cross.reshape(freq_count, 2, row_width, block_width)]
    mul x0 -> x1, other arithmetic: none -> 3.81 us  [per_device(): return pair_lags * norm_scale]
    dynamic_slice x1 -> x2, local copies, waits for them, and re-layouts: 1.1 us -> 4.56 us  [per_device(): lax.dynamic_slice_in_dim(own_block, tm_index * row_width, row_width, axis=3)]
    concatenate x1 -> x3, local copies, waits for them, and re-layouts: 2.98 us -> 6.1 us  [per_device(): jnp.concatenate([rows, turned], axis=4)]
    dot_general x3 -> x12, matrix products: 20 us -> 22.3 us  [the longest x4 14.4 us: per_device(): jnp.einsum('kqa,kqw->kaw', left, every[:, column_chan], preferred_element...]
where the time goes in v5:
time: 160 us; the launch traced here: 159 us
  waiting for transfers between devices  79.6 us (50%)
  local copies, waits for them, and re-layouts  33.2 us (21%)
  matrix products  25.9 us (16%)
  between operations  13.6 us (8%)
  other arithmetic  6.82 us (4%)
    all_gather x1, waiting for transfers between devices, per_device(): every = lax.all_gather(local_spec, ('chan', 'tm'), axis=1)  79.6 us
    dot_general x4, matrix products, per_device(): jnp.einsum('kqa,kqw->kaw', left, every[:, column_chan], preferred_element...  14.4 us
    all_gather x1, local copies, waits for them, and re-layouts, per_device(): every = lax.all_gather(local_spec, ('chan', 'tm'), axis=1)  9.18 us
    reshape x4, local copies, waits for them, and re-layouts, per_device(): cross = cross.reshape(freq_count, 2, row_width, block_width)  8.89 us
    concatenate x3, local copies, waits for them, and re-layouts, per_device(): jnp.concatenate([rows, turned], axis=4)  6.1 us
    dynamic_slice x2, local copies, waits for them, and re-layouts, per_device(): lax.dynamic_slice_in_dim(own_block, tm_index * row_width, row_width, axis=3)  4.56 us
    dot_general x4, matrix products, per_device(): jnp.einsum('kriw,rkl->iwl', low, table, preferred_element_type=jnp.float32)  4.4 us
    mul x1, other arithmetic, per_device(): return pair_lags * norm_scale  3.81 us
  transfers between devices with their start and end apart: 1, of which 1 were waited for; matrix products, arithmetic and copies ran while one was open for 0% of the time, Pallas kernels for 0%

profile of v5, /device:TPU:0, one launch (start us, length us, event | category | flops | bytes accessed | tf_op | source)
XLA Modules:
  0.0 159.2 jit_solution(15601011110743458039)
XLA Ops:
  6.5 0.0 all-gather.2.cloned.1.call-start
  6.6 0.1 and.156
  6.7 0.1 mul.393
  6.8 0.1 add.278
  6.8 0.1 add.275
  6.9 0.1 add.276
  7.0 0.2 fusion.43
  7.1 0.3 fusion.41
  7.5 0.6 multiply_subtract_fusion.1
  8.1 0.0 copy-start.3
  8.1 1.0 fusion.13
  9.1 1.2 copy-done.3
  10.3 3.6 %fusion.8 = f32[512,256]{0,1:T(8,128)S(1)} fusion(f32[512,2048]{1,0:T(8,128)S(1)} %bitcast.116, f32[2048,128]{1,0:T(8,128)S(1)} %get-tuple-element.19, f32[2048,128]{1,0:T(8,128)S(1)} %get-tuple-element.18), kind=kOutput, calls=%fused_computation.21 | convolution fusion | flops 1611137024 | bytes 6815744 | tf_op jit(solution)/shard_map/dot_general | solution.py:66
  13.9 0.1 add_reduce_fusion
  14.0 0.1 reshape.523
  14.1 0.1 reshape.522
  14.2 0.1 multiply_convert_fusion.1
  14.4 0.9 copy.40
  15.2 0.0 all-gather.2.cloned.1.call-update
  15.3 0.6 cosine_convert_fusion
  15.9 79.6 %all-gather.2.cloned.1.call-done = bf16[128,32,8,128]{3,2,0,1:T(8,128)(2,1)} async-done(((bf16[128,1,8,128]{3,2,0,1:T(8,128)(2,1)}), bf16[128,32,8,128]{3,2,0,1:T(8,128)(2,1)}) %all-gather.2.cloned.1.call-update) | async-done | bytes 8388624 | tf_op jit(solution)/shard_map/all_gather | solution.py:76
  95.5 9.2 %copy.41 = bf16[128,32,8,128]{3,2,1,0:T(8,128)(2,1)} copy(bf16[128,32,8,128]{3,2,0,1:T(8,128)(2,1)} %all-gather.2.cloned.1.call-done) | data formatting | bytes 16777216 | tf_op jit(solution)/shard_map/all_gather | solution.py:76
  104.7 3.6 %fusion.60 = bf16[128,64,16]{2,1,0:T(8,128)(2,1)} fusion(bf16[128,4,8,8,128]{4,3,2,1,0:T(8,128)(2,1)} %bitcast.98, s32[]{:T(128)S(6)} %select_n.142, s32[]{:T(128)S(6)} %select_n.144), kind=kLoop, calls=%fused_computation.117 | loop fusion | bytes 524296 | tf_op jit(solution)/shard_map/concatenate | solution.py:84
  108.3 2.3 %constant_dynamic-slice_fusion = bf16[128,1,8,8,16]{4,3,2,1,0:T(8,128)(2,1)S(1)} fusion(bf16[128,4,8,8,128]{4,3,2,1,0:T(8,128)(2,1)} %bitcast.99, s32[]{:T(128)S(6)} %select_n.142, s32[]{:T(128)S(6)} %select_n.144), kind=kLoop, calls=%fused_computation.113 | loop fusion | bytes 524296 | tf_op jit(solution)/shard_map/dynamic_slice | solution.py:81
  110.6 1.9 %copy.44 = bf16[128,64,16]{1,2,0:T(8,128)(2,1)S(1)} copy(bf16[128,64,16]{2,1,0:T(8,128)(2,1)} %fusion.60) | data formatting | bytes 524288 | tf_op jit(solution)/shard_map/concatenate | solution.py:84
  112.6 2.3 %copy.43 = bf16[128,1,8,8,16]{0,4,3,2,1:T(8,128)(2,1)S(1)} copy(bf16[128,1,8,8,16]{4,3,2,1,0:T(8,128)(2,1)S(1)} %constant_dynamic-slice_fusion) | data formatting | bytes 524288 | tf_op jit(solution)/shard_map/dynamic_slice | solution.py:81
  114.9 0.5 copy.45
  115.5 3.6 %fusion.2 = f32[128,32,128]{2,1,0:T(8,128)} fusion(bf16[128,4,64,128]{3,2,1,0:T(8,128)(2,1)} %bitcast.100, bf16[128,64,16]{1,2,0:T(8,128)(2,1)S(1)} %copy.45, bf16[128,64,16]{1,2,0:T(8,128)(2,1)S(1)} %copy.44), kind=kOutput, calls=%fused_computation.6 | convolution fusion | flops 68157440 | bytes 4718592 | tf_op jit(solution)/shard_map/kqa,kqw->kaw/dot_general | solution.py:91
  119.1 3.6 %fusion.1 = f32[128,32,128]{2,1,0:T(8,128)} fusion(bf16[128,4,64,128]{3,2,1,0:T(8,128)(2,1)} %bitcast.101, bf16[128,64,16]{1,2,0:T(8,128)(2,1)S(1)} %copy.45, bf16[128,64,16]{1,2,0:T(8,128)(2,1)S(1)} %copy.44), kind=kOutput, calls=%fused_computation.4 | convolution fusion | flops 68157440 | bytes 4718592 | tf_op jit(solution)/shard_map/kqa,kqw->kaw/dot_general | solution.py:91
  122.7 3.6 %fusion = f32[128,32,128]{2,1,0:T(8,128)} fusion(bf16[128,4,64,128]{3,2,1,0:T(8,128)(2,1)} %bitcast.102, bf16[128,64,16]{1,2,0:T(8,128)(2,1)S(1)} %copy.45, bf16[128,64,16]{1,2,0:T(8,128)(2,1)S(1)} %copy.44), kind=kOutput, calls=%fused_computation.2 | convolution fusion | flops 68157440 | bytes 4718592 | tf_op jit(solution)/shard_map/kqa,kqw->kaw/dot_general | solution.py:91
  126.3 3.6 %fusion.3 = f32[128,32,128]{2,1,0:T(8,128)} fusion(bf16[128,4,64,128]{3,2,1,0:T(8,128)(2,1)} %bitcast.103, bf16[128,64,16]{1,2,0:T(8,128)(2,1)S(1)} %copy.45, bf16[128,64,16]{1,2,0:T(8,128)(2,1)S(1)} %copy.44), kind=kOutput, calls=%fused_computation.8 | convolution fusion | flops 68157440 | bytes 4718592 | tf_op jit(solution)/shard_map/kqa,kqw->kaw/dot_general | solution.py:91
  129.9 2.0 %copy.51 = f32[128,2,16,128]{0,3,1,2:T(8,128)S(1)} copy(f32[128,2,16,128]{3,2,1,0:T(8,128)} %bitcast.115) | data formatting | bytes 4194304 | tf_op jit(solution)/shard_map/reshape | solution.py:94
  131.9 0.4 fusion.21
  132.3 1.8 %bitcast_add_fusion.2 = f32[16,128,256]{2,1,0:T(8,128)} fusion(f32[16,128,256,1]{2,1,3,0:T(8,128)S(1)} %fusion.21, bf16[2,128,256,1]{2,1,0,3:T(8,128)(2,1)S(1)} %bitcast.105, f32[128,2,16,128]{0,3,1,2:T(8,128)S(1)} %copy.51), kind=kOutput, calls=%fused_computation.15 | convolution fusion | flops 271056896 | bytes 6422528 | tf_op jit(solution)/shard_map/kriw,rkl->iwl/dot_general | solution.py:99
  134.1 2.0 %copy.54 = f32[128,2,16,128]{0,3,1,2:T(8,128)S(1)} copy(f32[128,2,16,128]{3,2,1,0:T(8,128)} %bitcast.114) | data formatting | bytes 4194304 | tf_op jit(solution)/shard_map/reshape | solution.py:94
  136.1 0.4 fusion.18
  136.5 1.8 %bitcast_add_fusion.1 = f32[16,128,256]{2,1,0:T(8,128)} fusion(f32[16,128,256,1]{2,1,3,0:T(8,128)S(1)} %fusion.18, bf16[2,128,256,1]{2,1,0,3:T(8,128)(2,1)S(1)} %bitcast.107, f32[128,2,16,128]{0,3,1,2:T(8,128)S(1)} %copy.54), kind=kOutput, calls=%fused_computation.14 | convolution fusion | flops 271056896 | bytes 6422528 | tf_op jit(solution)/shard_map/kriw,rkl->iwl/dot_general | solution.py:99
  138.3 2.0 %copy.48 = f32[128,2,16,128]{0,3,1,2:T(8,128)S(1)} copy(f32[128,2,16,128]{3,2,1,0:T(8,128)} %bitcast.113) | data formatting | bytes 4194304 | tf_op jit(solution)/shard_map/reshape | solution.py:94
  140.3 2.9 %copy.57 = f32[128,2,16,128]{0,3,1,2:T(8,128)} copy(f32[128,2,16,128]{3,2,1,0:T(8,128)} %bitcast.112) | data formatting | bytes 4194304 | tf_op jit(solution)/shard_map/reshape | solution.py:94
  143.2 2.2 %fusion.15 = f32[16,128,256,1]{2,1,3,0:T(8,128)S(1)} fusion(bf16[2,128,256,1]{2,1,0,3:T(8,128)(2,1)S(1)} %bitcast.108, f32[128,2,16,128]{0,3,1,2:T(8,128)} %copy.57), kind=kOutput, calls=%fused_computation.35 | convolution fusion | flops 268959744 | bytes 4325376 | tf_op jit(solution)/shard_map/kriw,rkl->iwl/dot_general | solution.py:98
  145.4 0.1 copy-done
  145.4 0.4 bitcast_add_fusion
  145.9 0.4 fusion.24
  146.3 0.0 copy-start.1
  146.3 0.4 bitcast_add_fusion.3
  146.8 1.1 copy-done.1
  147.9 0.6 copy-done.2
  148.5 3.8 %maximum_multiply_fusion = f32[16,512,256]{2,1,0:T(8,128)} fusion(f32[16,128,256]{2,1,0:T(8,128)S(1)} %bitcast_add_fusion, f32[16,128,256]{2,1,0:T(8,128)S(1)} %copy-done.2, f32[16,128,256]{2,1,0:T(8,128)S(1)} %copy-done.1, f32[16,128,256]{2,1,0:T(8,128)S(1)} %bitcast_add_fusion.3), kind=kLoop, calls=%fused_computation | loop fusion | flops 8388608 | bytes 16777216 | tf_op jit(solution)/shard_map/mul | solution.py:103
  (17 shorter events, 0.2 us)
Async XLA Ops:
  6.5 89.0 %all-gather.2.cloned.1.call-start = ((), (), s32[]{:S(2)}) async-start(), calls=%async_computation | async-start | bytes 8650752 | tf_op jit(solution)/shard_map/all_gather | solution.py:76
  8.1 2.2 %copy-start.3 = (f32[4,128,2048]{2,1,0:T(8,128)S(1)}, f32[4,128,2048]{2,1,0:T(8,128)}, u32[]{:S(2)}) copy-start(f32[4,128,2048]{2,1,0:T(8,128)} %param.1) | copy-start | bytes 12582916
  143.2 2.2 %copy-start = (f32[128,2,16,128]{0,3,1,2:T(8,128)S(1)}, f32[128,2,16,128]{0,3,1,2:T(8,128)}, u32[]{:S(2)}) copy-start(f32[128,2,16,128]{0,3,1,2:T(8,128)} %copy.57) | copy-start | bytes 6291460
  146.3 1.6 %copy-start.1 = (f32[16,128,256]{2,1,0:T(8,128)S(1)}, f32[16,128,256]{2,1,0:T(8,128)}, u32[]{:S(2)}) copy-start(f32[16,128,256]{2,1,0:T(8,128)} %bitcast_add_fusion.2) | copy-start | bytes 6291460
  146.3 2.2 %copy-start.2 = (f32[16,128,256]{2,1,0:T(8,128)S(1)}, f32[16,128,256]{2,1,0:T(8,128)}, u32[]{:S(2)}) copy-start(f32[16,128,256]{2,1,0:T(8,128)} %bitcast_add_fusion.1) | copy-start | bytes 6291460
Sparse Core Ops, SparseCore 0:
  15.4 80.0 all-gather.1

commit v6 on v4

--- a/solution.py
+++ b/solution.py
@@ -78,14 +78,10 @@
     rows = lax.dynamic_slice_in_dim(own_block, tm_index * row_width, row_width, axis=3)
     turned = jnp.stack([rows[:, 1], -rows[:, 0]], axis=1)
     left = jnp.concatenate([rows, turned], axis=3)
-    cross = jnp.einsum("trsak,ctrswk->kacw", left, every, preferred_element_type=jnp.float32)
+    cross = jnp.einsum("trsak,ctrswk->kacw", left, every, preferred_element_type=jnp.bfloat16)
     cross = cross.reshape(freq_count, 2, row_width, channel_total)
     table = lag_table(freq_count, sample_count, LAGS).reshape(2, freq_count, LAGS)
-    high = cross.astype(jnp.bfloat16)
-    low = (cross - high.astype(jnp.float32)).astype(jnp.bfloat16)
-    pair_lags = jnp.einsum(
-        "krij,rkl->ijl", high, table, preferred_element_type=jnp.float32
-    ) + jnp.einsum("krij,rkl->ijl", low, table, preferred_element_type=jnp.float32)
+    pair_lags = jnp.einsum("krij,rkl->ijl", cross, table, preferred_element_type=jnp.float32)
     norm_scale = 1.0 / math.sqrt(freq_count * seg_count * time_count)
     return pair_lags * norm_scale
 

time: 152 us -> 143 us (0.941)
  matrix products: 23.6 us -> 17.3 us
  local copies, waits for them, and re-layouts: 30.9 us -> 28.4 us
    dot_general x2 -> x1, matrix products: 11.8 us -> 6.84 us  [per_device(): jnp.einsum('krij,rkl->ijl', cross, table, preferred_element_type=jnp.floa...]
    dot_general x1, local copies, waits for them, and re-layouts: 10.2 us -> 8.01 us  [per_device(): jnp.einsum('trsak,ctrswk->kacw', left, every, preferred_element_type=jnp....]
where the time goes in v6:
time: 143 us
  waiting for transfers between devices  79.6 us (56%)
  local copies, waits for them, and re-layouts  28.4 us (20%)
  matrix products  17.3 us (12%)
  between operations  13.6 us (10%)
  other arithmetic  3.77 us (3%)
    all_gather x1, waiting for transfers between devices, per_device(): every = lax.all_gather(local_spec, ('chan', 'tm'), axis=0)  79.6 us
    reshape x1, local copies, waits for them, and re-layouts, per_device(): every.reshape(chan_count, time_count, 2, seg_count, block_width, freq_count)  14.5 us
    dot_general x1, local copies, waits for them, and re-layouts, per_device(): jnp.einsum('trsak,ctrswk->kacw', left, every, preferred_element_type=jnp....  8.01 us
    dot_general x1, matrix products, per_device(): jnp.einsum('trsak,ctrswk->kacw', left, every, preferred_element_type=jnp....  6.86 us
    dot_general x1, matrix products, per_device(): jnp.einsum('krij,rkl->ijl', cross, table, preferred_element_type=jnp.floa...  6.84 us
    dot_general x1, matrix products, per_device(): jnp.dot(raw_rows, folded, precision=lax.Precision.HIGH, preferred_element...  3.62 us
    concatenate x1, local copies, waits for them, and re-layouts, per_device(): left = jnp.concatenate([rows, turned], axis=3)  2.98 us
  transfers between devices with their start and end apart: 1, of which 1 were waited for; matrix products, arithmetic and copies ran while one was open for 0% of the time, Pallas kernels for 0%

profile of v6, /device:TPU:0, one launch (start us, length us, event | category | flops | bytes accessed | tf_op | source)
XLA Modules:
  0.0 142.7 jit_solution(2680097948527729366)
XLA Ops:
  6.5 0.0 all-gather.2.cloned.1.call-start
  6.6 0.3 fusion.27
  6.9 0.2 fusion.29
  7.1 0.1 add.303
  7.2 0.1 add.300
  7.2 0.1 add.301
  7.3 0.1 and.156
  7.4 0.1 mul.429
  7.5 0.6 multiply_subtract_fusion.1
  8.1 0.0 copy-start
  8.1 1.0 fusion.9
  9.1 1.2 copy-done
  10.3 3.6 %fusion.4 = f32[512,256]{0,1:T(8,128)S(1)} fusion(f32[512,2048]{1,0:T(8,128)S(1)} %bitcast.56, f32[2048,128]{1,0:T(8,128)S(1)} %get-tuple-element.19, f32[2048,128]{1,0:T(8,128)S(1)} %get-tuple-element.18), kind=kOutput, calls=%fused_computation.6 | convolution fusion | flops 1611137024 | bytes 6815744 | tf_op jit(solution)/shard_map/dot_general | solution.py:66
  13.9 0.1 add_reduce_fusion
  14.0 0.1 copy.26
  14.1 0.1 copy.27
  14.3 0.2 fusion.13
  14.4 0.7 pad_maximum_fusion
  15.2 0.0 all-gather.2.cloned.1.call-update
  15.2 0.6 cosine_convert_fusion
  15.8 79.6 %all-gather.2.cloned.1.call-done = bf16[32,2,4,128,128]{4,3,2,1,0:T(8,128)(2,1)} async-done(((bf16[1,2,4,128,128]{4,3,2,1,0:T(8,128)(2,1)}), bf16[32,2,4,128,128]{4,3,2,1,0:T(8,128)(2,1)}) %all-gather.2.cloned.1.call-update) | async-done | bytes 8388624 | tf_op jit(solution)/shard_map/all_gather | solution.py:73
  95.4 14.5 %copy.19 = bf16[4,8,2,4,128,128]{4,1,3,2,0,5:T(8,128)(2,1)} copy(bf16[4,8,2,4,128,128]{5,4,3,2,1,0:T(8,128)(2,1)} %bitcast.54) | data formatting | bytes 16777216 | tf_op jit(solution)/shard_map/reshape | solution.py:74
  110.0 1.1 dynamic-slice_bitcast_fusion
  111.2 3.0 %copy.21 = bf16[8,2,4,32,128,1]{3,0,2,1,5,4:T(8,128)(2,1)S(1)} copy(bf16[8,2,4,32,128,1]{4,3,2,1,0,5:T(8,128)(2,1)S(1)} %maximum_bitcast_fusion) | data formatting | bytes 1048576 | tf_op jit(solution)/shard_map/concatenate | solution.py:80
  114.2 6.9 %convolution_bitcast_fusion = bf16[128,32,4,128]{3,1,2,0:T(8,128)(2,1)} fusion(bf16[8,2,4,32,128,1]{3,0,2,1,5,4:T(8,128)(2,1)S(1)} %copy.21, bf16[4,8,2,4,128,128]{4,1,3,2,0,5:T(8,128)(2,1)} %copy.19), kind=kOutput, calls=%fused_computation.1 | convolution fusion | flops 268435456 | bytes 13107200 | tf_op jit(solution)/shard_map/trsak,ctrswk->kacw/dot_general | solution.py:81
  121.0 8.0 %copy.20 = bf16[128,32,4,128]{0,3,2,1:T(8,128)(2,1)} copy(bf16[128,32,4,128]{3,1,2,0:T(8,128)(2,1)} %convolution_bitcast_fusion) | data formatting | bytes 8388608 | tf_op jit(solution)/shard_map/trsak,ctrswk->kacw/dot_general | solution.py:81
  129.0 6.8 %bitcast_multiply_fusion = f32[16,512,256]{2,1,0:T(8,128)} fusion(bf16[128,2,16,512]{0,3,2,1:T(8,128)(2,1)} %bitcast.53, bf16[2,128,256,1]{2,1,3,0:T(8,128)(2,1)S(1)} %bitcast.59), kind=kOutput, calls=%fused_computation | convolution fusion | flops 1075838976 | bytes 12713984 | tf_op jit(solution)/shard_map/krij,rkl->ijl/dot_general | solution.py:84
  (14 shorter events, 0.2 us)
Async XLA Ops:
  6.5 88.9 %all-gather.2.cloned.1.call-start = ((), (), s32[]{:S(2)}) async-start(), calls=%async_computation | async-start | bytes 8650752 | tf_op jit(solution)/shard_map/all_gather | solution.py:73
  8.1 2.2 %copy-start = (f32[4,128,2048]{2,1,0:T(8,128)S(1)}, f32[4,128,2048]{2,1,0:T(8,128)}, u32[]{:S(2)}) copy-start(f32[4,128,2048]{2,1,0:T(8,128)} %param.1) | copy-start | bytes 12582916
Sparse Core Ops, SparseCore 0:
  15.3 80.0 all-gather.1

commit v7 on v6

--- a/solution.py
+++ b/solution.py
@@ -70,15 +70,21 @@
     imag_part = spectrum[:, freq_count:].reshape(seg_count, block_width, freq_count)
     real_w, imag_w = whiten(real_part, imag_part)
     local_spec = jnp.stack([real_w, imag_w], axis=0).astype(jnp.bfloat16)
+    local_spec = jnp.transpose(local_spec, (3, 0, 1, 2))
     every = lax.all_gather(local_spec, ("chan", "tm"), axis=0)
-    every = every.reshape(chan_count, time_count, 2, seg_count, block_width, freq_count)
+    every = every.reshape(chan_count, time_count, freq_count, 2, seg_count, block_width)
     chan_index = lax.axis_index("chan")
     tm_index = lax.axis_index("tm")
     own_block = lax.dynamic_index_in_dim(every, chan_index, 0, keepdims=False)
-    rows = lax.dynamic_slice_in_dim(own_block, tm_index * row_width, row_width, axis=3)
-    turned = jnp.stack([rows[:, 1], -rows[:, 0]], axis=1)
-    left = jnp.concatenate([rows, turned], axis=3)
-    cross = jnp.einsum("trsak,ctrswk->kacw", left, every, preferred_element_type=jnp.bfloat16)
+    row_ids = tm_index * row_width + jnp.arange(row_width, dtype=jnp.int32)
+    pick = (jnp.arange(block_width, dtype=jnp.int32)[:, None] == row_ids[None, :])
+    rows = jnp.einsum(
+        "tkrsw,wi->tkrsi", own_block, pick.astype(jnp.bfloat16),
+        preferred_element_type=jnp.float32,
+    ).astype(jnp.bfloat16)
+    turned = jnp.stack([rows[:, :, 1], -rows[:, :, 0]], axis=2)
+    left = jnp.concatenate([rows, turned], axis=4)
+    cross = jnp.einsum("tkrsa,ctkrsw->kacw", left, every, preferred_element_type=jnp.bfloat16)
     cross = cross.reshape(freq_count, 2, row_width, channel_total)
     table = lag_table(freq_count, sample_count, LAGS).reshape(2, freq_count, LAGS)
     pair_lags = jnp.einsum("krij,rkl->ijl", cross, table, preferred_element_type=jnp.float32)

time: 143 us -> 146 us (1.021)
  matrix products: 17.3 us -> 35.2 us
  local copies, waits for them, and re-layouts: 28.4 us -> 12.9 us
    dot_general x1 -> x2, matrix products: 6.86 us -> 24.8 us  [the longest x1 22.5 us: per_device(): jnp.einsum('tkrsa,ctkrsw->kacw', left, every, preferred_element_type=jnp....]
    reshape x1 -> x0, local copies, waits for them, and re-layouts: 14.5 us -> none  [per_device(): every.reshape(chan_count, time_count, 2, seg_count, block_width, freq_count)]
where the time goes in v7:
time: 146 us
  waiting for transfers between devices  80.1 us (55%)
  matrix products  35.2 us (24%)
  between operations  13.6 us (9%)
  local copies, waits for them, and re-layouts  12.9 us (9%)
  other arithmetic  3.73 us (3%)
    all_gather x1, waiting for transfers between devices, per_device(): every = lax.all_gather(local_spec, ('chan', 'tm'), axis=0)  80.1 us
    dot_general x1, matrix products, per_device(): jnp.einsum('tkrsa,ctkrsw->kacw', left, every, preferred_element_type=jnp....  22.5 us
    dot_general x1, local copies, waits for them, and re-layouts, per_device(): jnp.einsum('tkrsa,ctkrsw->kacw', left, every, preferred_element_type=jnp....  7.98 us
    dot_general x1, matrix products, per_device(): jnp.einsum('krij,rkl->ijl', cross, table, preferred_element_type=jnp.floa...  6.84 us
    dot_general x1, matrix products, per_device(): jnp.dot(raw_rows, folded, precision=lax.Precision.HIGH, preferred_element...  3.63 us
    concatenate x1, local copies, waits for them, and re-layouts, per_device(): left = jnp.concatenate([rows, turned], axis=4)  3.16 us
  transfers between devices with their start and end apart: 1, of which 1 were waited for; matrix products, arithmetic and copies ran while one was open for 0% of the time, Pallas kernels for 0%

profile of v7, /device:TPU:0, one launch (start us, length us, event | category | flops | bytes accessed | tf_op | source)
XLA Modules:
  0.0 145.5 jit_solution(5084599163333660362)
XLA Ops:
  6.5 0.0 all-gather.3.cloned.1.call-start
  6.6 0.3 fusion.36
  6.9 0.2 fusion.38
  7.1 0.1 add.268
  7.2 0.1 add.265
  7.2 0.1 add.266
  7.3 0.1 and.156
  7.4 0.1 mul.393
  7.5 0.6 multiply_subtract_fusion.1
  8.1 0.0 copy-start
  8.1 1.0 fusion.20
  9.1 1.2 copy-done
  10.3 3.6 %fusion.12 = f32[512,256]{0,1:T(8,128)S(1)} fusion(f32[512,2048]{1,0:T(8,128)S(1)} %bitcast.63, f32[2048,128]{1,0:T(8,128)S(1)} %get-tuple-element.19, f32[2048,128]{1,0:T(8,128)S(1)} %get-tuple-element.18), kind=kOutput, calls=%fused_computation.11 | convolution fusion | flops 1611137024 | bytes 6815744 | tf_op jit(solution)/shard_map/dot_general | solution.py:66
  13.9 0.1 add_reduce_fusion
  14.0 0.1 reshape.508
  14.1 0.1 reshape.509
  14.2 0.1 multiply_convert_fusion.1
  14.3 0.7 maximum_bitcast_fusion.1
  15.0 0.0 all-gather.3.cloned.1.call-update
  15.1 0.6 cosine_convert_fusion
  15.7 80.1 %all-gather.3.cloned.1.call-done = bf16[4096,2,4,128]{3,0,2,1:T(8,128)(2,1)} async-done(((bf16[128,2,4,128]{3,0,2,1:T(8,128)(2,1)}), bf16[4096,2,4,128]{3,0,2,1:T(8,128)(2,1)}) %all-gather.3.cloned.1.call-update) | async-done | bytes 8388624 | tf_op jit(solution)/shard_map/all_gather | solution.py:74
  95.8 2.3 %fusion.15 = bf16[8,128,2,4,16]{1,4,3,2,0:T(8,128)(2,1)S(1)} fusion(s32[16]{0:T(128)S(1)} %iota_add_fusion, bf16[4,8,128,2,4,128]{5,2,1,0,4,3:T(8,128)(2,1)} %bitcast.61, s32[]{:T(128)S(6)} %select_n.134), kind=kOutput, calls=%fused_computation.12 | convolution fusion | flops 33687552 | bytes 2359364 | tf_op jit(solution)/shard_map/tkrsw,wi->tkrsi/dot_general | solution.py:81
  98.2 3.2 %copy.16 = bf16[8,128,2,4,32,1]{4,0,3,2,5,1:T(8,128)(2,1)S(1)} copy(bf16[8,128,2,4,32,1]{1,4,3,2,0,5:T(8,128)(2,1)S(1)} %maximum_bitcast_fusion) | data formatting | bytes 1048576 | tf_op jit(solution)/shard_map/concatenate | solution.py:86
  101.4 22.5 %fusion.2 = bf16[128,32,4,128]{3,1,2,0:T(8,128)(2,1)} fusion(bf16[8,128,2,4,32,1]{4,0,3,2,5,1:T(8,128)(2,1)S(1)} %copy.16, bf16[4,8,128,2,4,128]{5,2,1,0,4,3:T(8,128)(2,1)} %bitcast.62), kind=kOutput, calls=%fused_computation.3 | convolution fusion | flops 268435456 | bytes 13107200 | tf_op jit(solution)/shard_map/tkrsa,ctkrsw->kacw/dot_general | solution.py:87
  123.9 8.0 %copy.13 = bf16[128,32,4,128]{0,3,2,1:T(8,128)(2,1)} copy(bf16[128,32,4,128]{3,1,2,0:T(8,128)(2,1)} %fusion.2) | data formatting | bytes 8388608 | tf_op jit(solution)/shard_map/tkrsa,ctkrsw->kacw/dot_general | solution.py:87
  131.8 6.8 %bitcast_multiply_fusion = f32[16,512,256]{2,1,0:T(8,128)} fusion(bf16[128,2,16,512]{0,3,2,1:T(8,128)(2,1)} %bitcast.60, bf16[2,128,256,1]{2,1,3,0:T(8,128)(2,1)S(1)} %bitcast.64), kind=kOutput, calls=%fused_computation | convolution fusion | flops 1075838976 | bytes 12713984 | tf_op jit(solution)/shard_map/krij,rkl->ijl/dot_general | solution.py:90
  (15 shorter events, 0.2 us)
Async XLA Ops:
  6.5 89.3 %all-gather.3.cloned.1.call-start = ((), (), s32[]{:S(2)}) async-start(), calls=%async_computation | async-start | bytes 8650752 | tf_op jit(solution)/shard_map/all_gather | solution.py:74
  8.1 2.2 %copy-start = (f32[4,128,2048]{2,1,0:T(8,128)S(1)}, f32[4,128,2048]{2,1,0:T(8,128)}, u32[]{:S(2)}) copy-start(f32[4,128,2048]{2,1,0:T(8,128)} %param.1) | copy-start | bytes 12582916
Sparse Core Ops, SparseCore 0:
  15.2 80.5 all-gather.2

commit v8 on v7

--- a/solution.py
+++ b/solution.py
@@ -70,21 +70,26 @@
     imag_part = spectrum[:, freq_count:].reshape(seg_count, block_width, freq_count)
     real_w, imag_w = whiten(real_part, imag_part)
     local_spec = jnp.stack([real_w, imag_w], axis=0).astype(jnp.bfloat16)
-    local_spec = jnp.transpose(local_spec, (3, 0, 1, 2))
+    local_spec = jnp.transpose(local_spec, (3, 0, 1, 2)).reshape(
+        freq_count, 2 * seg_count, block_width
+    )
     every = lax.all_gather(local_spec, ("chan", "tm"), axis=0)
-    every = every.reshape(chan_count, time_count, freq_count, 2, seg_count, block_width)
+    every = every.reshape(chan_count, time_count, freq_count, 2 * seg_count, block_width)
     chan_index = lax.axis_index("chan")
     tm_index = lax.axis_index("tm")
     own_block = lax.dynamic_index_in_dim(every, chan_index, 0, keepdims=False)
     row_ids = tm_index * row_width + jnp.arange(row_width, dtype=jnp.int32)
     pick = (jnp.arange(block_width, dtype=jnp.int32)[:, None] == row_ids[None, :])
     rows = jnp.einsum(
-        "tkrsw,wi->tkrsi", own_block, pick.astype(jnp.bfloat16),
+        "tkqw,wi->tkqi", own_block, pick.astype(jnp.bfloat16),
         preferred_element_type=jnp.float32,
     ).astype(jnp.bfloat16)
+    rows = rows.reshape(time_count, freq_count, 2, seg_count, row_width)
     turned = jnp.stack([rows[:, :, 1], -rows[:, :, 0]], axis=2)
-    left = jnp.concatenate([rows, turned], axis=4)
-    cross = jnp.einsum("tkrsa,ctkrsw->kacw", left, every, preferred_element_type=jnp.bfloat16)
+    left = jnp.concatenate([rows, turned], axis=4).reshape(
+        time_count, freq_count, 2 * seg_count, 2 * row_width
+    )
+    cross = jnp.einsum("tkqa,ctkqw->kacw", left, every, preferred_element_type=jnp.bfloat16)
     cross = cross.reshape(freq_count, 2, row_width, channel_total)
     table = lag_table(freq_count, sample_count, LAGS).reshape(2, freq_count, LAGS)
     pair_lags = jnp.einsum("krij,rkl->ijl", cross, table, preferred_element_type=jnp.float32)

time: 146 us -> 130 us (0.89)
  matrix products: 35.2 us -> 18.1 us
  local copies, waits for them, and re-layouts: 12.9 us -> 15.3 us
    dot_general x2, matrix products: 24.8 us -> 7.66 us  [the longest x1 6.98 us: per_device(): jnp.einsum('tkqa,ctkqw->kacw', left, every, preferred_element_type=jnp.bf...]
    dynamic_slice x0 -> x1, local copies, waits for them, and re-layouts: none -> 1.74 us  [per_device(): own_block = lax.dynamic_index_in_dim(every, chan_index, 0, keepdims=False)]
where the time goes in v8:
time: 130 us
  waiting for transfers between devices  79.6 us (61%)
  matrix products  18.1 us (14%)
  local copies, waits for them, and re-layouts  15.3 us (12%)
  between operations  13.6 us (10%)
  other arithmetic  3.06 us (2%)
    all_gather x1, waiting for transfers between devices, per_device(): every = lax.all_gather(local_spec, ('chan', 'tm'), axis=0)  79.6 us
    dot_general x1, local copies, waits for them, and re-layouts, per_device(): jnp.einsum('tkqa,ctkqw->kacw', left, every, preferred_element_type=jnp.bf...  7.98 us
    dot_general x1, matrix products, per_device(): jnp.einsum('tkqa,ctkqw->kacw', left, every, preferred_element_type=jnp.bf...  6.98 us
    dot_general x1, matrix products, per_device(): jnp.einsum('krij,rkl->ijl', cross, table, preferred_element_type=jnp.floa...  6.84 us
    dot_general x1, matrix products, per_device(): jnp.dot(raw_rows, folded, precision=lax.Precision.HIGH, preferred_element...  3.62 us
    concatenate x1, local copies, waits for them, and re-layouts, per_device(): jnp.concatenate([rows, turned], axis=4)  2.98 us
  transfers between devices with their start and end apart: 1, of which 1 were waited for; matrix products, arithmetic and copies ran while one was open for 0% of the time, Pallas kernels for 0%

profile of v8, /device:TPU:0, one launch (start us, length us, event | category | flops | bytes accessed | tf_op | source)
XLA Modules:
  0.0 129.7 jit_solution(891758453147667318)
XLA Ops:
  6.5 0.0 all-gather.2.cloned.1.call-start
  6.6 0.3 fusion.36
  6.9 0.2 fusion.38
  7.1 0.1 add.268
  7.2 0.1 add.265
  7.2 0.1 add.266
  7.3 0.1 and.156
  7.4 0.1 mul.393
  7.5 0.6 multiply_subtract_fusion.1
  8.1 0.0 copy-start
  8.1 1.0 fusion.20
  9.1 1.2 copy-done
  10.3 3.6 %fusion.12 = f32[512,256]{0,1:T(8,128)S(1)} fusion(f32[512,2048]{1,0:T(8,128)S(1)} %bitcast.65, f32[2048,128]{1,0:T(8,128)S(1)} %get-tuple-element.19, f32[2048,128]{1,0:T(8,128)S(1)} %get-tuple-element.18), kind=kOutput, calls=%fused_computation.11 | convolution fusion | flops 1611137024 | bytes 6815744 | tf_op jit(solution)/shard_map/dot_general | solution.py:66
  13.9 0.1 add_reduce_fusion
  14.0 0.1 reshape.515
  14.1 0.1 reshape.516
  14.2 0.1 multiply_convert_fusion.1
  14.4 0.9 copy.22
  15.2 0.0 all-gather.2.cloned.1.call-update
  15.3 0.6 cosine_convert_fusion
  15.9 79.6 %all-gather.2.cloned.1.call-done = bf16[32,128,8,128]{3,2,1,0:T(8,128)(2,1)} async-done(((bf16[1,128,8,128]{3,2,1,0:T(8,128)(2,1)}), bf16[32,128,8,128]{3,2,1,0:T(8,128)(2,1)}) %all-gather.2.cloned.1.call-update) | async-done | bytes 8388624 | tf_op jit(solution)/shard_map/all_gather | solution.py:76
  95.5 1.7 %constant_dynamic-slice_fusion = bf16[1,8,128,8,128]{4,3,2,1,0:T(8,128)(2,1)S(1)} fusion(bf16[4,8,128,8,128]{4,3,2,1,0:T(8,128)(2,1)} %bitcast.63, s32[]{:T(128)S(6)} %select_n.134), kind=kLoop, calls=%fused_computation.96 | loop fusion | bytes 4194308 | tf_op jit(solution)/shard_map/jit(dynamic_index_in_dim)/dynamic_slice | solution.py:80
  97.3 0.7 fusion.15
  98.1 3.0 %copy.28 = bf16[8,128,8,32,1]{3,2,0,4,1:T(8,128)(2,1)S(1)} copy(bf16[8,128,8,32,1]{1,3,2,0,4:T(8,128)(2,1)S(1)} %maximum_bitcast_fusion) | data formatting | bytes 1048576 | tf_op jit(solution)/shard_map/concatenate | solution.py:89
  101.1 7.0 %fusion.2 = bf16[128,32,4,128]{3,1,2,0:T(8,128)(2,1)} fusion(bf16[8,128,8,32,1]{3,2,0,4,1:T(8,128)(2,1)S(1)} %copy.28, bf16[4,8,128,8,128]{4,3,2,1,0:T(8,128)(2,1)} %bitcast.64), kind=kOutput, calls=%fused_computation.3 | convolution fusion | flops 268435456 | bytes 13107200 | tf_op jit(solution)/shard_map/tkqa,ctkqw->kacw/dot_general | solution.py:92
  108.0 8.0 %copy.26 = bf16[128,32,4,128]{0,3,2,1:T(8,128)(2,1)} copy(bf16[128,32,4,128]{3,1,2,0:T(8,128)(2,1)} %fusion.2) | data formatting | bytes 8388608 | tf_op jit(solution)/shard_map/tkqa,ctkqw->kacw/dot_general | solution.py:92
  116.0 6.8 %bitcast_multiply_fusion = f32[16,512,256]{2,1,0:T(8,128)} fusion(bf16[128,2,16,512]{0,3,2,1:T(8,128)(2,1)} %bitcast.62, bf16[2,128,256,1]{2,1,3,0:T(8,128)(2,1)S(1)} %bitcast.69), kind=kOutput, calls=%fused_computation | convolution fusion | flops 1075838976 | bytes 12713984 | tf_op jit(solution)/shard_map/krij,rkl->ijl/dot_general | solution.py:95
  (17 shorter events, 0.2 us)
Async XLA Ops:
  6.5 89.0 %all-gather.2.cloned.1.call-start = ((), (), s32[]{:S(2)}) async-start(), calls=%async_computation | async-start | bytes 8650752 | tf_op jit(solution)/shard_map/all_gather | solution.py:76
  8.1 2.2 %copy-start = (f32[4,128,2048]{2,1,0:T(8,128)S(1)}, f32[4,128,2048]{2,1,0:T(8,128)}, u32[]{:S(2)}) copy-start(f32[4,128,2048]{2,1,0:T(8,128)} %param.1) | copy-start | bytes 12582916
Sparse Core Ops, SparseCore 0:
  15.4 80.0 all-gather.1

commit v9 on v8

--- a/solution.py
+++ b/solution.py
@@ -89,12 +89,12 @@
     left = jnp.concatenate([rows, turned], axis=4).reshape(
         time_count, freq_count, 2 * seg_count, 2 * row_width
     )
-    cross = jnp.einsum("tkqa,ctkqw->kacw", left, every, preferred_element_type=jnp.bfloat16)
+    norm_scale = 1.0 / math.sqrt(freq_count * seg_count * time_count)
+    cross = jnp.einsum("tkqa,ctkqw->kacw", left, every, preferred_element_type=jnp.float32)
+    cross = (cross * norm_scale).astype(jnp.bfloat16)
     cross = cross.reshape(freq_count, 2, row_width, channel_total)
     table = lag_table(freq_count, sample_count, LAGS).reshape(2, freq_count, LAGS)
-    pair_lags = jnp.einsum("krij,rkl->ijl", cross, table, preferred_element_type=jnp.float32)
-    norm_scale = 1.0 / math.sqrt(freq_count * seg_count * time_count)
-    return pair_lags * norm_scale
+    return jnp.einsum("krij,rkl->ijl", cross, table, preferred_element_type=jnp.float32)
 
 
 def solution(mesh):

time: 130 us -> 130 us (level)
    convert_element_type x0 -> x1, local copies, waits for them, and re-layouts: none -> 7.98 us  [per_device(): cross = (cross * norm_scale).astype(jnp.bfloat16)]
    dot_general x1 -> x0, local copies, waits for them, and re-layouts: 7.98 us -> none  [per_device(): jnp.einsum('tkqa,ctkqw->kacw', left, every, preferred_element_type=jnp.bf...]
where the time goes in v9:
time: 130 us
  waiting for transfers between devices  79.6 us (61%)
  matrix products  18.2 us (14%)
  local copies, waits for them, and re-layouts  15.3 us (12%)
  between operations  13.6 us (10%)
  other arithmetic  3.06 us (2%)
    all_gather x1, waiting for transfers between devices, per_device(): every = lax.all_gather(local_spec, ('chan', 'tm'), axis=0)  79.6 us
    convert_element_type x1, local copies, waits for them, and re-layouts, per_device(): cross = (cross * norm_scale).astype(jnp.bfloat16)  7.98 us
    dot_general x1, matrix products, per_device(): jnp.einsum('tkqa,ctkqw->kacw', left, every, preferred_element_type=jnp.fl...  7.08 us
    dot_general x1, matrix products, per_device(): jnp.einsum('krij,rkl->ijl', cross, table, preferred_element_type=jnp.floa...  6.83 us
    dot_general x1, matrix products, per_device(): jnp.dot(raw_rows, folded, precision=lax.Precision.HIGH, preferred_element...  3.62 us
    concatenate x1, local copies, waits for them, and re-layouts, per_device(): jnp.concatenate([rows, turned], axis=4)  2.98 us
  transfers between devices with their start and end apart: 1, of which 1 were waited for; matrix products, arithmetic and copies ran while one was open for 0% of the time, Pallas kernels for 0%

profile of v9, /device:TPU:0, one launch (start us, length us, event | category | flops | bytes accessed | tf_op | source)
XLA Modules:
  0.0 129.8 jit_solution(16172181624009519098)
XLA Ops:
  6.5 0.0 all-gather.2.cloned.1.call-start
  6.6 0.3 fusion.36
  6.9 0.2 fusion.38
  7.1 0.1 add.268
  7.2 0.1 add.265
  7.2 0.1 add.266
  7.3 0.1 and.156
  7.4 0.1 mul.393
  7.5 0.6 multiply_subtract_fusion.1
  8.1 0.0 copy-start
  8.1 1.0 fusion.20
  9.1 1.2 copy-done
  10.3 3.6 %fusion.12 = f32[512,256]{0,1:T(8,128)S(1)} fusion(f32[512,2048]{1,0:T(8,128)S(1)} %bitcast.67, f32[2048,128]{1,0:T(8,128)S(1)} %get-tuple-element.19, f32[2048,128]{1,0:T(8,128)S(1)} %get-tuple-element.18), kind=kOutput, calls=%fused_computation.12 | convolution fusion | flops 1611137024 | bytes 6815744 | tf_op jit(solution)/shard_map/dot_general | solution.py:66
  13.9 0.1 add_reduce_fusion
  14.0 0.1 reshape.515
  14.1 0.1 reshape.516
  14.2 0.1 multiply_convert_fusion.1
  14.4 0.9 copy.22
  15.2 0.0 all-gather.2.cloned.1.call-update
  15.3 0.6 cosine_convert_fusion
  15.9 79.6 %all-gather.2.cloned.1.call-done = bf16[32,128,8,128]{3,2,1,0:T(8,128)(2,1)} async-done(((bf16[1,128,8,128]{3,2,1,0:T(8,128)(2,1)}), bf16[32,128,8,128]{3,2,1,0:T(8,128)(2,1)}) %all-gather.2.cloned.1.call-update) | async-done | bytes 8388624 | tf_op jit(solution)/shard_map/all_gather | solution.py:76
  95.5 1.7 %constant_dynamic-slice_fusion = bf16[1,8,128,8,128]{4,3,2,1,0:T(8,128)(2,1)S(1)} fusion(bf16[4,8,128,8,128]{4,3,2,1,0:T(8,128)(2,1)} %bitcast.65, s32[]{:T(128)S(6)} %select_n.134), kind=kLoop, calls=%fused_computation.97 | loop fusion | bytes 4194308 | tf_op jit(solution)/shard_map/jit(dynamic_index_in_dim)/dynamic_slice | solution.py:80
  97.3 0.7 fusion.15
  98.1 3.0 %copy.28 = bf16[8,128,8,32,1]{3,2,0,4,1:T(8,128)(2,1)S(1)} copy(bf16[8,128,8,32,1]{1,3,2,0,4:T(8,128)(2,1)S(1)} %maximum_bitcast_fusion) | data formatting | bytes 1048576 | tf_op jit(solution)/shard_map/concatenate | solution.py:89
  101.1 7.1 %fusion = bf16[128,32,4,128]{3,1,2,0:T(8,128)(2,1)} fusion(bf16[8,128,8,32,1]{3,2,0,4,1:T(8,128)(2,1)S(1)} %copy.28, bf16[4,8,128,8,128]{4,3,2,1,0:T(8,128)(2,1)} %bitcast.66), kind=kOutput, calls=%fused_computation.1 | convolution fusion | flops 272629760 | bytes 13107200 | tf_op jit(solution)/shard_map/tkqa,ctkqw->kacw/dot_general | solution.py:93
  108.1 8.0 %copy.26 = bf16[128,32,4,128]{0,3,2,1:T(8,128)(2,1)} copy(bf16[128,32,4,128]{3,1,2,0:T(8,128)(2,1)} %fusion) | data formatting | bytes 8388608 | tf_op jit(solution)/shard_map/convert_element_type | solution.py:94
  116.1 6.8 %convolution_bitcast_fusion = f32[16,512,256]{2,1,0:T(8,128)} fusion(bf16[128,2,16,512]{0,3,2,1:T(8,128)(2,1)} %bitcast.64, bf16[2,128,256,1]{2,1,3,0:T(8,128)(2,1)S(1)} %bitcast.71), kind=kOutput, calls=%fused_computation.4 | convolution fusion | flops 1073741824 | bytes 12713984 | tf_op jit(solution)/shard_map/krij,rkl->ijl/dot_general | solution.py:97
  (17 shorter events, 0.2 us)
Async XLA Ops:
  6.5 89.0 %all-gather.2.cloned.1.call-start = ((), (), s32[]{:S(2)}) async-start(), calls=%async_computation | async-start | bytes 8650752 | tf_op jit(solution)/shard_map/all_gather | solution.py:76
  8.1 2.2 %copy-start = (f32[4,128,2048]{2,1,0:T(8,128)S(1)}, f32[4,128,2048]{2,1,0:T(8,128)}, u32[]{:S(2)}) copy-start(f32[4,128,2048]{2,1,0:T(8,128)} %param.1) | copy-start | bytes 12582916
Sparse Core Ops, SparseCore 0:
  15.4 80.0 all-gather.1

commit v10 on v9

--- a/solution.py
+++ b/solution.py
@@ -3,6 +3,7 @@
 import jax
 import jax.numpy as jnp
 from jax import lax
+from jax.experimental import pallas as pl
 from jax.sharding import PartitionSpec as P
 
 LAGS = 256
@@ -53,6 +54,35 @@
     return both.reshape(2 * sample_count, 2 * freq_count)
 
 
+def lag_kernel(cross_ref, table_ref, out_ref):
+    row_width = out_ref.shape[0]
+    table = table_ref[...]
+    for row in range(row_width):
+        real_rows = cross_ref[:, row, :].astype(jnp.float32)
+        imag_rows = cross_ref[:, row_width + row, :].astype(jnp.float32)
+        both = jnp.concatenate([real_rows, imag_rows], axis=0)
+        out_ref[row] = jnp.dot(
+            both.T.astype(jnp.bfloat16), table, preferred_element_type=jnp.float32
+        )
+
+
+def lag_transform(cross, table, interpret=False):
+    freq_count, chan_count, pair_rows, block_width = cross.shape
+    row_width = pair_rows // 2
+    lag_count = table.shape[1]
+    return pl.pallas_call(
+        lag_kernel,
+        grid=(chan_count,),
+        in_specs=[
+            pl.BlockSpec((freq_count, None, pair_rows, block_width), lambda c: (0, c, 0, 0)),
+            pl.BlockSpec((2 * freq_count, lag_count), lambda c: (0, 0)),
+        ],
+        out_specs=pl.BlockSpec((row_width, block_width, lag_count), lambda c: (0, c, 0)),
+        out_shape=jax.ShapeDtypeStruct((row_width, chan_count * block_width, lag_count), jnp.float32),
+        interpret=interpret,
+    )(cross, table)
+
+
 def per_device(raw_samples):
     seg_count, block_width, raw_length = raw_samples.shape
     sample_count = raw_length // 2
@@ -90,11 +120,10 @@
         time_count, freq_count, 2 * seg_count, 2 * row_width
     )
     norm_scale = 1.0 / math.sqrt(freq_count * seg_count * time_count)
-    cross = jnp.einsum("tkqa,ctkqw->kacw", left, every, preferred_element_type=jnp.float32)
+    cross = jnp.einsum("tkqa,ctkqw->kcaw", left, every, preferred_element_type=jnp.float32)
     cross = (cross * norm_scale).astype(jnp.bfloat16)
-    cross = cross.reshape(freq_count, 2, row_width, channel_total)
-    table = lag_table(freq_count, sample_count, LAGS).reshape(2, freq_count, LAGS)
-    return jnp.einsum("krij,rkl->ijl", cross, table, preferred_element_type=jnp.float32)
+    table = lag_table(freq_count, sample_count, LAGS)
+    return lag_transform(cross, table)
 
 
 def solution(mesh):

time: 130 us -> 125 us (0.962)
  Pallas kernels: 0 us -> 9.26 us
  local copies, waits for them, and re-layouts: 15.3 us -> 7.36 us
  matrix products: 18.2 us -> 11.3 us
    pallas_call x0 -> x1, Pallas kernels: none -> 9.26 us  [lag_transform(): pl.pallas_call(lag_kernel, grid=(chan_count,), in_specs=[pl.BlockSpec((fr...]
    convert_element_type x1 -> x0, local copies, waits for them, and re-layouts: 7.98 us -> none  [per_device(): cross = (cross * norm_scale).astype(jnp.bfloat16)]
    dot_general x2 -> x1, matrix products: 13.9 us -> 7.03 us  [per_device(): jnp.einsum('tkqa,ctkqw->kcaw', left, every, preferred_element_type=jnp.fl...]
  transfers between devices with their start and end apart: 1 -> 1, of which waited for: 1 -> 1; matrix products, arithmetic and copies ran while one was open for 0% -> 1% of each run, Pallas kernels for 0% -> 0%
where the time goes in v10:
time: 125 us; the launch traced here: 124 us
  waiting for transfers between devices  79 us (63%)
  between operations  13.6 us (11%)
  matrix products  11.3 us (9%)
  Pallas kernels  9.26 us (7%)
  local copies, waits for them, and re-layouts  7.36 us (6%)
  other arithmetic  3.7 us (3%)
    all_gather x1, waiting for transfers between devices, per_device(): every = lax.all_gather(local_spec, ('chan', 'tm'), axis=0)  79 us
    pallas_call x1, Pallas kernels, lag_transform(): pl.pallas_call(lag_kernel, grid=(chan_count,), in_specs=[pl.BlockSpec((fr...  9.26 us
    dot_general x1, matrix products, per_device(): jnp.einsum('tkqa,ctkqw->kcaw', left, every, preferred_element_type=jnp.fl...  7.03 us
    dot_general x1, matrix products, per_device(): jnp.dot(raw_rows, folded, precision=lax.Precision.HIGH, preferred_element...  3.62 us
    concatenate x1, local copies, waits for them, and re-layouts, per_device(): jnp.concatenate([rows, turned], axis=4)  2.98 us
  transfers between devices with their start and end apart: 1, of which 1 were waited for; matrix products, arithmetic and copies ran while one was open for 1% of the time, Pallas kernels for 0%

profile of v10, /device:TPU:0, one launch (start us, length us, event | category | flops | bytes accessed | tf_op | source)
XLA Modules:
  0.0 124.2 jit_solution(1038324283957887318)
XLA Ops:
  6.5 0.0 all-gather.2.cloned.1.call-start
  6.6 0.3 fusion.37
  6.9 0.2 fusion.39
  7.1 0.1 add.268
  7.2 0.1 add.265
  7.2 0.1 add.266
  7.3 0.1 and.156
  7.4 0.1 mul.394
  7.5 0.6 multiply_subtract_fusion.1
  8.1 0.0 copy-start
  8.1 1.0 fusion.21
  9.1 1.2 copy-done
  10.3 3.6 %fusion.13 = f32[512,256]{0,1:T(8,128)S(1)} fusion(f32[512,2048]{1,0:T(8,128)S(1)} %bitcast.58, f32[2048,128]{1,0:T(8,128)S(1)} %get-tuple-element.19, f32[2048,128]{1,0:T(8,128)S(1)} %get-tuple-element.18), kind=kOutput, calls=%fused_computation.12 | convolution fusion | flops 1611137024 | bytes 6815744 | tf_op jit(solution)/shard_map/dot_general | solution.py:96
  13.9 0.1 add_reduce_fusion
  14.0 0.1 reshape.509
  14.1 0.1 reshape.510
  14.2 0.1 multiply_convert_fusion.1
  14.4 0.9 copy.20
  15.2 0.0 all-gather.2.cloned.1.call-update
  15.3 0.6 cosine_convert_fusion
  15.9 0.7 pad_maximum_fusion.2.table_ref
  16.5 79.0 %all-gather.2.cloned.1.call-done = bf16[32,128,8,128]{3,2,1,0:T(8,128)(2,1)} async-done(((bf16[1,128,8,128]{3,2,1,0:T(8,128)(2,1)}), bf16[32,128,8,128]{3,2,1,0:T(8,128)(2,1)}) %all-gather.2.cloned.1.call-update) | async-done | bytes 8388624 | tf_op jit(solution)/shard_map/all_gather | solution.py:106
  95.5 1.7 %constant_dynamic-slice_fusion = bf16[1,8,128,8,128]{4,3,2,1,0:T(8,128)(2,1)S(1)} fusion(bf16[4,8,128,8,128]{4,3,2,1,0:T(8,128)(2,1)} %bitcast.62, s32[]{:T(128)S(6)} %select_n.134), kind=kLoop, calls=%fused_computation.97 | loop fusion | bytes 4194308 | tf_op jit(solution)/shard_map/jit(dynamic_index_in_dim)/dynamic_slice | solution.py:110
  97.3 0.7 fusion.16
  98.1 3.0 %copy.25 = bf16[8,128,8,32,1]{3,2,0,4,1:T(8,128)(2,1)S(1)} copy(bf16[8,128,8,32,1]{1,3,2,0,4:T(8,128)(2,1)S(1)} %maximum_bitcast_fusion) | data formatting | bytes 1048576 | tf_op jit(solution)/shard_map/concatenate | solution.py:119
  101.1 7.0 %fusion.3.cross_ref = bf16[128,4,32,128]{3,2,1,0:T(8,128)(2,1)} fusion(bf16[8,128,8,32,1]{3,2,0,4,1:T(8,128)(2,1)S(1)} %copy.25, bf16[4,8,128,8,128]{4,3,2,1,0:T(8,128)(2,1)} %bitcast.63), kind=kOutput, calls=%fused_computation.4 | convolution fusion | flops 272629760 | bytes 13107200 | tf_op jit(solution)/shard_map/tkqa,ctkqw->kcaw/dot_general | solution.py:123
  108.1 9.3 %shard_map.17 = f32[16,512,256]{2,1,0:T(8,128)} custom-call(bf16[128,4,32,128]{3,2,1,0:T(8,128)(2,1)} %fusion.3.cross_ref, bf16[256,256]{1,0:T(8,128)(2,1)} %pad_maximum_fusion.2.table_ref), custom_call_target="tpu_custom_call" | custom-call | tf_op jit(solution)/shard_map/pallas_call | solution.py:73
  (16 shorter events, 0.2 us)
Async XLA Ops:
  6.5 89.0 %all-gather.2.cloned.1.call-start = ((), (), s32[]{:S(2)}) async-start(), calls=%async_computation | async-start | bytes 8650752 | tf_op jit(solution)/shard_map/all_gather | solution.py:106
  8.1 2.2 %copy-start = (f32[4,128,2048]{2,1,0:T(8,128)S(1)}, f32[4,128,2048]{2,1,0:T(8,128)}, u32[]{:S(2)}) copy-start(f32[4,128,2048]{2,1,0:T(8,128)} %param.1) | copy-start | bytes 12582916
Sparse Core Ops, SparseCore 0:
  15.4 80.0 all-gather.1

commit v11 on v10

--- a/solution.py
+++ b/solution.py
@@ -55,11 +55,10 @@
 
 
 def lag_kernel(cross_ref, table_ref, out_ref):
-    row_width = out_ref.shape[0]
     table = table_ref[...]
-    for row in range(row_width):
-        real_rows = cross_ref[:, row, :].astype(jnp.float32)
-        imag_rows = cross_ref[:, row_width + row, :].astype(jnp.float32)
+    for row in range(out_ref.shape[0]):
+        real_rows = cross_ref[:, 0, row, :].astype(jnp.float32)
+        imag_rows = cross_ref[:, 1, row, :].astype(jnp.float32)
         both = jnp.concatenate([real_rows, imag_rows], axis=0)
         out_ref[row] = jnp.dot(
             both.T.astype(jnp.bfloat16), table, preferred_element_type=jnp.float32
@@ -69,15 +68,19 @@
 def lag_transform(cross, table, interpret=False):
     freq_count, chan_count, pair_rows, block_width = cross.shape
     row_width = pair_rows // 2
+    step_rows = 8 if row_width % 8 == 0 else row_width
     lag_count = table.shape[1]
+    cross = cross.reshape(freq_count, chan_count, 2, row_width, block_width)
     return pl.pallas_call(
         lag_kernel,
-        grid=(chan_count,),
+        grid=(chan_count, row_width // step_rows),
         in_specs=[
-            pl.BlockSpec((freq_count, None, pair_rows, block_width), lambda c: (0, c, 0, 0)),
-            pl.BlockSpec((2 * freq_count, lag_count), lambda c: (0, 0)),
+            pl.BlockSpec(
+                (freq_count, None, 2, step_rows, block_width), lambda c, h: (0, c, 0, h, 0)
+            ),
+            pl.BlockSpec((2 * freq_count, lag_count), lambda c, h: (0, 0)),
         ],
-        out_specs=pl.BlockSpec((row_width, block_width, lag_count), lambda c: (0, c, 0)),
+        out_specs=pl.BlockSpec((step_rows, block_width, lag_count), lambda c, h: (h, c, 0)),
         out_shape=jax.ShapeDtypeStruct((row_width, chan_count * block_width, lag_count), jnp.float32),
         interpret=interpret,
     )(cross, table)

time: 125 us -> 126 us (level)
  Pallas kernels: 9.26 us -> 10.8 us
    pallas_call x1, Pallas kernels: 9.26 us -> 10.8 us  [lag_transform(): pl.pallas_call(lag_kernel, grid=(chan_count, row_width // step_rows), in_...]
where the time goes in v11:
time: 126 us
  waiting for transfers between devices  79 us (63%)
  between operations  13.6 us (11%)
  matrix products  11.3 us (9%)
  Pallas kernels  10.8 us (9%)
  local copies, waits for them, and re-layouts  7.36 us (6%)
  other arithmetic  3.7 us (3%)
    all_gather x1, waiting for transfers between devices, per_device(): every = lax.all_gather(local_spec, ('chan', 'tm'), axis=0)  79 us
    pallas_call x1, Pallas kernels, lag_transform(): pl.pallas_call(lag_kernel, grid=(chan_count, row_width // step_rows), in_...  10.8 us
    dot_general x1, matrix products, per_device(): jnp.einsum('tkqa,ctkqw->kcaw', left, every, preferred_element_type=jnp.fl...  7.03 us
    dot_general x1, matrix products, per_device(): jnp.dot(raw_rows, folded, precision=lax.Precision.HIGH, preferred_element...  3.62 us
    concatenate x1, local copies, waits for them, and re-layouts, per_device(): jnp.concatenate([rows, turned], axis=4)  2.98 us
  transfers between devices with their start and end apart: 1, of which 1 were waited for; matrix products, arithmetic and copies ran while one was open for 1% of the time, Pallas kernels for 0%

profile of v11, /device:TPU:0, one launch (start us, length us, event | category | flops | bytes accessed | tf_op | source)
XLA Modules:
  0.0 125.8 jit_solution(3984790142027138854)
XLA Ops:
  6.5 0.0 all-gather.2.cloned.1.call-start
  6.6 0.3 fusion.36
  6.9 0.2 fusion.38
  7.1 0.1 add.268
  7.2 0.1 add.265
  7.2 0.1 add.266
  7.3 0.1 and.156
  7.4 0.1 mul.394
  7.5 0.6 multiply_subtract_fusion.1
  8.1 0.0 copy-start
  8.1 1.0 fusion.20
  9.1 1.2 copy-done
  10.3 3.6 %fusion.12 = f32[512,256]{0,1:T(8,128)S(1)} fusion(f32[512,2048]{1,0:T(8,128)S(1)} %bitcast.58, f32[2048,128]{1,0:T(8,128)S(1)} %get-tuple-element.19, f32[2048,128]{1,0:T(8,128)S(1)} %get-tuple-element.18), kind=kOutput, calls=%fused_computation.11 | convolution fusion | flops 1611137024 | bytes 6815744 | tf_op jit(solution)/shard_map/dot_general | solution.py:99
  13.9 0.1 add_reduce_fusion
  14.0 0.1 reshape.512
  14.1 0.1 reshape.513
  14.2 0.1 multiply_convert_fusion.1
  14.4 0.9 copy.20
  15.2 0.0 all-gather.2.cloned.1.call-update
  15.3 0.6 cosine_convert_fusion
  15.9 0.7 pad_maximum_fusion.2.table_ref
  16.5 79.0 %all-gather.2.cloned.1.call-done = bf16[32,128,8,128]{3,2,1,0:T(8,128)(2,1)} async-done(((bf16[1,128,8,128]{3,2,1,0:T(8,128)(2,1)}), bf16[32,128,8,128]{3,2,1,0:T(8,128)(2,1)}) %all-gather.2.cloned.1.call-update) | async-done | bytes 8388624 | tf_op jit(solution)/shard_map/all_gather | solution.py:109
  95.5 1.7 %constant_dynamic-slice_fusion = bf16[1,8,128,8,128]{4,3,2,1,0:T(8,128)(2,1)S(1)} fusion(bf16[4,8,128,8,128]{4,3,2,1,0:T(8,128)(2,1)} %bitcast.62, s32[]{:T(128)S(6)} %select_n.134), kind=kLoop, calls=%fused_computation.96 | loop fusion | bytes 4194308 | tf_op jit(solution)/shard_map/jit(dynamic_index_in_dim)/dynamic_slice | solution.py:113
  97.3 0.7 fusion.15
  98.1 3.0 %copy.25 = bf16[8,128,8,32,1]{3,2,0,4,1:T(8,128)(2,1)S(1)} copy(bf16[8,128,8,32,1]{1,3,2,0,4:T(8,128)(2,1)S(1)} %maximum_bitcast_fusion) | data formatting | bytes 1048576 | tf_op jit(solution)/shard_map/concatenate | solution.py:122
  101.1 7.0 %fusion = bf16[128,4,128,32]{2,3,1,0:T(8,128)(2,1)} fusion(bf16[8,128,8,32,1]{3,2,0,4,1:T(8,128)(2,1)S(1)} %copy.25, bf16[4,8,128,8,128]{4,3,2,1,0:T(8,128)(2,1)} %bitcast.63), kind=kOutput, calls=%fused_computation.1 | convolution fusion | flops 272629760 | bytes 13107200 | tf_op jit(solution)/shard_map/tkqa,ctkqw->kcaw/dot_general | solution.py:126
  108.1 10.8 %shard_map.17 = f32[16,512,256]{2,1,0:T(8,128)} custom-call(bf16[128,4,2,16,128]{4,3,2,1,0:T(8,128)(2,1)} %bitcast.57, bf16[256,256]{1,0:T(8,128)(2,1)} %pad_maximum_fusion.2.table_ref), custom_call_target="tpu_custom_call" | custom-call | tf_op jit(solution)/shard_map/pallas_call | solution.py:74
  (16 shorter events, 0.2 us)
Async XLA Ops:
  6.5 89.0 %all-gather.2.cloned.1.call-start = ((), (), s32[]{:S(2)}) async-start(), calls=%async_computation | async-start | bytes 8650752 | tf_op jit(solution)/shard_map/all_gather | solution.py:109
  8.1 2.2 %copy-start = (f32[4,128,2048]{2,1,0:T(8,128)S(1)}, f32[4,128,2048]{2,1,0:T(8,128)}, u32[]{:S(2)}) copy-start(f32[4,128,2048]{2,1,0:T(8,128)} %param.1) | copy-start | bytes 12582916
Sparse Core Ops, SparseCore 0:
  15.4 80.0 all-gather.1

commit v12 on v10

--- a/solution.py
+++ b/solution.py
@@ -58,11 +58,11 @@
     row_width = out_ref.shape[0]
     table = table_ref[...]
     for row in range(row_width):
-        real_rows = cross_ref[:, row, :].astype(jnp.float32)
-        imag_rows = cross_ref[:, row_width + row, :].astype(jnp.float32)
+        real_rows = cross_ref[:, row, :]
+        imag_rows = cross_ref[:, row_width + row, :]
         both = jnp.concatenate([real_rows, imag_rows], axis=0)
-        out_ref[row] = jnp.dot(
-            both.T.astype(jnp.bfloat16), table, preferred_element_type=jnp.float32
+        out_ref[row] = lax.dot_general(
+            both, table, (((0,), (0,)), ((), ())), preferred_element_type=jnp.float32
         )
 
 

time: 125 us -> 124 us (level)
  no operation moved by 1% of the time
where the time goes in v12:
time: 124 us
  waiting for transfers between devices  79 us (64%)
  between operations  13.6 us (11%)
  matrix products  11.3 us (9%)
  Pallas kernels  9.19 us (7%)
  local copies, waits for them, and re-layouts  7.36 us (6%)
  other arithmetic  3.7 us (3%)
    all_gather x1, waiting for transfers between devices, per_device(): every = lax.all_gather(local_spec, ('chan', 'tm'), axis=0)  79 us
    pallas_call x1, Pallas kernels, lag_transform(): pl.pallas_call(lag_kernel, grid=(chan_count,), in_specs=[pl.BlockSpec((fr...  9.19 us
    dot_general x1, matrix products, per_device(): jnp.einsum('tkqa,ctkqw->kcaw', left, every, preferred_element_type=jnp.fl...  7.03 us
    dot_general x1, matrix products, per_device(): jnp.dot(raw_rows, folded, precision=lax.Precision.HIGH, preferred_element...  3.62 us
    concatenate x1, local copies, waits for them, and re-layouts, per_device(): jnp.concatenate([rows, turned], axis=4)  2.98 us
  transfers between devices with their start and end apart: 1, of which 1 were waited for; matrix products, arithmetic and copies ran while one was open for 1% of the time, Pallas kernels for 0%

profile of v12, /device:TPU:0, one launch (start us, length us, event | category | flops | bytes accessed | tf_op | source)
XLA Modules:
  0.0 124.1 jit_solution(7687231576638342504)
XLA Ops:
  6.5 0.0 all-gather.2.cloned.1.call-start
  6.6 0.3 fusion.37
  6.9 0.2 fusion.39
  7.1 0.1 add.268
  7.2 0.1 add.265
  7.2 0.1 add.266
  7.3 0.1 and.156
  7.4 0.1 mul.394
  7.5 0.6 multiply_subtract_fusion.1
  8.1 0.0 copy-start
  8.1 1.0 fusion.21
  9.1 1.2 copy-done
  10.3 3.6 %fusion.13 = f32[512,256]{0,1:T(8,128)S(1)} fusion(f32[512,2048]{1,0:T(8,128)S(1)} %bitcast.58, f32[2048,128]{1,0:T(8,128)S(1)} %get-tuple-element.19, f32[2048,128]{1,0:T(8,128)S(1)} %get-tuple-element.18), kind=kOutput, calls=%fused_computation.12 | convolution fusion | flops 1611137024 | bytes 6815744 | tf_op jit(solution)/shard_map/dot_general | solution.py:96
  13.9 0.1 add_reduce_fusion
  14.0 0.1 reshape.509
  14.1 0.1 reshape.510
  14.2 0.1 multiply_convert_fusion.1
  14.4 0.9 copy.20
  15.2 0.0 all-gather.2.cloned.1.call-update
  15.3 0.6 cosine_convert_fusion
  15.9 0.7 pad_maximum_fusion.2.table_ref
  16.5 79.0 %all-gather.2.cloned.1.call-done = bf16[32,128,8,128]{3,2,1,0:T(8,128)(2,1)} async-done(((bf16[1,128,8,128]{3,2,1,0:T(8,128)(2,1)}), bf16[32,128,8,128]{3,2,1,0:T(8,128)(2,1)}) %all-gather.2.cloned.1.call-update) | async-done | bytes 8388624 | tf_op jit(solution)/shard_map/all_gather | solution.py:106
  95.5 1.7 %constant_dynamic-slice_fusion = bf16[1,8,128,8,128]{4,3,2,1,0:T(8,128)(2,1)S(1)} fusion(bf16[4,8,128,8,128]{4,3,2,1,0:T(8,128)(2,1)} %bitcast.62, s32[]{:T(128)S(6)} %select_n.134), kind=kLoop, calls=%fused_computation.97 | loop fusion | bytes 4194308 | tf_op jit(solution)/shard_map/jit(dynamic_index_in_dim)/dynamic_slice | solution.py:110
  97.3 0.7 fusion.16
  98.1 3.0 %copy.25 = bf16[8,128,8,32,1]{3,2,0,4,1:T(8,128)(2,1)S(1)} copy(bf16[8,128,8,32,1]{1,3,2,0,4:T(8,128)(2,1)S(1)} %maximum_bitcast_fusion) | data formatting | bytes 1048576 | tf_op jit(solution)/shard_map/concatenate | solution.py:119
  101.1 7.0 %fusion.3.cross_ref = bf16[128,4,32,128]{3,2,1,0:T(8,128)(2,1)} fusion(bf16[8,128,8,32,1]{3,2,0,4,1:T(8,128)(2,1)S(1)} %copy.25, bf16[4,8,128,8,128]{4,3,2,1,0:T(8,128)(2,1)} %bitcast.63), kind=kOutput, calls=%fused_computation.4 | convolution fusion | flops 272629760 | bytes 13107200 | tf_op jit(solution)/shard_map/tkqa,ctkqw->kcaw/dot_general | solution.py:123
  108.1 9.2 %shard_map.17 = f32[16,512,256]{2,1,0:T(8,128)} custom-call(bf16[128,4,32,128]{3,2,1,0:T(8,128)(2,1)} %fusion.3.cross_ref, bf16[256,256]{1,0:T(8,128)(2,1)} %pad_maximum_fusion.2.table_ref), custom_call_target="tpu_custom_call" | custom-call | tf_op jit(solution)/shard_map/pallas_call | solution.py:73
  (16 shorter events, 0.2 us)
Async XLA Ops:
  6.5 89.0 %all-gather.2.cloned.1.call-start = ((), (), s32[]{:S(2)}) async-start(), calls=%async_computation | async-start | bytes 8650752 | tf_op jit(solution)/shard_map/all_gather | solution.py:106
  8.1 2.2 %copy-start = (f32[4,128,2048]{2,1,0:T(8,128)S(1)}, f32[4,128,2048]{2,1,0:T(8,128)}, u32[]{:S(2)}) copy-start(f32[4,128,2048]{2,1,0:T(8,128)} %param.1) | copy-start | bytes 12582916
Sparse Core Ops, SparseCore 0:
  15.4 80.0 all-gather.1

commit v13 on v12

--- a/solution.py
+++ b/solution.py
@@ -107,13 +107,9 @@
     every = every.reshape(chan_count, time_count, freq_count, 2 * seg_count, block_width)
     chan_index = lax.axis_index("chan")
     tm_index = lax.axis_index("tm")
-    own_block = lax.dynamic_index_in_dim(every, chan_index, 0, keepdims=False)
-    row_ids = tm_index * row_width + jnp.arange(row_width, dtype=jnp.int32)
-    pick = (jnp.arange(block_width, dtype=jnp.int32)[:, None] == row_ids[None, :])
-    rows = jnp.einsum(
-        "tkqw,wi->tkqi", own_block, pick.astype(jnp.bfloat16),
-        preferred_element_type=jnp.float32,
-    ).astype(jnp.bfloat16)
+    parts = local_spec.reshape(freq_count, 2 * seg_count, time_count, row_width)
+    parts = lax.all_to_all(parts, "tm", 2, 2, tiled=True)
+    rows = jnp.transpose(parts, (2, 0, 1, 3))
     rows = rows.reshape(time_count, freq_count, 2, seg_count, row_width)
     turned = jnp.stack([rows[:, :, 1], -rows[:, :, 0]], axis=2)
     left = jnp.concatenate([rows, turned], axis=4).reshape(

time: 124 us -> 121 us (0.976)
  waiting for transfers between devices: 79 us -> 70.7 us
  starting transfers between devices: 0.01 us -> 6.33 us
    all_gather x1, waiting for transfers between devices: 79 us -> 60.5 us  [per_device(): every = lax.all_gather(local_spec, ('chan', 'tm'), axis=0)]
    all_to_all x0 -> x1, waiting for transfers between devices: none -> 10.1 us  [per_device(): parts = lax.all_to_all(parts, 'tm', 2, 2, tiled=True)]
    all_to_all x0 -> x1, starting transfers between devices: none -> 6.32 us  [per_device(): parts = lax.all_to_all(parts, 'tm', 2, 2, tiled=True)]
    dynamic_slice x1 -> x0, local copies, waits for them, and re-layouts: 1.74 us -> none  [per_device(): own_block = lax.dynamic_index_in_dim(every, chan_index, 0, keepdims=False)]
  transfers between devices with their start and end apart: 1 -> 2, of which waited for: 1 -> 2; matrix products, arithmetic and copies ran while one was open for 1% -> 4% of each run, Pallas kernels for 0% -> 0%
where the time goes in v13:
time: 121 us
  waiting for transfers between devices  70.7 us (58%)
  between operations  13.5 us (11%)
  matrix products  10.7 us (9%)
  Pallas kernels  9.19 us (8%)
  local copies, waits for them, and re-layouts  6.57 us (5%)
  starting transfers between devices  6.33 us (5%)
  other arithmetic  3.72 us (3%)
    all_gather x1, waiting for transfers between devices, per_device(): every = lax.all_gather(local_spec, ('chan', 'tm'), axis=0)  60.5 us
    all_to_all x1, waiting for transfers between devices, per_device(): parts = lax.all_to_all(parts, 'tm', 2, 2, tiled=True)  10.1 us
    pallas_call x1, Pallas kernels, lag_transform(): pl.pallas_call(lag_kernel, grid=(chan_count,), in_specs=[pl.BlockSpec((fr...  9.19 us
    dot_general x1, matrix products, per_device(): jnp.einsum('tkqa,ctkqw->kcaw', left, every, preferred_element_type=jnp.fl...  7.11 us
    all_to_all x1, starting transfers between devices, per_device(): parts = lax.all_to_all(parts, 'tm', 2, 2, tiled=True)  6.32 us
    dot_general x1, matrix products, per_device(): jnp.dot(raw_rows, folded, precision=lax.Precision.HIGH, preferred_element...  3.59 us
    concatenate x1, local copies, waits for them, and re-layouts, per_device(): jnp.concatenate([rows, turned], axis=4)  2.98 us
  transfers between devices with their start and end apart: 2, of which 2 were waited for; matrix products, arithmetic and copies ran while one was open for 4% of the time, Pallas kernels for 0%

profile of v13, /device:TPU:0, one launch (start us, length us, event | category | flops | bytes accessed | tf_op | source)
XLA Modules:
  0.0 120.7 jit_solution(16544910496288088861)
XLA Ops:
  6.5 0.0 all-gather.2.cloned.1.call-start
  6.6 0.3 fusion.31
  6.9 0.2 fusion.33
  7.1 0.1 add.254
  7.2 0.1 add.251
  7.2 0.1 add.252
  7.3 0.1 and.154
  7.4 0.1 mul.391
  7.5 0.6 multiply_subtract_fusion.1
  8.1 0.0 copy-start
  8.1 1.0 fusion.15
  9.1 1.2 copy-done
  10.3 3.6 %fusion.10 = f32[512,256]{0,1:T(8,128)S(1)} fusion(f32[512,2048]{1,0:T(8,128)S(1)} %bitcast.52, f32[2048,128]{1,0:T(8,128)S(1)} %get-tuple-element.21, f32[2048,128]{1,0:T(8,128)S(1)} %get-tuple-element.20), kind=kOutput, calls=%fused_computation.9 | convolution fusion | flops 1611137024 | bytes 6815744 | tf_op jit(solution)/shard_map/dot_general | solution.py:96
  13.9 0.1 add_reduce_fusion
  14.0 0.1 reshape.505
  14.1 0.1 reshape.506
  14.2 0.1 multiply_convert_fusion.1
  14.3 0.9 copy.19
  15.3 0.0 all-gather.2.cloned.1.call-update
  15.3 0.2 copy.20
  15.5 0.7 copy.21
  16.2 6.3 %all-to-all-start = ((bf16[128,8,8,16]{0,3,1,2:T(8,128)(2,1)}), bf16[128,8,8,16]{0,3,1,2:T(8,128)(2,1)S(1)}, u32[]{:S(2)}, u32[]{:S(2)}) async-start(bf16[128,8,8,16]{0,3,1,2:T(8,128)(2,1)} %copy.21), calls=%async_computation | async-start | bytes 524288 | tf_op jit(solution)/shard_map/all_to_all | solution.py:111
  22.5 0.6 cosine_convert_fusion
  23.2 0.7 pad_maximum_fusion.2.table_ref
  23.8 10.1 %all-to-all-done = bf16[128,8,8,16]{0,3,1,2:T(8,128)(2,1)S(1)} async-done(((bf16[128,8,8,16]{0,3,1,2:T(8,128)(2,1)}), bf16[128,8,8,16]{0,3,1,2:T(8,128)(2,1)S(1)}, u32[]{:S(2)}, u32[]{:S(2)}) %all-to-all-start) | async-done | bytes 262176 | tf_op jit(solution)/shard_map/all_to_all | solution.py:111
  34.1 3.0 %copy.24 = bf16[8,128,8,32,1]{3,2,0,4,1:T(8,128)(2,1)S(1)} copy(bf16[8,128,8,32,1]{1,3,2,0,4:T(8,128)(2,1)S(1)} %maximum_bitcast_fusion) | data formatting | bytes 1048576 | tf_op jit(solution)/shard_map/concatenate | solution.py:115
  37.1 60.5 %all-gather.2.cloned.1.call-done = bf16[32,128,8,128]{3,2,1,0:T(8,128)(2,1)} async-done(((bf16[1,128,8,128]{3,2,1,0:T(8,128)(2,1)}), bf16[32,128,8,128]{3,2,1,0:T(8,128)(2,1)}) %all-gather.2.cloned.1.call-update) | async-done | bytes 8388624 | tf_op jit(solution)/shard_map/all_gather | solution.py:106
  97.6 7.1 %fusion.3.cross_ref = bf16[128,4,32,128]{3,2,1,0:T(8,128)(2,1)} fusion(bf16[8,128,8,32,1]{3,2,0,4,1:T(8,128)(2,1)S(1)} %copy.24, bf16[4,8,128,8,128]{4,3,2,1,0:T(8,128)(2,1)} %bitcast.58), kind=kOutput, calls=%fused_computation.4 | convolution fusion | flops 272629760 | bytes 13107200 | tf_op jit(solution)/shard_map/tkqa,ctkqw->kcaw/dot_general | solution.py:119
  104.7 9.2 %shard_map.17 = f32[16,512,256]{2,1,0:T(8,128)} custom-call(bf16[128,4,32,128]{3,2,1,0:T(8,128)(2,1)} %fusion.3.cross_ref, bf16[256,256]{1,0:T(8,128)(2,1)} %pad_maximum_fusion.2.table_ref), custom_call_target="tpu_custom_call" | custom-call | tf_op jit(solution)/shard_map/pallas_call | solution.py:73
  (15 shorter events, 0.2 us)
Async XLA Ops:
  6.5 91.0 %all-gather.2.cloned.1.call-start = ((), (), s32[]{:S(2)}) async-start(), calls=%async_computation.1 | async-start | bytes 8650752 | tf_op jit(solution)/shard_map/all_gather | solution.py:106
  8.1 2.2 %copy-start = (f32[4,128,2048]{2,1,0:T(8,128)S(1)}, f32[4,128,2048]{2,1,0:T(8,128)}, u32[]{:S(2)}) copy-start(f32[4,128,2048]{2,1,0:T(8,128)} %param.1) | copy-start | bytes 12582916
  16.2 17.8 %all-to-all-start = ((bf16[128,8,8,16]{0,3,1,2:T(8,128)(2,1)}), bf16[128,8,8,16]{0,3,1,2:T(8,128)(2,1)S(1)}, u32[]{:S(2)}, u32[]{:S(2)}) async-start(bf16[128,8,8,16]{0,3,1,2:T(8,128)(2,1)} %copy.21), calls=%async_computation | async-start | bytes 524288 | tf_op jit(solution)/shard_map/all_to_all | solution.py:111
Sparse Core Ops, SparseCore 0:
  15.4 82.1 all-gather.1

commit v14 on v13

--- a/solution.py
+++ b/solution.py
@@ -56,28 +56,34 @@
 
 def lag_kernel(cross_ref, table_ref, out_ref):
     row_width = out_ref.shape[0]
+    block_count = cross_ref.shape[1]
+    block_width = cross_ref.shape[3]
     table = table_ref[...]
-    for row in range(row_width):
-        real_rows = cross_ref[:, row, :]
-        imag_rows = cross_ref[:, row_width + row, :]
-        both = jnp.concatenate([real_rows, imag_rows], axis=0)
-        out_ref[row] = lax.dot_general(
-            both, table, (((0,), (0,)), ((), ())), preferred_element_type=jnp.float32
-        )
+    for block in range(block_count):
+        for row in range(row_width):
+            real_rows = cross_ref[:, block, row, :]
+            imag_rows = cross_ref[:, block, row_width + row, :]
+            both = jnp.concatenate([real_rows, imag_rows], axis=0)
+            out_ref[row, block * block_width:(block + 1) * block_width, :] = lax.dot_general(
+                both, table, (((0,), (0,)), ((), ())), preferred_element_type=jnp.float32
+            )
 
 
 def lag_transform(cross, table, interpret=False):
     freq_count, chan_count, pair_rows, block_width = cross.shape
     row_width = pair_rows // 2
+    step_blocks = 2 if chan_count % 2 == 0 else 1
     lag_count = table.shape[1]
     return pl.pallas_call(
         lag_kernel,
-        grid=(chan_count,),
+        grid=(chan_count // step_blocks,),
         in_specs=[
-            pl.BlockSpec((freq_count, None, pair_rows, block_width), lambda c: (0, c, 0, 0)),
+            pl.BlockSpec((freq_count, step_blocks, pair_rows, block_width), lambda c: (0, c, 0, 0)),
             pl.BlockSpec((2 * freq_count, lag_count), lambda c: (0, 0)),
         ],
-        out_specs=pl.BlockSpec((row_width, block_width, lag_count), lambda c: (0, c, 0)),
+        out_specs=pl.BlockSpec(
+            (row_width, step_blocks * block_width, lag_count), lambda c: (0, c, 0)
+        ),
         out_shape=jax.ShapeDtypeStruct((row_width, chan_count * block_width, lag_count), jnp.float32),
         interpret=interpret,
     )(cross, table)

time: 121 us -> 121 us (level)
  no operation moved by 1% of the time
where the time goes in v14:
time: 121 us
  waiting for transfers between devices  70.7 us (58%)
  between operations  13.5 us (11%)
  matrix products  10.7 us (9%)
  Pallas kernels  9.3 us (8%)
  local copies, waits for them, and re-layouts  6.57 us (5%)
  starting transfers between devices  6.33 us (5%)
  other arithmetic  3.72 us (3%)
    all_gather x1, waiting for transfers between devices, per_device(): every = lax.all_gather(local_spec, ('chan', 'tm'), axis=0)  60.5 us
    all_to_all x1, waiting for transfers between devices, per_device(): parts = lax.all_to_all(parts, 'tm', 2, 2, tiled=True)  10.1 us
    pallas_call x1, Pallas kernels, lag_transform(): pl.pallas_call(lag_kernel, grid=(chan_count // step_blocks,), in_specs=[p...  9.3 us
    dot_general x1, matrix products, per_device(): jnp.einsum('tkqa,ctkqw->kcaw', left, every, preferred_element_type=jnp.fl...  7.11 us
    all_to_all x1, starting transfers between devices, per_device(): parts = lax.all_to_all(parts, 'tm', 2, 2, tiled=True)  6.33 us
    dot_general x1, matrix products, per_device(): jnp.dot(raw_rows, folded, precision=lax.Precision.HIGH, preferred_element...  3.59 us
    concatenate x1, local copies, waits for them, and re-layouts, per_device(): jnp.concatenate([rows, turned], axis=4)  2.98 us
  transfers between devices with their start and end apart: 2, of which 2 were waited for; matrix products, arithmetic and copies ran while one was open for 4% of the time, Pallas kernels for 0%

profile of v14, /device:TPU:0, one launch (start us, length us, event | category | flops | bytes accessed | tf_op | source)
XLA Modules:
  0.0 120.8 jit_solution(3821897267600763218)
XLA Ops:
  6.5 0.0 all-gather.2.cloned.1.call-start
  6.6 0.3 fusion.31
  6.9 0.2 fusion.33
  7.1 0.1 add.254
  7.2 0.1 add.251
  7.2 0.1 add.252
  7.3 0.1 and.154
  7.4 0.1 mul.391
  7.5 0.6 multiply_subtract_fusion.1
  8.1 0.0 copy-start
  8.1 1.0 fusion.15
  9.1 1.2 copy-done
  10.3 3.6 %fusion.10 = f32[512,256]{0,1:T(8,128)S(1)} fusion(f32[512,2048]{1,0:T(8,128)S(1)} %bitcast.52, f32[2048,128]{1,0:T(8,128)S(1)} %get-tuple-element.21, f32[2048,128]{1,0:T(8,128)S(1)} %get-tuple-element.20), kind=kOutput, calls=%fused_computation.9 | convolution fusion | flops 1611137024 | bytes 6815744 | tf_op jit(solution)/shard_map/dot_general | solution.py:102
  13.9 0.1 add_reduce_fusion
  14.0 0.1 reshape.505
  14.1 0.1 reshape.506
  14.2 0.1 multiply_convert_fusion.1
  14.3 0.9 copy.19
  15.3 0.0 all-gather.2.cloned.1.call-update
  15.3 0.2 copy.20
  15.5 0.7 copy.21
  16.2 6.3 %all-to-all-start = ((bf16[128,8,8,16]{0,3,1,2:T(8,128)(2,1)}), bf16[128,8,8,16]{0,3,1,2:T(8,128)(2,1)S(1)}, u32[]{:S(2)}, u32[]{:S(2)}) async-start(bf16[128,8,8,16]{0,3,1,2:T(8,128)(2,1)} %copy.21), calls=%async_computation | async-start | bytes 524288 | tf_op jit(solution)/shard_map/all_to_all | solution.py:117
  22.5 0.6 cosine_convert_fusion
  23.2 0.7 pad_maximum_fusion.2.table_ref
  23.8 10.1 %all-to-all-done = bf16[128,8,8,16]{0,3,1,2:T(8,128)(2,1)S(1)} async-done(((bf16[128,8,8,16]{0,3,1,2:T(8,128)(2,1)}), bf16[128,8,8,16]{0,3,1,2:T(8,128)(2,1)S(1)}, u32[]{:S(2)}, u32[]{:S(2)}) %all-to-all-start) | async-done | bytes 262176 | tf_op jit(solution)/shard_map/all_to_all | solution.py:117
  34.1 3.0 %copy.24 = bf16[8,128,8,32,1]{3,2,0,4,1:T(8,128)(2,1)S(1)} copy(bf16[8,128,8,32,1]{1,3,2,0,4:T(8,128)(2,1)S(1)} %maximum_bitcast_fusion) | data formatting | bytes 1048576 | tf_op jit(solution)/shard_map/concatenate | solution.py:121
  37.1 60.5 %all-gather.2.cloned.1.call-done = bf16[32,128,8,128]{3,2,1,0:T(8,128)(2,1)} async-done(((bf16[1,128,8,128]{3,2,1,0:T(8,128)(2,1)}), bf16[32,128,8,128]{3,2,1,0:T(8,128)(2,1)}) %all-gather.2.cloned.1.call-update) | async-done | bytes 8388624 | tf_op jit(solution)/shard_map/all_gather | solution.py:112
  97.6 7.1 %fusion.3.cross_ref = bf16[128,4,32,128]{3,2,1,0:T(8,128)(2,1)} fusion(bf16[8,128,8,32,1]{3,2,0,4,1:T(8,128)(2,1)S(1)} %copy.24, bf16[4,8,128,8,128]{4,3,2,1,0:T(8,128)(2,1)} %bitcast.58), kind=kOutput, calls=%fused_computation.4 | convolution fusion | flops 272629760 | bytes 13107200 | tf_op jit(solution)/shard_map/tkqa,ctkqw->kcaw/dot_general | solution.py:125
  104.7 9.3 %shard_map.17 = f32[16,512,256]{2,1,0:T(8,128)} custom-call(bf16[128,4,32,128]{3,2,1,0:T(8,128)(2,1)} %fusion.3.cross_ref, bf16[256,256]{1,0:T(8,128)(2,1)} %pad_maximum_fusion.2.table_ref), custom_call_target="tpu_custom_call" | custom-call | tf_op jit(solution)/shard_map/pallas_call | solution.py:77
  (15 shorter events, 0.2 us)
Async XLA Ops:
  6.5 91.0 %all-gather.2.cloned.1.call-start = ((), (), s32[]{:S(2)}) async-start(), calls=%async_computation.1 | async-start | bytes 8650752 | tf_op jit(solution)/shard_map/all_gather | solution.py:112
  8.1 2.2 %copy-start = (f32[4,128,2048]{2,1,0:T(8,128)S(1)}, f32[4,128,2048]{2,1,0:T(8,128)}, u32[]{:S(2)}) copy-start(f32[4,128,2048]{2,1,0:T(8,128)} %param.1) | copy-start | bytes 12582916
  16.2 17.8 %all-to-all-start = ((bf16[128,8,8,16]{0,3,1,2:T(8,128)(2,1)}), bf16[128,8,8,16]{0,3,1,2:T(8,128)(2,1)S(1)}, u32[]{:S(2)}, u32[]{:S(2)}) async-start(bf16[128,8,8,16]{0,3,1,2:T(8,128)(2,1)} %copy.21), calls=%async_computation | async-start | bytes 524288 | tf_op jit(solution)/shard_map/all_to_all | solution.py:117
Sparse Core Ops, SparseCore 0:
  15.4 82.1 all-gather.1

commit v15 on v14

--- a/solution.py
+++ b/solution.py
@@ -59,14 +59,26 @@
     block_count = cross_ref.shape[1]
     block_width = cross_ref.shape[3]
     table = table_ref[...]
+    pair = 2 if row_width % 2 == 0 else 1
     for block in range(block_count):
-        for row in range(row_width):
-            real_rows = cross_ref[:, block, row, :]
-            imag_rows = cross_ref[:, block, row_width + row, :]
-            both = jnp.concatenate([real_rows, imag_rows], axis=0)
-            out_ref[row, block * block_width:(block + 1) * block_width, :] = lax.dot_general(
+        for first in range(0, row_width, pair):
+            both = jnp.concatenate(
+                [
+                    jnp.concatenate(
+                        [cross_ref[:, block, row, :], cross_ref[:, block, row_width + row, :]],
+                        axis=0,
+                    )
+                    for row in range(first, first + pair)
+                ],
+                axis=1,
+            )
+            lags = lax.dot_general(
                 both, table, (((0,), (0,)), ((), ())), preferred_element_type=jnp.float32
             )
+            for offset in range(pair):
+                out_ref[first + offset, block * block_width:(block + 1) * block_width, :] = lags[
+                    offset * block_width:(offset + 1) * block_width
+                ]
 
 
 def lag_transform(cross, table, interpret=False):

time: 121 us -> 122 us (level)
  Pallas kernels: 9.3 us -> 10.6 us
    pallas_call x1, Pallas kernels: 9.3 us -> 10.6 us  [lag_transform(): pl.pallas_call(lag_kernel, grid=(chan_count // step_blocks,), in_specs=[p...]
where the time goes in v15:
time: 122 us
  waiting for transfers between devices  70.7 us (58%)
  between operations  13.5 us (11%)
  matrix products  10.7 us (9%)
  Pallas kernels  10.6 us (9%)
  local copies, waits for them, and re-layouts  6.57 us (5%)
  starting transfers between devices  6.33 us (5%)
  other arithmetic  3.72 us (3%)
    all_gather x1, waiting for transfers between devices, per_device(): every = lax.all_gather(local_spec, ('chan', 'tm'), axis=0)  60.5 us
    pallas_call x1, Pallas kernels, lag_transform(): pl.pallas_call(lag_kernel, grid=(chan_count // step_blocks,), in_specs=[p...  10.6 us
    all_to_all x1, waiting for transfers between devices, per_device(): parts = lax.all_to_all(parts, 'tm', 2, 2, tiled=True)  10.1 us
    dot_general x1, matrix products, per_device(): jnp.einsum('tkqa,ctkqw->kcaw', left, every, preferred_element_type=jnp.fl...  7.11 us
    all_to_all x1, starting transfers between devices, per_device(): parts = lax.all_to_all(parts, 'tm', 2, 2, tiled=True)  6.33 us
    dot_general x1, matrix products, per_device(): jnp.dot(raw_rows, folded, precision=lax.Precision.HIGH, preferred_element...  3.59 us
    concatenate x1, local copies, waits for them, and re-layouts, per_device(): jnp.concatenate([rows, turned], axis=4)  2.98 us
  transfers between devices with their start and end apart: 2, of which 2 were waited for; matrix products, arithmetic and copies ran while one was open for 4% of the time, Pallas kernels for 0%

profile of v15, /device:TPU:0, one launch (start us, length us, event | category | flops | bytes accessed | tf_op | source)
XLA Modules:
  0.0 122.2 jit_solution(16279045019645878140)
XLA Ops:
  6.5 0.0 all-gather.2.cloned.1.call-start
  6.6 0.3 fusion.31
  6.9 0.2 fusion.33
  7.1 0.1 add.254
  7.2 0.1 add.251
  7.2 0.1 add.252
  7.3 0.1 and.154
  7.4 0.1 mul.391
  7.5 0.6 multiply_subtract_fusion.1
  8.1 0.0 copy-start
  8.1 1.0 fusion.15
  9.1 1.2 copy-done
  10.3 3.6 %fusion.10 = f32[512,256]{0,1:T(8,128)S(1)} fusion(f32[512,2048]{1,0:T(8,128)S(1)} %bitcast.52, f32[2048,128]{1,0:T(8,128)S(1)} %get-tuple-element.21, f32[2048,128]{1,0:T(8,128)S(1)} %get-tuple-element.20), kind=kOutput, calls=%fused_computation.9 | convolution fusion | flops 1611137024 | bytes 6815744 | tf_op jit(solution)/shard_map/dot_general | solution.py:114
  13.9 0.1 add_reduce_fusion
  14.0 0.1 reshape.505
  14.1 0.1 reshape.506
  14.2 0.1 multiply_convert_fusion.1
  14.3 0.9 copy.19
  15.3 0.0 all-gather.2.cloned.1.call-update
  15.3 0.2 copy.20
  15.5 0.7 copy.21
  16.2 6.3 %all-to-all-start = ((bf16[128,8,8,16]{0,3,1,2:T(8,128)(2,1)}), bf16[128,8,8,16]{0,3,1,2:T(8,128)(2,1)S(1)}, u32[]{:S(2)}, u32[]{:S(2)}) async-start(bf16[128,8,8,16]{0,3,1,2:T(8,128)(2,1)} %copy.21), calls=%async_computation | async-start | bytes 524288 | tf_op jit(solution)/shard_map/all_to_all | solution.py:129
  22.5 0.6 cosine_convert_fusion
  23.2 0.7 pad_maximum_fusion.2.table_ref
  23.8 10.1 %all-to-all-done = bf16[128,8,8,16]{0,3,1,2:T(8,128)(2,1)S(1)} async-done(((bf16[128,8,8,16]{0,3,1,2:T(8,128)(2,1)}), bf16[128,8,8,16]{0,3,1,2:T(8,128)(2,1)S(1)}, u32[]{:S(2)}, u32[]{:S(2)}) %all-to-all-start) | async-done | bytes 262176 | tf_op jit(solution)/shard_map/all_to_all | solution.py:129
  34.1 3.0 %copy.24 = bf16[8,128,8,32,1]{3,2,0,4,1:T(8,128)(2,1)S(1)} copy(bf16[8,128,8,32,1]{1,3,2,0,4:T(8,128)(2,1)S(1)} %maximum_bitcast_fusion) | data formatting | bytes 1048576 | tf_op jit(solution)/shard_map/concatenate | solution.py:133
  37.1 60.5 %all-gather.2.cloned.1.call-done = bf16[32,128,8,128]{3,2,1,0:T(8,128)(2,1)} async-done(((bf16[1,128,8,128]{3,2,1,0:T(8,128)(2,1)}), bf16[32,128,8,128]{3,2,1,0:T(8,128)(2,1)}) %all-gather.2.cloned.1.call-update) | async-done | bytes 8388624 | tf_op jit(solution)/shard_map/all_gather | solution.py:124
  97.6 7.1 %fusion.3.cross_ref = bf16[128,4,32,128]{3,2,1,0:T(8,128)(2,1)} fusion(bf16[8,128,8,32,1]{3,2,0,4,1:T(8,128)(2,1)S(1)} %copy.24, bf16[4,8,128,8,128]{4,3,2,1,0:T(8,128)(2,1)} %bitcast.58), kind=kOutput, calls=%fused_computation.4 | convolution fusion | flops 272629760 | bytes 13107200 | tf_op jit(solution)/shard_map/tkqa,ctkqw->kcaw/dot_general | solution.py:137
  104.7 10.6 %shard_map.17 = f32[16,512,256]{2,1,0:T(8,128)} custom-call(bf16[128,4,32,128]{3,2,1,0:T(8,128)(2,1)} %fusion.3.cross_ref, bf16[256,256]{1,0:T(8,128)(2,1)} %pad_maximum_fusion.2.table_ref), custom_call_target="tpu_custom_call" | custom-call | tf_op jit(solution)/shard_map/pallas_call | solution.py:89
  (15 shorter events, 0.2 us)
Async XLA Ops:
  6.5 91.0 %all-gather.2.cloned.1.call-start = ((), (), s32[]{:S(2)}) async-start(), calls=%async_computation.1 | async-start | bytes 8650752 | tf_op jit(solution)/shard_map/all_gather | solution.py:124
  8.1 2.2 %copy-start = (f32[4,128,2048]{2,1,0:T(8,128)S(1)}, f32[4,128,2048]{2,1,0:T(8,128)}, u32[]{:S(2)}) copy-start(f32[4,128,2048]{2,1,0:T(8,128)} %param.1) | copy-start | bytes 12582916
  16.2 17.8 %all-to-all-start = ((bf16[128,8,8,16]{0,3,1,2:T(8,128)(2,1)}), bf16[128,8,8,16]{0,3,1,2:T(8,128)(2,1)S(1)}, u32[]{:S(2)}, u32[]{:S(2)}) async-start(bf16[128,8,8,16]{0,3,1,2:T(8,128)(2,1)} %copy.21), calls=%async_computation | async-start | bytes 524288 | tf_op jit(solution)/shard_map/all_to_all | solution.py:129
Sparse Core Ops, SparseCore 0:
  15.4 82.1 all-gather.1

commit v16 on v14

--- a/solution.py
+++ b/solution.py
@@ -1,4 +1,6 @@
 import math
+
+import numpy as np
 
 import jax
 import jax.numpy as jnp
@@ -25,33 +27,15 @@
 
 
 def folded_tables(sample_count, freq_count):
-    fine_rows = 64
-    coarse_rows = 2 * sample_count // fine_rows
-    scale = 2.0 * math.pi / sample_count
-    freq_index = jnp.arange(1, freq_count + 1, dtype=jnp.int32)[None, None, :]
-    coarse_time = jnp.arange(coarse_rows, dtype=jnp.int32)[:, None, None] * (fine_rows // 2)
-    fine = jnp.arange(fine_rows, dtype=jnp.int32)[None, :, None]
-    fine_time = fine // 2
-    odd = (fine % 2) == 1
-
-    def angle(times):
-        return (times * freq_index % sample_count).astype(jnp.float32) * scale
-
-    coarse_angle = angle(coarse_time)
-    coarse_cos, coarse_sin = jnp.cos(coarse_angle), jnp.sin(coarse_angle)
-    this_angle = angle(fine_time)
-    next_angle = angle(fine_time + 1)
-    this_cos = coarse_cos * jnp.cos(this_angle) - coarse_sin * jnp.sin(this_angle)
-    this_sin = coarse_sin * jnp.cos(this_angle) + coarse_cos * jnp.sin(this_angle)
-    next_cos = coarse_cos * jnp.cos(next_angle) - coarse_sin * jnp.sin(next_angle)
-    next_sin = coarse_sin * jnp.cos(next_angle) + coarse_cos * jnp.sin(next_angle)
-    last_row = (coarse_time + fine_time + 1) >= sample_count
-    this_weight = jnp.where(odd, 0.25, 0.5)
-    next_weight = jnp.where(odd & ~last_row, 0.25, 0.0)
-    cos_part = this_weight * this_cos + next_weight * next_cos
-    sin_part = -(this_weight * this_sin + next_weight * next_sin)
-    both = jnp.concatenate([cos_part, sin_part], axis=-1)
-    return both.reshape(2 * sample_count, 2 * freq_count)
+    time_index = np.arange(sample_count + 1, dtype=np.int64)[:, None]
+    freq_index = np.arange(1, freq_count + 1, dtype=np.int64)[None, :]
+    angle = (time_index * freq_index % sample_count) * (2.0 * np.pi / sample_count)
+    table = np.concatenate([np.cos(angle), -np.sin(angle)], axis=1)
+    table[sample_count] = 0.0
+    folded = np.empty((2 * sample_count, 2 * freq_count))
+    folded[0::2] = 0.5 * table[:sample_count]
+    folded[1::2] = 0.25 * table[:sample_count] + 0.25 * table[1:]
+    return jnp.asarray(folded.astype(np.float32))
 
 
 def lag_kernel(cross_ref, table_ref, out_ref):

time: 121 us -> 120 us (level)
  matrix products: 10.7 us -> 13.3 us
  other arithmetic: 3.72 us -> 1.58 us
  local copies, waits for them, and re-layouts: 6.57 us -> 4.96 us
    dot_general x1, matrix products: 3.59 us -> 6.29 us  [per_device(): jnp.dot(raw_rows, folded, precision=lax.Precision.HIGH, preferred_element...]
where the time goes in v16:
time: 120 us
  waiting for transfers between devices  70.7 us (59%)
  between operations  13.5 us (11%)
  matrix products  13.3 us (11%)
  Pallas kernels  9.3 us (8%)
  starting transfers between devices  6.33 us (5%)
  local copies, waits for them, and re-layouts  4.96 us (4%)
  other arithmetic  1.58 us (1%)
    all_gather x1, waiting for transfers between devices, per_device(): every = lax.all_gather(local_spec, ('chan', 'tm'), axis=0)  60.5 us
    all_to_all x1, waiting for transfers between devices, per_device(): parts = lax.all_to_all(parts, 'tm', 2, 2, tiled=True)  10.1 us
    pallas_call x1, Pallas kernels, lag_transform(): pl.pallas_call(lag_kernel, grid=(chan_count // step_blocks,), in_specs=[p...  9.3 us
    dot_general x1, matrix products, per_device(): jnp.einsum('tkqa,ctkqw->kcaw', left, every, preferred_element_type=jnp.fl...  7.03 us
    all_to_all x1, starting transfers between devices, per_device(): parts = lax.all_to_all(parts, 'tm', 2, 2, tiled=True)  6.33 us
    dot_general x1, matrix products, per_device(): jnp.dot(raw_rows, folded, precision=lax.Precision.HIGH, preferred_element...  6.29 us
    concatenate x1, local copies, waits for them, and re-layouts, per_device(): jnp.concatenate([rows, turned], axis=4)  2.98 us
  transfers between devices with their start and end apart: 2, of which 2 were waited for; matrix products, arithmetic and copies ran while one was open for 4% of the time, Pallas kernels for 0%

profile of v16, /device:TPU:0, one launch (start us, length us, event | category | flops | bytes accessed | tf_op | source)
XLA Modules:
  0.0 119.6 jit_solution(8727636097949801389)
XLA Ops:
  6.5 0.0 all-gather.2.cloned.1.call-start
  6.5 6.3 %convolution_bitcast_fusion = f32[512,256]{0,1:T(8,128)S(1)} fusion(f32[2048,256]{1,0:T(8,128)} %constant.44.clone, f32[512,2048]{1,0:T(8,128)} %bitcast.33), kind=kOutput, calls=%fused_computation.5 | convolution fusion | flops 1610612736 | bytes 6815744 | tf_op jit(solution)/shard_map/dot_general | solution.py:86
  12.8 0.1 add_reduce_fusion
  12.9 0.1 reshape.113
  13.0 0.1 reshape.114
  13.1 0.1 multiply_convert_fusion.1
  13.3 0.9 copy.20
  14.2 0.0 all-gather.2.cloned.1.call-update
  14.2 0.2 copy.21
  14.4 0.7 copy.22
  15.1 6.3 %all-to-all-start = ((bf16[128,8,8,16]{0,3,1,2:T(8,128)(2,1)}), bf16[128,8,8,16]{0,3,1,2:T(8,128)(2,1)S(1)}, u32[]{:S(2)}, u32[]{:S(2)}) async-start(bf16[128,8,8,16]{0,3,1,2:T(8,128)(2,1)} %copy.22), calls=%async_computation | async-start | bytes 524288 | tf_op jit(solution)/shard_map/all_to_all | solution.py:101
  21.4 0.6 cosine_convert_fusion
  22.1 0.7 pad_maximum_fusion.2.table_ref
  22.7 10.1 %all-to-all-done = bf16[128,8,8,16]{0,3,1,2:T(8,128)(2,1)S(1)} async-done(((bf16[128,8,8,16]{0,3,1,2:T(8,128)(2,1)}), bf16[128,8,8,16]{0,3,1,2:T(8,128)(2,1)S(1)}, u32[]{:S(2)}, u32[]{:S(2)}) %all-to-all-start) | async-done | bytes 262176 | tf_op jit(solution)/shard_map/all_to_all | solution.py:101
  33.0 3.0 %copy.25 = bf16[8,128,8,32,1]{3,2,0,4,1:T(8,128)(2,1)S(1)} copy(bf16[8,128,8,32,1]{1,3,2,0,4:T(8,128)(2,1)S(1)} %maximum_bitcast_fusion) | data formatting | bytes 1048576 | tf_op jit(solution)/shard_map/concatenate | solution.py:105
  36.0 60.5 %all-gather.2.cloned.1.call-done = bf16[32,128,8,128]{3,2,1,0:T(8,128)(2,1)} async-done(((bf16[1,128,8,128]{3,2,1,0:T(8,128)(2,1)}), bf16[32,128,8,128]{3,2,1,0:T(8,128)(2,1)}) %all-gather.2.cloned.1.call-update) | async-done | bytes 8388624 | tf_op jit(solution)/shard_map/all_gather | solution.py:96
  96.5 7.0 %fusion.3.cross_ref = bf16[128,4,32,128]{3,2,1,0:T(8,128)(2,1)} fusion(bf16[8,128,8,32,1]{3,2,0,4,1:T(8,128)(2,1)S(1)} %copy.25, bf16[4,8,128,8,128]{4,3,2,1,0:T(8,128)(2,1)} %bitcast.39), kind=kOutput, calls=%fused_computation.4 | convolution fusion | flops 272629760 | bytes 13107200 | tf_op jit(solution)/shard_map/tkqa,ctkqw->kcaw/dot_general | solution.py:109
  103.5 9.3 %shard_map.28 = f32[16,512,256]{2,1,0:T(8,128)} custom-call(bf16[128,4,32,128]{3,2,1,0:T(8,128)(2,1)} %fusion.3.cross_ref, bf16[256,256]{1,0:T(8,128)(2,1)} %pad_maximum_fusion.2.table_ref), custom_call_target="tpu_custom_call" | custom-call | tf_op jit(solution)/shard_map/pallas_call | solution.py:61
  (7 shorter events, 0.1 us)
Async XLA Ops:
  6.5 89.9 %all-gather.2.cloned.1.call-start = ((), (), s32[]{:S(2)}) async-start(), calls=%async_computation.1 | async-start | bytes 8650752 | tf_op jit(solution)/shard_map/all_gather | solution.py:96
  15.1 17.8 %all-to-all-start = ((bf16[128,8,8,16]{0,3,1,2:T(8,128)(2,1)}), bf16[128,8,8,16]{0,3,1,2:T(8,128)(2,1)S(1)}, u32[]{:S(2)}, u32[]{:S(2)}) async-start(bf16[128,8,8,16]{0,3,1,2:T(8,128)(2,1)} %copy.22), calls=%async_computation | async-start | bytes 524288 | tf_op jit(solution)/shard_map/all_to_all | solution.py:101
Sparse Core Ops, SparseCore 0:
  14.3 82.1 all-gather.1

commit v17 on v16

--- a/solution.py
+++ b/solution.py
@@ -1,5 +1,6 @@
 import math
 
+import ml_dtypes
 import numpy as np
 
 import jax
@@ -35,7 +36,9 @@
     folded = np.empty((2 * sample_count, 2 * freq_count))
     folded[0::2] = 0.5 * table[:sample_count]
     folded[1::2] = 0.25 * table[:sample_count] + 0.25 * table[1:]
-    return jnp.asarray(folded.astype(np.float32))
+    head = folded.astype(np.float32).astype(ml_dtypes.bfloat16)
+    tail = (folded - head.astype(np.float64)).astype(np.float32).astype(ml_dtypes.bfloat16)
+    return jnp.asarray(head), jnp.asarray(tail)
 
 
 def lag_kernel(cross_ref, table_ref, out_ref):
@@ -82,9 +85,13 @@
     channel_total = block_width * chan_count
     row_width = channel_total // (chan_count * time_count)
     raw_rows = raw_samples.reshape(seg_count * block_width, raw_length)
-    folded = folded_tables(sample_count, freq_count)
-    spectrum = jnp.dot(
-        raw_rows, folded, precision=lax.Precision.HIGH, preferred_element_type=jnp.float32
+    table_head, table_tail = folded_tables(sample_count, freq_count)
+    raw_head = raw_rows.astype(jnp.bfloat16)
+    raw_tail = (raw_rows - raw_head.astype(jnp.float32)).astype(jnp.bfloat16)
+    spectrum = (
+        jnp.dot(raw_head, table_head, preferred_element_type=jnp.float32)
+        + jnp.dot(raw_head, table_tail, preferred_element_type=jnp.float32)
+        + jnp.dot(raw_tail, table_head, preferred_element_type=jnp.float32)
     )
     real_part = spectrum[:, :freq_count].reshape(seg_count, block_width, freq_count)
     imag_part = spectrum[:, freq_count:].reshape(seg_count, block_width, freq_count)

time: 120 us -> 120 us (level)
  matrix products: 13.3 us -> 9.31 us
  other arithmetic: 1.58 us -> 4.66 us
    dot_general x1 -> x3, matrix products: 6.29 us -> 2.28 us  [the longest x1 0.77 us: per_device(): jnp.dot(raw_head, table_head, preferred_element_type=jnp.float32)]
    convert_element_type x0 -> x1, other arithmetic: none -> 3.07 us  [per_device(): raw_tail = (raw_rows - raw_head.astype(jnp.float32)).astype(jnp.bfloat16)]
where the time goes in v17:
time: 120 us; the launch traced here: 119 us
  waiting for transfers between devices  70.7 us (59%)
  between operations  13.5 us (11%)
  matrix products  9.31 us (8%)
  Pallas kernels  9.3 us (8%)
  starting transfers between devices  6.33 us (5%)
  local copies, waits for them, and re-layouts  5.43 us (5%)
  other arithmetic  4.66 us (4%)
    all_gather x1, waiting for transfers between devices, per_device(): every = lax.all_gather(local_spec, ('chan', 'tm'), axis=0)  60.5 us
    all_to_all x1, waiting for transfers between devices, per_device(): parts = lax.all_to_all(parts, 'tm', 2, 2, tiled=True)  10.1 us
    pallas_call x1, Pallas kernels, lag_transform(): pl.pallas_call(lag_kernel, grid=(chan_count // step_blocks,), in_specs=[p...  9.3 us
    dot_general x1, matrix products, per_device(): jnp.einsum('tkqa,ctkqw->kcaw', left, every, preferred_element_type=jnp.fl...  7.03 us
    all_to_all x1, starting transfers between devices, per_device(): parts = lax.all_to_all(parts, 'tm', 2, 2, tiled=True)  6.33 us
    convert_element_type x1, other arithmetic, per_device(): raw_tail = (raw_rows - raw_head.astype(jnp.float32)).astype(jnp.bfloat16)  3.07 us
    concatenate x1, local copies, waits for them, and re-layouts, per_device(): jnp.concatenate([rows, turned], axis=4)  2.98 us
  transfers between devices with their start and end apart: 2, of which 2 were waited for; matrix products, arithmetic and copies ran while one was open for 4% of the time, Pallas kernels for 0%

profile of v17, /device:TPU:0, one launch (start us, length us, event | category | flops | bytes accessed | tf_op | source)
XLA Modules:
  0.0 119.2 jit_solution(6451861548600031249)
XLA Ops:
  6.5 0.0 copy-start
  6.5 0.0 all-gather.2.cloned.1.call-start
  6.5 3.1 %fusion.4 = (bf16[512,2048]{1,0:T(8,128)(2,1)S(1)}, bf16[512,2048]{1,0:T(8,128)(2,1)S(1)}) fusion(f32[4,128,2048]{2,1,0:T(8,128)} %param.3), kind=kLoop, calls=%fused_computation.7 | loop fusion | flops 4194304 | bytes 8388608 | tf_op jit(solution)/shard_map/convert_element_type | solution.py:90
  9.6 0.0 copy-start.1
  9.6 0.0 copy-done
  9.6 0.8 fusion.14
  10.4 0.4 copy-done.1
  10.9 0.8 fusion.7
  11.6 0.8 convolution_add_fusion
  12.4 0.1 add_reduce_fusion
  12.5 0.1 reshape.113
  12.6 0.1 reshape.114
  12.7 0.1 multiply_convert_fusion.1
  12.8 0.9 copy.24
  13.7 0.0 all-gather.2.cloned.1.call-update
  13.8 0.2 copy.25
  13.9 0.7 copy.26
  14.7 6.3 %all-to-all-start = ((bf16[128,8,8,16]{0,3,1,2:T(8,128)(2,1)}), bf16[128,8,8,16]{0,3,1,2:T(8,128)(2,1)S(1)}, u32[]{:S(2)}, u32[]{:S(2)}) async-start(bf16[128,8,8,16]{0,3,1,2:T(8,128)(2,1)} %copy.26), calls=%async_computation | async-start | bytes 524288 | tf_op jit(solution)/shard_map/all_to_all | solution.py:108
  21.0 0.6 cosine_convert_fusion
  21.6 0.7 pad_maximum_fusion.2.table_ref
  22.3 10.1 %all-to-all-done = bf16[128,8,8,16]{0,3,1,2:T(8,128)(2,1)S(1)} async-done(((bf16[128,8,8,16]{0,3,1,2:T(8,128)(2,1)}), bf16[128,8,8,16]{0,3,1,2:T(8,128)(2,1)S(1)}, u32[]{:S(2)}, u32[]{:S(2)}) %all-to-all-start) | async-done | bytes 262176 | tf_op jit(solution)/shard_map/all_to_all | solution.py:108
  32.5 3.0 %copy.30 = bf16[8,128,8,32,1]{3,2,0,4,1:T(8,128)(2,1)S(1)} copy(bf16[8,128,8,32,1]{1,3,2,0,4:T(8,128)(2,1)S(1)} %maximum_bitcast_fusion) | data formatting | bytes 1048576 | tf_op jit(solution)/shard_map/concatenate | solution.py:112
  35.5 60.5 %all-gather.2.cloned.1.call-done = bf16[32,128,8,128]{3,2,1,0:T(8,128)(2,1)} async-done(((bf16[1,128,8,128]{3,2,1,0:T(8,128)(2,1)}), bf16[32,128,8,128]{3,2,1,0:T(8,128)(2,1)}) %all-gather.2.cloned.1.call-update) | async-done | bytes 8388624 | tf_op jit(solution)/shard_map/all_gather | solution.py:103
  96.0 7.0 %fusion.3.cross_ref = bf16[128,4,32,128]{3,2,1,0:T(8,128)(2,1)} fusion(bf16[8,128,8,32,1]{3,2,0,4,1:T(8,128)(2,1)S(1)} %copy.30, bf16[4,8,128,8,128]{4,3,2,1,0:T(8,128)(2,1)} %bitcast.47), kind=kOutput, calls=%fused_computation.4 | convolution fusion | flops 272629760 | bytes 13107200 | tf_op jit(solution)/shard_map/tkqa,ctkqw->kcaw/dot_general | solution.py:116
  103.1 9.3 %shard_map.37 = f32[16,512,256]{2,1,0:T(8,128)} custom-call(bf16[128,4,32,128]{3,2,1,0:T(8,128)(2,1)} %fusion.3.cross_ref, bf16[256,256]{1,0:T(8,128)(2,1)} %pad_maximum_fusion.2.table_ref), custom_call_target="tpu_custom_call" | custom-call | tf_op jit(solution)/shard_map/pallas_call | solution.py:64
  (7 shorter events, 0.1 us)
Async XLA Ops:
  6.5 3.1 %copy-start = (bf16[2048,256]{1,0:T(8,128)(2,1)S(1)}, bf16[2048,256]{1,0:T(8,128)(2,1)}, u32[]{:S(2)}) copy-start(bf16[2048,256]{1,0:T(8,128)(2,1)} %constant.46.clone) | copy-start | bytes 3145732
  6.5 89.5 %all-gather.2.cloned.1.call-start = ((), (), s32[]{:S(2)}) async-start(), calls=%async_computation.1 | async-start | bytes 8650752 | tf_op jit(solution)/shard_map/all_gather | solution.py:103
  9.6 1.2 %copy-start.1 = (bf16[2048,256]{1,0:T(8,128)(2,1)S(1)}, bf16[2048,256]{1,0:T(8,128)(2,1)}, u32[]{:S(2)}) copy-start(bf16[2048,256]{1,0:T(8,128)(2,1)} %constant.47.clone) | copy-start | bytes 3145732
  14.7 17.8 %all-to-all-start = ((bf16[128,8,8,16]{0,3,1,2:T(8,128)(2,1)}), bf16[128,8,8,16]{0,3,1,2:T(8,128)(2,1)S(1)}, u32[]{:S(2)}, u32[]{:S(2)}) async-start(bf16[128,8,8,16]{0,3,1,2:T(8,128)(2,1)} %copy.26), calls=%async_computation | async-start | bytes 524288 | tf_op jit(solution)/shard_map/all_to_all | solution.py:108
Sparse Core Ops, SparseCore 0:
  13.9 82.1 all-gather.1

commit v18 on v16

--- a/solution.py
+++ b/solution.py
@@ -47,7 +47,7 @@
         for row in range(row_width):
             real_rows = cross_ref[:, block, row, :]
             imag_rows = cross_ref[:, block, row_width + row, :]
-            both = jnp.concatenate([real_rows, imag_rows], axis=0)
+            both = jnp.concatenate([real_rows, imag_rows], axis=0).astype(jnp.bfloat16)
             out_ref[row, block * block_width:(block + 1) * block_width, :] = lax.dot_general(
                 both, table, (((0,), (0,)), ((), ())), preferred_element_type=jnp.float32
             )
@@ -107,7 +107,7 @@
     )
     norm_scale = 1.0 / math.sqrt(freq_count * seg_count * time_count)
     cross = jnp.einsum("tkqa,ctkqw->kcaw", left, every, preferred_element_type=jnp.float32)
-    cross = (cross * norm_scale).astype(jnp.bfloat16)
+    cross = cross * norm_scale
     table = lag_table(freq_count, sample_count, LAGS)
     return lag_transform(cross, table)
 

time: 120 us -> 121 us (level)
  no operation moved by 1% of the time
where the time goes in v18:
time: 121 us
  waiting for transfers between devices  70.7 us (58%)
  matrix products  14.5 us (12%)
  between operations  13.5 us (11%)
  Pallas kernels  9.56 us (8%)
  starting transfers between devices  6.33 us (5%)
  local copies, waits for them, and re-layouts  4.96 us (4%)
  other arithmetic  1.59 us (1%)
    all_gather x1, waiting for transfers between devices, per_device(): every = lax.all_gather(local_spec, ('chan', 'tm'), axis=0)  60.5 us
    all_to_all x1, waiting for transfers between devices, per_device(): parts = lax.all_to_all(parts, 'tm', 2, 2, tiled=True)  10.1 us
    pallas_call x1, Pallas kernels, lag_transform(): pl.pallas_call(lag_kernel, grid=(chan_count // step_blocks,), in_specs=[p...  9.56 us
    dot_general x1, matrix products, per_device(): jnp.einsum('tkqa,ctkqw->kcaw', left, every, preferred_element_type=jnp.fl...  8.17 us
    all_to_all x1, starting transfers between devices, per_device(): parts = lax.all_to_all(parts, 'tm', 2, 2, tiled=True)  6.33 us
    dot_general x1, matrix products, per_device(): jnp.dot(raw_rows, folded, precision=lax.Precision.HIGH, preferred_element...  6.29 us
    concatenate x1, local copies, waits for them, and re-layouts, per_device(): jnp.concatenate([rows, turned], axis=4)  2.98 us
  transfers between devices with their start and end apart: 2, of which 2 were waited for; matrix products, arithmetic and copies ran while one was open for 4% of the time, Pallas kernels for 0%

profile of v18, /device:TPU:0, one launch (start us, length us, event | category | flops | bytes accessed | tf_op | source)
XLA Modules:
  0.0 121.0 jit_solution(11873865953451295327)
XLA Ops:
  6.5 0.0 all-gather.2.cloned.1.call-start
  6.5 6.3 %convolution_bitcast_fusion = f32[512,256]{0,1:T(8,128)S(1)} fusion(f32[2048,256]{1,0:T(8,128)} %constant.44.clone, f32[512,2048]{1,0:T(8,128)} %bitcast.32), kind=kOutput, calls=%fused_computation.4 | convolution fusion | flops 1610612736 | bytes 6815744 | tf_op jit(solution)/shard_map/dot_general | solution.py:86
  12.8 0.1 add_reduce_fusion
  12.9 0.1 reshape.113
  13.0 0.1 reshape.114
  13.1 0.1 multiply_convert_fusion.1
  13.3 0.9 copy.20
  14.2 0.0 all-gather.2.cloned.1.call-update
  14.2 0.2 copy.21
  14.4 0.7 copy.22
  15.1 6.3 %all-to-all-start = ((bf16[128,8,8,16]{0,3,1,2:T(8,128)(2,1)}), bf16[128,8,8,16]{0,3,1,2:T(8,128)(2,1)S(1)}, u32[]{:S(2)}, u32[]{:S(2)}) async-start(bf16[128,8,8,16]{0,3,1,2:T(8,128)(2,1)} %copy.22), calls=%async_computation | async-start | bytes 524288 | tf_op jit(solution)/shard_map/all_to_all | solution.py:101
  21.4 0.6 cosine_convert_fusion
  22.1 0.7 pad_maximum_fusion.2.table_ref
  22.7 10.1 %all-to-all-done = bf16[128,8,8,16]{0,3,1,2:T(8,128)(2,1)S(1)} async-done(((bf16[128,8,8,16]{0,3,1,2:T(8,128)(2,1)}), bf16[128,8,8,16]{0,3,1,2:T(8,128)(2,1)S(1)}, u32[]{:S(2)}, u32[]{:S(2)}) %all-to-all-start) | async-done | bytes 262176 | tf_op jit(solution)/shard_map/all_to_all | solution.py:101
  33.0 3.0 %copy.25 = bf16[8,128,8,32,1]{3,2,0,4,1:T(8,128)(2,1)S(1)} copy(bf16[8,128,8,32,1]{1,3,2,0,4:T(8,128)(2,1)S(1)} %maximum_bitcast_fusion) | data formatting | bytes 1048576 | tf_op jit(solution)/shard_map/concatenate | solution.py:105
  36.0 60.5 %all-gather.2.cloned.1.call-done = bf16[32,128,8,128]{3,2,1,0:T(8,128)(2,1)} async-done(((bf16[1,128,8,128]{3,2,1,0:T(8,128)(2,1)}), bf16[32,128,8,128]{3,2,1,0:T(8,128)(2,1)}) %all-gather.2.cloned.1.call-update) | async-done | bytes 8388624 | tf_op jit(solution)/shard_map/all_gather | solution.py:96
  96.5 8.2 %fusion.cross_ref = f32[128,4,32,128]{3,2,1,0:T(8,128)} fusion(bf16[8,128,8,32,1]{3,2,0,4,1:T(8,128)(2,1)S(1)} %copy.25, bf16[4,8,128,8,128]{4,3,2,1,0:T(8,128)(2,1)} %bitcast.31), kind=kOutput, calls=%fused_computation.1 | convolution fusion | flops 270532608 | bytes 17301504 | tf_op jit(solution)/shard_map/tkqa,ctkqw->kcaw/dot_general | solution.py:109
  104.6 9.6 %shard_map.28 = f32[16,512,256]{2,1,0:T(8,128)} custom-call(f32[128,4,32,128]{3,2,1,0:T(8,128)} %fusion.cross_ref, bf16[256,256]{1,0:T(8,128)(2,1)} %pad_maximum_fusion.2.table_ref), custom_call_target="tpu_custom_call" | custom-call | tf_op jit(solution)/shard_map/pallas_call | solution.py:61
  (7 shorter events, 0.1 us)
Async XLA Ops:
  6.5 89.9 %all-gather.2.cloned.1.call-start = ((), (), s32[]{:S(2)}) async-start(), calls=%async_computation.1 | async-start | bytes 8650752 | tf_op jit(solution)/shard_map/all_gather | solution.py:96
  15.1 17.8 %all-to-all-start = ((bf16[128,8,8,16]{0,3,1,2:T(8,128)(2,1)}), bf16[128,8,8,16]{0,3,1,2:T(8,128)(2,1)S(1)}, u32[]{:S(2)}, u32[]{:S(2)}) async-start(bf16[128,8,8,16]{0,3,1,2:T(8,128)(2,1)} %copy.22), calls=%async_computation | async-start | bytes 524288 | tf_op jit(solution)/shard_map/all_to_all | solution.py:101
Sparse Core Ops, SparseCore 0:
  14.3 82.1 all-gather.1

commit v19 on v16

--- a/solution.py
+++ b/solution.py
@@ -83,16 +83,17 @@
     row_width = channel_total // (chan_count * time_count)
     raw_rows = raw_samples.reshape(seg_count * block_width, raw_length)
     folded = folded_tables(sample_count, freq_count)
-    spectrum = jnp.dot(
-        raw_rows, folded, precision=lax.Precision.HIGH, preferred_element_type=jnp.float32
+    spectrum = jnp.einsum(
+        "nk,rn->kr", folded, raw_rows, precision=lax.Precision.HIGH,
+        preferred_element_type=jnp.float32,
     )
-    real_part = spectrum[:, :freq_count].reshape(seg_count, block_width, freq_count)
-    imag_part = spectrum[:, freq_count:].reshape(seg_count, block_width, freq_count)
-    real_w, imag_w = whiten(real_part, imag_part)
-    local_spec = jnp.stack([real_w, imag_w], axis=0).astype(jnp.bfloat16)
-    local_spec = jnp.transpose(local_spec, (3, 0, 1, 2)).reshape(
-        freq_count, 2 * seg_count, block_width
-    )
+    real_part = spectrum[:freq_count].reshape(freq_count, seg_count, block_width)
+    imag_part = spectrum[freq_count:].reshape(freq_count, seg_count, block_width)
+    power = real_part * real_part + imag_part * imag_part
+    level = jnp.mean(power, axis=0, keepdims=True)
+    factor = 1.0 / jnp.sqrt(power + 0.1 * level + 1e-06)
+    local_spec = jnp.stack([real_part * factor, imag_part * factor], axis=1).astype(jnp.bfloat16)
+    local_spec = local_spec.reshape(freq_count, 2 * seg_count, block_width)
     every = lax.all_gather(local_spec, ("chan", "tm"), axis=0)
     every = every.reshape(chan_count, time_count, freq_count, 2 * seg_count, block_width)
     chan_index = lax.axis_index("chan")

time: 120 us -> 120 us (level)
    convert_element_type x0 -> x3, local copies, waits for them, and re-layouts: none -> 1.8 us  [per_device(): jnp.stack([real_part * factor, imag_part * factor], axis=1)]
    another operation x2 -> x0, local copies, waits for them, and re-layouts: 1.62 us -> none  [the longest x1 0.9 us: per_device(): every = lax.all_gather(local_spec, ('chan', 'tm'), axis=0)]
where the time goes in v19:
time: 120 us
  waiting for transfers between devices  70.7 us (59%)
  between operations  13.5 us (11%)
  matrix products  13.3 us (11%)
  Pallas kernels  9.3 us (8%)
  starting transfers between devices  6.33 us (5%)
  local copies, waits for them, and re-layouts  4.96 us (4%)
  other arithmetic  1.58 us (1%)
    all_gather x1, waiting for transfers between devices, per_device(): every = lax.all_gather(local_spec, ('chan', 'tm'), axis=0)  60.5 us
    all_to_all x1, waiting for transfers between devices, per_device(): parts = lax.all_to_all(parts, 'tm', 2, 2, tiled=True)  10.1 us
    pallas_call x1, Pallas kernels, lag_transform(): pl.pallas_call(lag_kernel, grid=(chan_count // step_blocks,), in_specs=[p...  9.3 us
    dot_general x1, matrix products, per_device(): jnp.einsum('tkqa,ctkqw->kcaw', left, every, preferred_element_type=jnp.fl...  7.03 us
    all_to_all x1, starting transfers between devices, per_device(): parts = lax.all_to_all(parts, 'tm', 2, 2, tiled=True)  6.33 us
    dot_general x1, matrix products, per_device(): jnp.einsum('nk,rn->kr', folded, raw_rows, precision=lax.Precision.HIGH, p...  6.29 us
    concatenate x1, local copies, waits for them, and re-layouts, per_device(): jnp.concatenate([rows, turned], axis=4)  2.98 us
  transfers between devices with their start and end apart: 2, of which 2 were waited for; matrix products, arithmetic and copies ran while one was open for 4% of the time, Pallas kernels for 0%

profile of v19, /device:TPU:0, one launch (start us, length us, event | category | flops | bytes accessed | tf_op | source)
XLA Modules:
  0.0 119.6 jit_solution(16433407802642567503)
XLA Ops:
  6.5 0.0 all-gather.2.cloned.1.call-start
  6.5 6.3 %fusion.13 = f32[256,512]{1,0:T(8,128)S(1)} fusion(f32[2048,256]{1,0:T(8,128)} %constant.44.clone, f32[512,2048]{1,0:T(8,128)} %bitcast.24), kind=kOutput, calls=%fused_computation.31 | convolution fusion | flops 1610612736 | bytes 6815744 | tf_op jit(solution)/shard_map/nk,rn->kr/dot_general | solution.py:86
  12.8 0.1 add_reduce_fusion
  12.9 0.1 reshape.126
  13.0 0.1 reshape.127
  13.1 0.1 fusion.7
  13.3 0.9 copy.20
  14.2 0.0 all-gather.2.cloned.1.call-update
  14.2 0.2 copy.21
  14.4 0.7 copy.22
  15.1 6.3 %all-to-all-start = ((bf16[128,8,8,16]{0,3,1,2:T(8,128)(2,1)}), bf16[128,8,8,16]{0,3,1,2:T(8,128)(2,1)S(1)}, u32[]{:S(2)}, u32[]{:S(2)}) async-start(bf16[128,8,8,16]{0,3,1,2:T(8,128)(2,1)} %copy.22), calls=%async_computation | async-start | bytes 524288 | tf_op jit(solution)/shard_map/all_to_all | solution.py:102
  21.4 0.6 cosine_convert_fusion
  22.1 0.7 pad_maximum_fusion.1.table_ref
  22.7 10.1 %all-to-all-done = bf16[128,8,8,16]{0,3,1,2:T(8,128)(2,1)S(1)} async-done(((bf16[128,8,8,16]{0,3,1,2:T(8,128)(2,1)}), bf16[128,8,8,16]{0,3,1,2:T(8,128)(2,1)S(1)}, u32[]{:S(2)}, u32[]{:S(2)}) %all-to-all-start) | async-done | bytes 262176 | tf_op jit(solution)/shard_map/all_to_all | solution.py:102
  33.0 3.0 %copy.25 = bf16[8,128,8,32,1]{3,2,0,4,1:T(8,128)(2,1)S(1)} copy(bf16[8,128,8,32,1]{1,3,2,0,4:T(8,128)(2,1)S(1)} %maximum_bitcast_fusion) | data formatting | bytes 1048576 | tf_op jit(solution)/shard_map/concatenate | solution.py:106
  35.9 60.5 %all-gather.2.cloned.1.call-done = bf16[32,128,8,128]{3,2,1,0:T(8,128)(2,1)} async-done(((bf16[1,128,8,128]{3,2,1,0:T(8,128)(2,1)}), bf16[32,128,8,128]{3,2,1,0:T(8,128)(2,1)}) %all-gather.2.cloned.1.call-update) | async-done | bytes 8388624 | tf_op jit(solution)/shard_map/all_gather | solution.py:97
  96.5 7.0 %fusion.3.cross_ref = bf16[128,4,32,128]{3,2,1,0:T(8,128)(2,1)} fusion(bf16[8,128,8,32,1]{3,2,0,4,1:T(8,128)(2,1)S(1)} %copy.25, bf16[4,8,128,8,128]{4,3,2,1,0:T(8,128)(2,1)} %bitcast.30), kind=kOutput, calls=%fused_computation.4 | convolution fusion | flops 272629760 | bytes 13107200 | tf_op jit(solution)/shard_map/tkqa,ctkqw->kcaw/dot_general | solution.py:110
  103.5 9.3 %shard_map.28 = f32[16,512,256]{2,1,0:T(8,128)} custom-call(bf16[128,4,32,128]{3,2,1,0:T(8,128)(2,1)} %fusion.3.cross_ref, bf16[256,256]{1,0:T(8,128)(2,1)} %pad_maximum_fusion.1.table_ref), custom_call_target="tpu_custom_call" | custom-call | tf_op jit(solution)/shard_map/pallas_call | solution.py:61
  (7 shorter events, 0.1 us)
Async XLA Ops:
  6.5 89.9 %all-gather.2.cloned.1.call-start = ((), (), s32[]{:S(2)}) async-start(), calls=%async_computation.1 | async-start | bytes 8650752 | tf_op jit(solution)/shard_map/all_gather | solution.py:97
  15.1 17.8 %all-to-all-start = ((bf16[128,8,8,16]{0,3,1,2:T(8,128)(2,1)}), bf16[128,8,8,16]{0,3,1,2:T(8,128)(2,1)S(1)}, u32[]{:S(2)}, u32[]{:S(2)}) async-start(bf16[128,8,8,16]{0,3,1,2:T(8,128)(2,1)} %copy.22), calls=%async_computation | async-start | bytes 524288 | tf_op jit(solution)/shard_map/all_to_all | solution.py:102
Sparse Core Ops, SparseCore 0:
  14.3 82.1 all-gather.1
